TPU v7x, 512 devices: a whole 4x4x16 slice. The times are simulated.
512 devices in a mesh: seq: 32 (over z, y_hi), ep: 16 (over x, y_lo, core).
Axes of the slice: x: 4, y: 4 (y_hi: 2, y_lo: 2; y = y_hi * 2 + y_lo), z: 16, core: 2. Of those that a mesh axis runs over, the one named last changes fastest.
Arguments:
- queries: bfloat16 [12288, 6144], P('seq', 'ep'), may hold values from -5 to 5
- key_heads: bfloat16 [12288, 2048], P('seq', 'ep'), may hold values from -4 to 4, as said below
- value_heads: bfloat16 [12288, 2048], P('seq', 'ep'), may hold values from -6 to 6, as said below
- attn_grad: bfloat16 [12288, 6144], P('seq', 'ep'), may hold values from -6 to 6
- segments: int32 [12288], P('seq'), may hold values from 0 to 63, never falling along the last dimension, each value on 1 to 1153 neighbouring positions
- moe_grad: bfloat16 [12288, 6144], P(('seq', 'ep')), may hold values from -6 to 6
- expert_out: bfloat16 [12288, 2, 6144], P(('seq', 'ep')), may hold values from -6 to 6
- normed: bfloat16 [12288, 6144], P(('seq', 'ep')), may hold values from -6 to 6
- router: bfloat16 [8, 6144], replicated, may hold values from -0.078125 to 0.078125
- routes: int32 [12288, 2], P(('seq', 'ep')), may hold values from 0 to 7, all different within a row; in each aligned block of 24 rows (0 to 23, 24 to 47, ...) at most 6 rows name the same one
Outputs:
- query_grad: bfloat16 [12288, 6144], P('seq', 'ep')
- key_grad: bfloat16 [12288, 2048], P('seq', 'ep')
- value_grad: bfloat16 [12288, 2048], P('seq', 'ep')
- normed_grad: bfloat16 [12288, 6144], P(('seq', 'ep'))
- router_grad: float32 [8, 6144], replicated
- routed_grads: bfloat16 [8192, 6, 6144], P(('seq', 'ep'))
Inputs may be any that keep to these rules, and one draw needn't show every extreme that they name: `key_heads`: the 2 indices of ep e with the same e // 2 hold identical copies. `value_heads`: the 2 indices of ep e with the same e // 2 hold identical copies. `segments`: segment numbers never fall along the sequence; every document has 1 to 1153 tokens and one has exactly 1153. A token names two different experts; in each aligned block of 24 tokens (the tokens of one device) every expert is named by exactly 6 routes.
All inputs are finite; a program needn't handle non-finite values.
Results may differ from a plain program's by a relative error of at most 0.0071.
Values may be sent and summed in bfloat16 or wider, within the bound.
No kernel may reach another device: no remote copies, remote signals or barrier semaphores. Data moves between devices by JAX's collectives and lax.ppermute only.
A program may use at most 64 MiB of HBM per device.

v0:
```python
import functools
import math

import jax
import jax.numpy as jnp
from jax import lax
from jax.sharding import PartitionSpec as P

EXPERTS = 8
HD = 128
TOP = 2
REACH = 3


MASKED = -1e30


def from_behind(value, axis, by):
    devices = lax.axis_size(axis)
    pairs = [(i, i + by) for i in range(devices) if 0 <= i + by < devices]
    return lax.ppermute(value, axis, pairs)


def allowed_pairs(seg_rows, seg_keys, seq_index, offset, tok_rows):
    positions = jnp.arange(tok_rows, dtype=jnp.int32)
    row_pos = seq_index * tok_rows + positions
    key_pos = (seq_index - offset) * tok_rows + positions
    same_doc = seg_rows[:, None] == seg_keys[None, :]
    causal = key_pos[None, :] <= row_pos[:, None]
    return same_doc & causal & (seq_index - offset >= 0)


def masked_scores(query_rows, key_block, allowed, score_scale):
    raw_scores = (
        jnp.einsum("qhgd,thd->hgqt", query_rows, key_block, preferred_element_type=jnp.float32)
        * score_scale
    )
    return jnp.where(allowed, raw_scores, MASKED)


def stats_update(running, query_rows, grad_rows, key_block, value_block, allowed, score_scale):
    row_peak, row_total, weighted = running
    scores = masked_scores(query_rows, key_block, allowed, score_scale)
    prob_grad = jnp.einsum(
        "qhgd,thd->hgqt", grad_rows, value_block, preferred_element_type=jnp.float32
    )
    new_peak = jnp.maximum(row_peak, jnp.max(scores, axis=-1))
    factor = jnp.exp(row_peak - new_peak)
    weights = jnp.where(allowed, jnp.exp(scores - new_peak[..., None]), 0.0)
    return (
        new_peak,
        row_total * factor + jnp.sum(weights, axis=-1),
        weighted * factor + jnp.sum(weights * prob_grad, axis=-1),
    )


def block_grads(
    query_rows, grad_rows, key_block, value_block, allowed, log_total, delta, score_scale
):
    scores = masked_scores(query_rows, key_block, allowed, score_scale)
    soft_probs = jnp.where(allowed, jnp.exp(scores - log_total[..., None]), 0.0)
    probs_low = soft_probs.astype(jnp.bfloat16)
    value_part = jnp.einsum(
        "hgqt,qhgd->thd", probs_low, grad_rows, preferred_element_type=jnp.float32
    )
    prob_grad = jnp.einsum(
        "qhgd,thd->hgqt", grad_rows, value_block, preferred_element_type=jnp.float32
    )
    score_low = (soft_probs * (prob_grad - delta[..., None])).astype(jnp.bfloat16)
    query_part = (
        jnp.einsum("hgqt,thd->qhgd", score_low, key_block, preferred_element_type=jnp.float32)
        * score_scale
    )
    key_part = (
        jnp.einsum("hgqt,qhgd->thd", score_low, query_rows, preferred_element_type=jnp.float32)
        * score_scale
    )
    return (query_part, key_part, value_part)


def on_device(
    queries,
    key_heads,
    value_heads,
    attn_grad,
    segments,
    moe_grad,
    expert_out,
    normed,
    router,
    routes,
):
    tok_rows = queries.shape[0]
    kv_heads = key_heads.shape[1] // HD
    group_size = queries.shape[1] // (kv_heads * HD)
    score_scale = 1.0 / math.sqrt(HD)
    query_rows = queries.reshape(tok_rows, kv_heads, group_size, HD)
    grad_rows = attn_grad.reshape(tok_rows, kv_heads, group_size, HD)
    key_block = key_heads.reshape(tok_rows, kv_heads, HD)
    value_block = value_heads.reshape(tok_rows, kv_heads, HD)
    seq_index = lax.axis_index("seq")
    ep_size = lax.axis_size("ep")
    gathered = [(key_block, value_block, segments)]
    for offset in range(1, REACH + 1):
        gathered.append(from_behind((key_block, value_block, segments), "seq", offset))
    stat_shape = (kv_heads, group_size, tok_rows)
    running = (
        jnp.full(stat_shape, MASKED, jnp.float32),
        jnp.zeros(stat_shape, jnp.float32),
        jnp.zeros(stat_shape, jnp.float32),
    )
    masks = []
    for offset, (keys_now, values_now, segs_now) in enumerate(gathered):
        allowed = allowed_pairs(segments, segs_now, seq_index, offset, tok_rows)
        masks.append(allowed)
        compute = functools.partial(
            stats_update, running, query_rows, grad_rows, keys_now, values_now, allowed, score_scale
        )
        if offset == 0:
            running = compute()
        else:
            running = compute()
    row_peak, row_total, weighted = running
    log_total = row_peak + jnp.log(row_total)
    delta = weighted / row_total
    parts = []
    for offset, (keys_now, values_now, segs_now) in enumerate(gathered):
        compute = functools.partial(
            block_grads,
            query_rows,
            grad_rows,
            keys_now,
            values_now,
            masks[offset],
            log_total,
            delta,
            score_scale,
        )
        if offset == 0:
            parts.append(compute())
        else:
            parts.append(compute())
    query_total = parts[0][0]
    for offset in range(1, REACH + 1):
        query_total = query_total + parts[offset][0]
    key_total = parts[0][1]
    value_total = parts[0][2]
    for offset in range(1, REACH + 1):
        key_back, value_back = from_behind((parts[offset][1], parts[offset][2]), "seq", -offset)
        key_total = key_total + key_back
        value_total = value_total + value_back
    query_grad = query_total.reshape(tok_rows, -1).astype(jnp.bfloat16)
    key_grad = key_total.reshape(tok_rows, -1).astype(jnp.bfloat16)
    value_grad = value_total.reshape(tok_rows, -1).astype(jnp.bfloat16)
    moe_rows = moe_grad.shape[0]
    capacity = moe_rows * TOP // EXPERTS
    copies = max(1, ep_size // EXPERTS)
    logits = jnp.einsum("td,ed->te", normed, router, preferred_element_type=jnp.float32)
    expert_ids = jnp.arange(EXPERTS, dtype=jnp.int32)
    onehot = (routes[:, :, None] == expert_ids[None, None, :]).astype(jnp.float32)
    chosen = jnp.sum(onehot * logits[:, None, :], axis=2)
    first_gate = 1.0 / (1.0 + jnp.exp(chosen[:, 1] - chosen[:, 0]))
    second_gate = 1.0 - first_gate
    gate_grad = jnp.einsum("td,tkd->tk", moe_grad, expert_out, preferred_element_type=jnp.float32)
    logit_step = first_gate * second_gate * (gate_grad[:, 0] - gate_grad[:, 1])
    logit_grad = (onehot[:, 0, :] - onehot[:, 1, :]) * logit_step[:, None]
    normed_grad = jnp.dot(
        logit_grad, router.astype(jnp.float32), precision=lax.Precision.HIGHEST
    ).astype(jnp.bfloat16)
    local_router = jnp.dot(
        logit_grad.T, normed.astype(jnp.float32), precision=lax.Precision.HIGHEST
    )
    all_tokens = moe_rows * lax.axis_size("seq") * ep_size
    router_grad = lax.psum(local_router, ("seq", "ep")) / all_tokens
    gates = jnp.stack([first_gate, second_gate], axis=1)
    expert_rows = (gates[:, :, None] * moe_grad.astype(jnp.float32)[:, None, :]).astype(
        jnp.bfloat16
    )
    flat_routes = routes.reshape(-1)
    hot = (flat_routes[:, None] == expert_ids[None, :]).astype(jnp.int32)
    ranks = jnp.sum((jnp.cumsum(hot, axis=0) - 1) * hot, axis=1)
    order = jnp.argsort(flat_routes * capacity + ranks)
    outgoing = expert_rows.reshape(-1, expert_rows.shape[2])[order]
    outgoing = jnp.repeat(outgoing.reshape(EXPERTS, capacity, -1), copies, axis=0)
    routed_grads = lax.all_to_all(outgoing, "ep", split_axis=0, concat_axis=0, tiled=True)
    return (query_grad, key_grad, value_grad, normed_grad, router_grad, routed_grads)


def solution(mesh):
    return jax.shard_map(
        on_device,
        mesh=mesh,
        in_specs=(
            P("seq", "ep"),
            P("seq", "ep"),
            P("seq", "ep"),
            P("seq", "ep"),
            P("seq"),
            P(("seq", "ep"), None),
            P(("seq", "ep"), None, None),
            P(("seq", "ep"), None),
            P(),
            P(("seq", "ep"), None),
        ),
        out_specs=(
            P("seq", "ep"),
            P("seq", "ep"),
            P("seq", "ep"),
            P(("seq", "ep"), None),
            P(),
            P(("seq", "ep"), None, None),
        ),
        check_vma=False,
    )
```

profile of v0, /device:TPU:1, one launch (start us, length us, event | category | flops | bytes accessed | tf_op | source)
XLA Modules:
  0.0 550.0 jit_solution(5663272044852819062)
XLA Ops:
  7.2 5.8 %collective-permute-start = (s32[384]{0:T(512)}, s32[384]{0:T(512)S(1)}, u32[]{:S(2)}, u32[]{:S(2)}) collective-permute-start(s32[384]{0:T(512)} %param.14), channel_id=1, source_target_pairs={{0,16},{16,32},{32,48},{48,64},{64,80},{80,96},{96,112},{112,128},... | collective-permute-start | bytes 4616 | tf_op jit(solution)/shard_map/ppermute | solution.py:21
  13.0 3.5 collective-permute-start.2
  16.5 4.7 collective-permute-start.4
  21.2 8.1 %collective-permute-start.5 = (bf16[384,1,128]{2,0,1:T(8,128)(2,1)}, bf16[384,1,128]{2,0,1:T(8,128)(2,1)}, u32[]{:S(2)}, u32[]{:S(2)}) collective-permute-start(bf16[384,1,128]{2,0,1:T(8,128)(2,1)} %bitcast.331), channel_id=1, source_target_pairs={{0,48},{16,64},{32,80},{48,96},{64,112},{80,128},{96,144},{112,160... | collective-permute-start | bytes 294920 | tf_op jit(solution)/shard_map/ppermute | solution.py:21
  29.3 3.3 collective-permute-start.1
  32.6 0.8 copy.135
  33.8 2.0 sort.17
  35.8 1.2 fusion.103
  37.0 0.7 select_reduce_fusion.1
  37.9 1.5 mul.339
  39.4 0.8 mul.340
  40.4 0.9 gather_fusion
  41.5 1.3 broadcast_in_dim.98
  42.8 7.5 %all-to-all-start = ((bf16[16,6,6144]{2,1,0:T(8,128)(2,1)}), bf16[16,6,6144]{2,1,0:T(8,128)(2,1)}, u32[]{:S(2)}, u32[]{:S(2)}) async-start(bf16[16,6,6144]{2,1,0:T(8,128)(2,1)} %bitcast.92), calls=%async_computation | async-start | bytes 3145728 | tf_op jit(solution)/shard_map/all_to_all | solution.py:185
  50.5 1.4 fusion.65
  52.0 1.0 fusion.89
  53.0 1.2 convolution_convert_fusion
  54.6 2.9 collective-permute-start.3
  57.6 4.5 collective-permute-start.6
  62.1 6.2 %collective-permute-start.8 = (bf16[384,1,128]{2,0,1:T(8,128)(2,1)}, bf16[384,1,128]{2,0,1:T(8,128)(2,1)S(1)}, u32[]{:S(2)}, u32[]{:S(2)}) collective-permute-start(bf16[384,1,128]{2,0,1:T(8,128)(2,1)} %bitcast.22), channel_id=1, source_target_pairs={{0,48},{16,64},{32,80},{48,96},{64,112},{80,128},{96,144},{112,160... | collective-permute-start | bytes 294920 | tf_op jit(solution)/shard_map/ppermute | solution.py:21
  68.3 0.8 and_and_fusion.3
  69.6 2.7 collective-permute-start.7
  72.3 1.4 fusion.99
  74.6 1.5 fusion.9
  78.2 1.1 convolution_bitcast_fusion.2
  79.3 1.1 convolution_bitcast_fusion
  80.4 1.1 convolution_bitcast_fusion.1
  81.6 1.3 collective-permute-start.12
  82.8 1.3 collective-permute-start.14
  84.1 1.5 collective-permute-start.13
  85.7 2.7 fusion.51
  88.4 0.9 copy-done.2
  89.3 1.1 fusion.29
  90.3 1.3 collective-permute-start.10
  91.6 1.1 fusion.30
  92.7 1.3 collective-permute-start.11
  94.0 1.2 fusion.82
  95.2 424.3 %all-reduce.2.cloned.1.call-done = f32[8,6144]{1,0:T(8,128)} async-done(((f32[8,6144]{1,0:T(8,128)}), f32[8,6144]{1,0:T(8,128)}) %all-reduce.2.cloned.1.call-update) | async-done | bytes 196624 | tf_op jit(solution)/shard_map/psum | solution.py:174
  519.5 1.7 broadcast_multiply_fusion
  521.2 1.8 convolution_add_fusion.1
  523.0 1.4 fusion.75
  524.4 1.1 fusion.28
  525.4 1.3 collective-permute-start.9
  527.1 0.9 copy.136
  528.0 7.5 %collective-permute-done.9 = f32[384,1,128]{2,0,1:T(8,128)} collective-permute-done((f32[384,1,128]{2,0,1:T(8,128)}, f32[384,1,128]{2,0,1:T(8,128)}, u32[]{:S(2)}, u32[]{:S(2)}) %collective-permute-start.9) | collective-permute-done | bytes 196640 | tf_op jit(solution)/shard_map/ppermute | solution.py:21
  535.5 2.4 fusion.40
  537.9 2.2 fusion.39
  540.1 3.1 copy.137
  (77 shorter events, 5.5 us)
Async XLA Ops:
  7.2 43.3 %copy-start = (bf16[24,2,6144]{2,1,0:T(2,128)(2,1)S(1)}, bf16[24,2,6144]{2,1,0:T(2,128)(2,1)}, u32[]{:S(2)}) copy-start(bf16[24,2,6144]{2,1,0:T(2,128)(2,1)} %param.16) | copy-start | bytes 1769476
  7.2 47.5 %collective-permute-start = (s32[384]{0:T(512)}, s32[384]{0:T(512)S(1)}, u32[]{:S(2)}, u32[]{:S(2)}) collective-permute-start(s32[384]{0:T(512)} %param.14), channel_id=1, source_target_pairs={{0,16},{16,32},{32,48},{48,64},{64,80},{80,96},{96,112},{112,128},... | collective-permute-start | bytes 4616 | tf_op jit(solution)/shard_map/ppermute | solution.py:21
  13.0 44.6 %collective-permute-start.2 = (s32[384]{0:T(512)}, s32[384]{0:T(512)S(1)}, u32[]{:S(2)}, u32[]{:S(2)}) collective-permute-start(s32[384]{0:T(512)} %param.14), channel_id=1, source_target_pairs={{0,32},{16,48},{32,64},{48,80},{64,96},{80,112},{96,128},{112,144}... | collective-permute-start | bytes 4616 | tf_op jit(solution)/shard_map/ppermute | solution.py:21
  16.5 45.6 %collective-permute-start.4 = (s32[384]{0:T(512)}, s32[384]{0:T(512)S(1)}, u32[]{:S(2)}, u32[]{:S(2)}) collective-permute-start(s32[384]{0:T(512)} %param.14), channel_id=1, source_target_pairs={{0,48},{16,64},{32,80},{48,96},{64,112},{80,128},{96,144},{112,160... | collective-permute-start | bytes 4616 | tf_op jit(solution)/shard_map/ppermute | solution.py:21
  21.2 48.4 %collective-permute-start.5 = (bf16[384,1,128]{2,0,1:T(8,128)(2,1)}, bf16[384,1,128]{2,0,1:T(8,128)(2,1)}, u32[]{:S(2)}, u32[]{:S(2)}) collective-permute-start(bf16[384,1,128]{2,0,1:T(8,128)(2,1)} %bitcast.331), channel_id=1, source_target_pairs={{0,48},{16,64},{32,80},{48,96},{64,112},{80,128},{96,144},{112,160... | collective-permute-start | bytes 294920 | tf_op jit(solution)/shard_map/ppermute | solution.py:21
  29.3 44.4 %collective-permute-start.1 = (bf16[384,1,128]{2,0,1:T(8,128)(2,1)}, bf16[384,1,128]{2,0,1:T(8,128)(2,1)S(1)}, u32[]{:S(2)}, u32[]{:S(2)}) collective-permute-start(bf16[384,1,128]{2,0,1:T(8,128)(2,1)} %bitcast.332), channel_id=1, source_target_pairs={{0,16},{16,32},{32,48},{48,64},{64,80},{80,96},{96,112},{112,128},... | collective-permute-start | bytes 294920 | tf_op jit(solution)/shard_map/ppermute | solution.py:21
  42.8 7.6 %copy-start.13 = (s32[24,2]{0,1:T(2,128)S(1)}, s32[24,2]{0,1:T(2,128)}, u32[]{:S(2)}) copy-start(s32[24,2]{0,1:T(2,128)} %param.19) | copy-start | bytes 580
  42.8 7.6 %copy-start.12 = (bf16[24,6144]{1,0:T(8,128)(2,1)S(1)}, bf16[24,6144]{1,0:T(8,128)(2,1)}, u32[]{:S(2)}) copy-start(bf16[24,6144]{1,0:T(8,128)(2,1)} %param.15) | copy-start | bytes 884740
  42.8 497.3 %all-to-all-start = ((bf16[16,6,6144]{2,1,0:T(8,128)(2,1)}), bf16[16,6,6144]{2,1,0:T(8,128)(2,1)}, u32[]{:S(2)}, u32[]{:S(2)}) async-start(bf16[16,6,6144]{2,1,0:T(8,128)(2,1)} %bitcast.92), calls=%async_computation | async-start | bytes 3145728 | tf_op jit(solution)/shard_map/all_to_all | solution.py:185
  50.4 469.1 %all-reduce.2.cloned.1.call-start = ((), (), s32[]{:S(2)}) async-start(), calls=%async_computation.1 | async-start | bytes 393216 | tf_op jit(solution)/shard_map/psum | solution.py:174
  50.5 1.6 copy-start.7
  50.5 2.5 copy-start.8
  50.5 3.7 copy-start.10
  51.9 2.5 copy-start.11
  51.9 2.7 copy-start.9
  51.9 16.4 %copy-start.14 = (s32[384]{0:T(512)S(1)}, s32[384]{0:T(512)}, u32[]{:S(2)}) copy-start(s32[384]{0:T(512)} %param.14) | copy-start | bytes 4612
  54.6 19.5 %collective-permute-start.3 = (bf16[384,1,128]{2,0,1:T(8,128)(2,1)S(1)}, bf16[384,1,128]{2,0,1:T(8,128)(2,1)S(1)}, u32[]{:S(2)}, u32[]{:S(2)}) collective-permute-start(bf16[384,1,128]{2,0,1:T(8,128)(2,1)S(1)} %bitcast.333), channel_id=1, source_target_pairs={{0,32},{16,48},{32,64},{48,80},{64,96},{80,112},{96,128},{112,144}... | collective-permute-start | bytes 294920 | tf_op jit(solution)/shard_map/ppermute | solution.py:21
  57.6 18.6 %collective-permute-start.6 = (bf16[384,1,128]{2,0,1:T(8,128)(2,1)}, bf16[384,1,128]{2,0,1:T(8,128)(2,1)S(1)}, u32[]{:S(2)}, u32[]{:S(2)}) collective-permute-start(bf16[384,1,128]{2,0,1:T(8,128)(2,1)} %bitcast.22), channel_id=1, source_target_pairs={{0,16},{16,32},{32,48},{48,64},{64,80},{80,96},{96,112},{112,128},... | collective-permute-start | bytes 294920 | tf_op jit(solution)/shard_map/ppermute | solution.py:21
  62.1 14.7 %collective-permute-start.8 = (bf16[384,1,128]{2,0,1:T(8,128)(2,1)}, bf16[384,1,128]{2,0,1:T(8,128)(2,1)S(1)}, u32[]{:S(2)}, u32[]{:S(2)}) collective-permute-start(bf16[384,1,128]{2,0,1:T(8,128)(2,1)} %bitcast.22), channel_id=1, source_target_pairs={{0,48},{16,64},{32,80},{48,96},{64,112},{80,128},{96,144},{112,160... | collective-permute-start | bytes 294920 | tf_op jit(solution)/shard_map/ppermute | solution.py:21
  69.6 7.8 %collective-permute-start.7 = (bf16[384,1,128]{2,0,1:T(8,128)(2,1)}, bf16[384,1,128]{2,0,1:T(8,128)(2,1)S(1)}, u32[]{:S(2)}, u32[]{:S(2)}) collective-permute-start(bf16[384,1,128]{2,0,1:T(8,128)(2,1)} %bitcast.22), channel_id=1, source_target_pairs={{0,32},{16,48},{32,64},{48,80},{64,96},{80,112},{96,128},{112,144}... | collective-permute-start | bytes 294920 | tf_op jit(solution)/shard_map/ppermute | solution.py:21
  81.6 456.4 %collective-permute-start.12 = (f32[384,1,128]{2,0,1:T(8,128)}, f32[384,1,128]{2,0,1:T(8,128)}, u32[]{:S(2)}, u32[]{:S(2)}) collective-permute-start(f32[384,1,128]{2,0,1:T(8,128)} %convolution_bitcast_fusion.2), channel_id=1, source_target_pairs={{16,0},{32,16},{48,32},{64,48},{80,64},{96,80},{112,96},{128,112},... | collective-permute-start | bytes 589832 | tf_op jit(solution)/shard_map/ppermute | solution.py:21
  82.8 455.1 %collective-permute-start.14 = (f32[384,1,128]{2,0,1:T(8,128)}, f32[384,1,128]{2,0,1:T(8,128)}, u32[]{:S(2)}, u32[]{:S(2)}) collective-permute-start(f32[384,1,128]{2,0,1:T(8,128)} %convolution_bitcast_fusion), channel_id=1, source_target_pairs={{48,0},{64,16},{80,32},{96,48},{112,64},{128,80},{144,96},{160,112... | collective-permute-start | bytes 589832 | tf_op jit(solution)/shard_map/ppermute | solution.py:21
  84.1 453.8 %collective-permute-start.13 = (f32[384,1,128]{2,0,1:T(8,128)}, f32[384,1,128]{2,0,1:T(8,128)}, u32[]{:S(2)}, u32[]{:S(2)}) collective-permute-start(f32[384,1,128]{2,0,1:T(8,128)} %convolution_bitcast_fusion.1), channel_id=1, source_target_pairs={{32,0},{48,16},{64,32},{80,48},{96,64},{112,80},{128,96},{144,112}... | collective-permute-start | bytes 589832 | tf_op jit(solution)/shard_map/ppermute | solution.py:21
  88.4 0.9 copy-start.2
  88.4 3.3 copy-start.4
  88.4 5.7 %copy-start.1 = (bf16[3,384,384]{1,2,0:T(8,128)(2,1)}, bf16[3,384,384]{1,2,0:T(8,128)(2,1)S(1)}, u32[]{:S(2)}) copy-start(bf16[3,384,384]{1,2,0:T(8,128)(2,1)S(1)} %get-tuple-element.50) | copy-start | bytes 2654212
  90.3 435.1 %collective-permute-start.10 = (f32[384,1,128]{2,0,1:T(8,128)}, f32[384,1,128]{2,0,1:T(8,128)}, u32[]{:S(2)}, u32[]{:S(2)}) collective-permute-start(f32[384,1,128]{2,0,1:T(8,128)} %fusion.29), channel_id=1, source_target_pairs={{32,0},{48,16},{64,32},{80,48},{96,64},{112,80},{128,96},{144,112}... | collective-permute-start | bytes 589832 | tf_op jit(solution)/shard_map/ppermute | solution.py:21
  92.7 435.3 %collective-permute-start.11 = (f32[384,1,128]{2,0,1:T(8,128)}, f32[384,1,128]{2,0,1:T(8,128)}, u32[]{:S(2)}, u32[]{:S(2)}) collective-permute-start(f32[384,1,128]{2,0,1:T(8,128)} %fusion.30), channel_id=1, source_target_pairs={{48,0},{64,16},{80,32},{96,48},{112,64},{128,80},{144,96},{160,112... | collective-permute-start | bytes 589832 | tf_op jit(solution)/shard_map/ppermute | solution.py:21
  519.5 3.5 copy-start.5
  521.2 3.2 copy-start.6
  523.0 3.7 copy-start.3
  525.4 10.1 %collective-permute-start.9 = (f32[384,1,128]{2,0,1:T(8,128)}, f32[384,1,128]{2,0,1:T(8,128)}, u32[]{:S(2)}, u32[]{:S(2)}) collective-permute-start(f32[384,1,128]{2,0,1:T(8,128)} %fusion.28), channel_id=1, source_target_pairs={{16,0},{32,16},{48,32},{64,48},{80,64},{96,80},{112,96},{128,112},... | collective-permute-start | bytes 589832 | tf_op jit(solution)/shard_map/ppermute | solution.py:21
Sparse Core Ops, SparseCore 0:
  57.2 462.2 all-reduce.1
where the time goes:
time: 551 us; the launch traced here: 550 us
  waiting for transfers between devices  432 us (78%)
  starting transfers between devices  57.1 us (10%)
  matrix products  26.9 us (5%)
  between operations  14.5 us (3%)
  local copies, waits for them, and re-layouts  11.2 us (2%)
  other arithmetic  8.58 us (2%)
    psum x1, waiting for transfers between devices, on_device(): router_grad = lax.psum(local_router, ('seq', 'ep')) / all_tokens  424 us
    ppermute x15, starting transfers between devices, from_behind(): return lax.ppermute(value, axis, pairs)  49.5 us
  transfers between devices with their start and end apart: 17, of which 2 were waited for; matrix products, arithmetic and copies ran while one was open for 8% of the time, Pallas kernels for 0%

commit v1 on v0

--- a/solution.py
+++ b/solution.py
@@ -19,6 +19,21 @@
     devices = lax.axis_size(axis)
     pairs = [(i, i + by) for i in range(devices) if 0 <= i + by < devices]
     return lax.ppermute(value, axis, pairs)
+
+
+def scatter_sum(flat, axis):
+    parts = flat.reshape(lax.axis_size(axis), -1)
+    return lax.all_to_all(parts, axis, 0, 0, tiled=True).sum(axis=0)
+
+
+def gather_back(flat, axis):
+    copies = jnp.broadcast_to(flat[None], (lax.axis_size(axis),) + flat.shape)
+    return lax.all_to_all(copies, axis, 0, 0, tiled=True).reshape(-1)
+
+
+def sum_everywhere(value):
+    flat = scatter_sum(scatter_sum(value.reshape(-1), "ep"), "seq")
+    return gather_back(gather_back(flat, "seq"), "ep").reshape(value.shape)
 
 
 def allowed_pairs(seg_rows, seg_keys, seq_index, offset, tok_rows):
@@ -171,7 +186,7 @@
         logit_grad.T, normed.astype(jnp.float32), precision=lax.Precision.HIGHEST
     )
     all_tokens = moe_rows * lax.axis_size("seq") * ep_size
-    router_grad = lax.psum(local_router, ("seq", "ep")) / all_tokens
+    router_grad = sum_everywhere(local_router) / all_tokens
     gates = jnp.stack([first_gate, second_gate], axis=1)
     expert_rows = (gates[:, :, None] * moe_grad.astype(jnp.float32)[:, None, :]).astype(
         jnp.bfloat16

time: 551 us -> 198 us (0.36)
  waiting for transfers between devices: 432 us -> 43.4 us
  starting transfers between devices: 57.1 us -> 92.9 us
  between operations: 14.5 us -> 1.13 us
  local copies, waits for them, and re-layouts: 11.2 us -> 17.8 us
  matrix products: 26.9 us -> 32.7 us
    psum x1 -> x0, waiting for transfers between devices: 424 us -> none  [on_device(): router_grad = lax.psum(local_router, ('seq', 'ep')) / all_tokens]
    all_to_all x0 -> x4, starting transfers between devices: none -> 38.9 us  [the longest x2 24.3 us: scatter_sum(): return lax.all_to_all(parts, axis, 0, 0, tiled=True).sum(axis=0)]
    all_to_all x0 -> x4, waiting for transfers between devices: none -> 25.4 us  [the longest x2 15.4 us: gather_back(): return lax.all_to_all(copies, axis, 0, 0, tiled=True).reshape(-1)]
    ppermute x15, waiting for transfers between devices: 7.5 us -> 18 us  [from_behind(): return lax.ppermute(value, axis, pairs)]
  transfers between devices with their start and end apart: 17 -> 20, of which waited for: 2 -> 4; matrix products, arithmetic and copies ran while one was open for 8% -> 27% of each run, Pallas kernels for 0% -> 0%
where the time goes in v1:
time: 198 us; the launch traced here: 197 us
  starting transfers between devices  92.9 us (47%)
  waiting for transfers between devices  43.4 us (22%)
  matrix products  32.7 us (17%)
  local copies, waits for them, and re-layouts  17.8 us (9%)
  other arithmetic  9.25 us (5%)
    ppermute x15, starting transfers between devices, from_behind(): return lax.ppermute(value, axis, pairs)  49.5 us
    all_to_all x2, starting transfers between devices, scatter_sum(): return lax.all_to_all(parts, axis, 0, 0, tiled=True).sum(axis=0)  24.3 us
    ppermute x15, waiting for transfers between devices, from_behind(): return lax.ppermute(value, axis, pairs)  18 us
    all_to_all x2, waiting for transfers between devices, gather_back(): return lax.all_to_all(copies, axis, 0, 0, tiled=True).reshape(-1)  15.4 us
    all_to_all x2, starting transfers between devices, gather_back(): return lax.all_to_all(copies, axis, 0, 0, tiled=True).reshape(-1)  14.6 us
    all_to_all x2, waiting for transfers between devices, scatter_sum(): return lax.all_to_all(parts, axis, 0, 0, tiled=True).sum(axis=0)  9.99 us
    dot_general x4, matrix products, block_grads(): jnp.einsum('hgqt,qhgd->thd', score_low, query_rows, preferred_element_typ...  7.95 us
    unnamed x29, local copies, waits for them, and re-layouts  7.21 us
  transfers between devices with their start and end apart: 20, of which 4 were waited for; matrix products, arithmetic and copies ran while one was open for 27% of the time, Pallas kernels for 0%

profile of v1, /device:TPU:1, one launch (start us, length us, event | category | flops | bytes accessed | tf_op | source)
XLA Modules:
  0.0 197.1 jit_solution(14860994869699326662)
XLA Ops:
  0.6 5.8 %collective-permute-start = (s32[384]{0:T(512)}, s32[384]{0:T(512)S(1)}, u32[]{:S(2)}, u32[]{:S(2)}) collective-permute-start(s32[384]{0:T(512)} %param.14), channel_id=1, source_target_pairs={{0,16},{16,32},{32,48},{48,64},{64,80},{80,96},{96,112},{112,128},... | collective-permute-start | bytes 4616 | tf_op jit(solution)/shard_map/ppermute | solution.py:21
  6.4 3.5 %collective-permute-start.2 = (s32[384]{0:T(512)}, s32[384]{0:T(512)S(1)}, u32[]{:S(2)}, u32[]{:S(2)}) collective-permute-start(s32[384]{0:T(512)} %param.14), channel_id=1, source_target_pairs={{0,32},{16,48},{32,64},{48,80},{64,96},{80,112},{96,128},{112,144}... | collective-permute-start | bytes 4616 | tf_op jit(solution)/shard_map/ppermute | solution.py:21
  10.0 4.7 %collective-permute-start.4 = (s32[384]{0:T(512)}, s32[384]{0:T(512)S(1)}, u32[]{:S(2)}, u32[]{:S(2)}) collective-permute-start(s32[384]{0:T(512)} %param.14), channel_id=1, source_target_pairs={{0,48},{16,64},{32,80},{48,96},{64,112},{80,128},{96,144},{112,160... | collective-permute-start | bytes 4616 | tf_op jit(solution)/shard_map/ppermute | solution.py:21
  14.7 8.0 %collective-permute-start.5 = (bf16[384,1,128]{2,0,1:T(8,128)(2,1)}, bf16[384,1,128]{2,0,1:T(8,128)(2,1)}, u32[]{:S(2)}, u32[]{:S(2)}) collective-permute-start(bf16[384,1,128]{2,0,1:T(8,128)(2,1)} %bitcast.4), channel_id=1, source_target_pairs={{0,48},{16,64},{32,80},{48,96},{64,112},{80,128},{96,144},{112,160... | collective-permute-start | bytes 294920 | tf_op jit(solution)/shard_map/ppermute | solution.py:21
  22.7 3.3 %collective-permute-start.1 = (bf16[384,1,128]{2,0,1:T(8,128)(2,1)}, bf16[384,1,128]{2,0,1:T(8,128)(2,1)S(1)}, u32[]{:S(2)}, u32[]{:S(2)}) collective-permute-start(bf16[384,1,128]{2,0,1:T(8,128)(2,1)} %bitcast.4), channel_id=1, source_target_pairs={{0,16},{16,32},{32,48},{48,64},{64,80},{80,96},{96,112},{112,128},... | collective-permute-start | bytes 294920 | tf_op jit(solution)/shard_map/ppermute | solution.py:21
  26.7 1.2 fusion.103
  28.6 2.4 %fusion.65 = f32[24,1,2]{2,1,0:T(1,128)S(1)} fusion(bf16[24,2,6144]{2,1,0:T(2,128)(2,1)S(1)} %copy-done, bf16[24,6144,1]{1,0,2:T(8,128)(2,1)} %bitcast.333), kind=kOutput, calls=%fused_computation.98 | convolution fusion | flops 589824 | bytes 884928 | tf_op jit(solution)/shard_map/td,tkd->tk/dot_general | solution.py:179
  31.4 0.9 all_to_all.30
  32.4 7.4 %all-to-all-start = ((f32[16,1,3072]{2,1,0:T(1,128)}), f32[16,1,3072]{2,1,0:T(1,128)S(1)}, u32[]{:S(2)}, u32[]{:S(2)}) async-start(f32[16,1,3072]{2,1,0:T(1,128)} %all_to_all.30), calls=%async_computation | async-start | bytes 393216 | tf_op jit(solution)/shard_map/all_to_all | solution.py:26
  39.9 1.2 convolution_convert_fusion
  41.5 2.0 %sort.17 = (s32[48]{0:T(128)}, s32[48]{0:T(128)S(1)}) sort(s32[48]{0:T(128)S(1)} %multiply_add_fusion.1, s32[48]{0:T(128)S(1)} %iota.37), dimensions={0}, to_apply=%region_17.18 | sort | flops 288 | bytes 768 | tf_op jit(solution)/shard_map/jit(argsort)/sort | solution.py:197
  46.3 1.2 copy.145
  48.3 1.1 reshape.437
  49.5 2.9 %collective-permute-start.3 = (bf16[384,1,128]{2,0,1:T(8,128)(2,1)}, bf16[384,1,128]{2,0,1:T(8,128)(2,1)S(1)}, u32[]{:S(2)}, u32[]{:S(2)}) collective-permute-start(bf16[384,1,128]{2,0,1:T(8,128)(2,1)} %bitcast.4), channel_id=1, source_target_pairs={{0,32},{16,48},{32,64},{48,80},{64,96},{80,112},{96,128},{112,144}... | collective-permute-start | bytes 294920 | tf_op jit(solution)/shard_map/ppermute | solution.py:21
  52.4 4.5 %collective-permute-start.6 = (bf16[384,1,128]{2,0,1:T(8,128)(2,1)}, bf16[384,1,128]{2,0,1:T(8,128)(2,1)S(1)}, u32[]{:S(2)}, u32[]{:S(2)}) collective-permute-start(bf16[384,1,128]{2,0,1:T(8,128)(2,1)} %bitcast.22), channel_id=1, source_target_pairs={{0,16},{16,32},{32,48},{48,64},{64,80},{80,96},{96,112},{112,128},... | collective-permute-start | bytes 294920 | tf_op jit(solution)/shard_map/ppermute | solution.py:21
  57.0 6.2 %collective-permute-start.8 = (bf16[384,1,128]{2,0,1:T(8,128)(2,1)}, bf16[384,1,128]{2,0,1:T(8,128)(2,1)S(1)}, u32[]{:S(2)}, u32[]{:S(2)}) collective-permute-start(bf16[384,1,128]{2,0,1:T(8,128)(2,1)} %bitcast.22), channel_id=1, source_target_pairs={{0,48},{16,64},{32,80},{48,96},{64,112},{80,128},{96,144},{112,160... | collective-permute-start | bytes 294920 | tf_op jit(solution)/shard_map/ppermute | solution.py:21
  64.0 1.4 fusion.102
  65.4 2.7 %collective-permute-start.7 = (bf16[384,1,128]{2,0,1:T(8,128)(2,1)}, bf16[384,1,128]{2,0,1:T(8,128)(2,1)S(1)}, u32[]{:S(2)}, u32[]{:S(2)}) collective-permute-start(bf16[384,1,128]{2,0,1:T(8,128)(2,1)} %bitcast.22), channel_id=1, source_target_pairs={{0,32},{16,48},{32,64},{48,80},{64,96},{80,112},{96,128},{112,144}... | collective-permute-start | bytes 294920 | tf_op jit(solution)/shard_map/ppermute | solution.py:21
  68.0 1.4 fusion.99
  70.3 1.5 fusion.9
  73.9 1.1 convolution_bitcast_fusion.2
  75.0 1.1 convolution_bitcast_fusion
  76.2 1.1 convolution_bitcast_fusion.1
  77.3 1.3 collective-permute-start.12
  78.6 1.3 collective-permute-start.14
  79.9 1.5 collective-permute-start.13
  81.4 3.0 %fusion.51 = (bf16[3,384,384]{1,2,0:T(8,128)(2,1)S(1)}, bf16[3,384,384]{1,2,0:T(8,128)(2,1)}, bf16[3,384,384]{1,2,0:T(8,128)(2,1)}, bf16[3,384,384]{1,2,0:T(8,128)(2,1)}) fusion(f32[384,384,3]{1,0,2:T(8,128)S(1)} %get-tuple-element.71, f32[1,3,384,384]{2,3,1,0:T(8,128)S(1)} %get-tuple-element.65, f32[3,384]{1,0:T(4,128)S(1)} %add_divide_fusion, ...), kind=kLoop, calls=%fused_computation.80 | loop fusion | flops 8847360 | bytes 18293760 | tf_op jit(solution)/shard_map/reshape.57
  85.3 1.1 fusion.29
  86.4 1.3 collective-permute-start.10
  88.5 16.9 %all-to-all-start.1 = ((f32[32,1,96]{2,1,0:T(1,128)}), f32[32,1,96]{2,1,0:T(1,128)S(1)}, u32[]{:S(2)}, u32[]{:S(2)}) async-start(f32[32,1,96]{2,1,0:T(1,128)} %all_to_all.25), calls=%async_computation.1 | async-start | bytes 32768 | tf_op jit(solution)/shard_map/all_to_all | solution.py:26
  105.4 2.2 %fusion.30 = f32[384,1,128]{2,0,1:T(8,128)} fusion(bf16[3,384,384]{1,2,0:T(8,128)(2,1)} %get-tuple-element.55, bf16[384,3,128]{0,2,1:T(8,128)(2,1)S(1)} %bitcast.320), kind=kOutput, calls=%fused_computation.63 | convolution fusion | flops 113295360 | bytes 1376256 | tf_op jit(solution)/shard_map/hgqt,qhgd->thd/dot_general | solution.py:90
  107.7 1.3 collective-permute-start.11
  109.0 10.0 %all-to-all-done.1 = f32[32,1,96]{2,1,0:T(1,128)S(1)} async-done(((f32[32,1,96]{2,1,0:T(1,128)}), f32[32,1,96]{2,1,0:T(1,128)S(1)}, u32[]{:S(2)}, u32[]{:S(2)}) %all-to-all-start.1) | async-done | bytes 12320 | tf_op jit(solution)/shard_map/all_to_all | solution.py:26
  119.6 4.9 %all-to-all-start.2 = ((f32[32,1,96]{2,1,0:T(1,128)}), f32[32,1,96]{2,1,0:T(1,128)S(1)}, u32[]{:S(2)}, u32[]{:S(2)}) async-start(f32[32,1,96]{2,1,0:T(1,128)} %broadcast_in_dim.110), calls=%async_computation.2 | async-start | bytes 32768 | tf_op jit(solution)/shard_map/all_to_all | solution.py:31
  124.5 2.4 %fusion.82 = f32[3,384,128]{1,2,0:T(8,128)} fusion(bf16[3,384,384]{1,2,0:T(8,128)(2,1)} %get-tuple-element.56, bf16[384,128]{1,0:T(8,128)(2,1)} %param.11), kind=kOutput, calls=%fused_computation.116 | convolution fusion | flops 113246208 | bytes 1572864 | tf_op jit(solution)/shard_map/hgqt,thd->qhgd/dot_general | solution.py:86
  126.9 11.1 %all-to-all-done.2 = f32[32,1,96]{2,1,0:T(1,128)S(1)} async-done(((f32[32,1,96]{2,1,0:T(1,128)}), f32[32,1,96]{2,1,0:T(1,128)S(1)}, u32[]{:S(2)}, u32[]{:S(2)}) %all-to-all-start.2) | async-done | bytes 12320 | tf_op jit(solution)/shard_map/all_to_all | solution.py:31
  140.1 9.6 %all-to-all-start.3 = ((f32[16,1,3072]{2,1,0:T(1,128)}), f32[16,1,3072]{2,1,0:T(1,128)S(1)}, u32[]{:S(2)}, u32[]{:S(2)}) async-start(f32[16,1,3072]{2,1,0:T(1,128)} %broadcast_in_dim.112), calls=%async_computation.3 | async-start | bytes 393216 | tf_op jit(solution)/shard_map/all_to_all | solution.py:31
  149.7 2.5 %convolution_add_fusion.1 = f32[3,384,128]{1,2,0:T(8,128)} fusion(f32[3,384,128]{1,2,0:T(8,128)} %fusion.82, bf16[3,384,384]{1,2,0:T(8,128)(2,1)} %get-tuple-element.54, bf16[384,1,128]{2,0,1:T(8,128)(2,1)S(1)} %collective-permute-done.1), kind=kOutput, calls=%fused_computation.43 | convolution fusion | flops 113393664 | bytes 2162688 | tf_op jit(solution)/shard_map/hgqt,thd->qhgd/dot_general | solution.py:86
  152.3 4.2 %all-to-all-done.3 = f32[16,1,3072]{2,1,0:T(1,128)S(1)} async-done(((f32[16,1,3072]{2,1,0:T(1,128)}), f32[16,1,3072]{2,1,0:T(1,128)S(1)}, u32[]{:S(2)}, u32[]{:S(2)}) %all-to-all-start.3) | async-done | bytes 196640 | tf_op jit(solution)/shard_map/all_to_all | solution.py:31
  156.5 2.5 %broadcast_in_dim.114 = bf16[8,2,6,6144]{3,2,1,0:T(8,128)(2,1)} broadcast(bf16[8,6,6144]{2,1,0:T(8,128)(2,1)} %reshape.437), dimensions={0,2,3} | broadcast | bytes 1769472 | tf_op jit(solution)/shard_map/broadcast_in_dim | solution.py:199
  159.0 4.5 %all-to-all-start.4 = ((bf16[16,6,6144]{2,1,0:T(8,128)(2,1)}), bf16[16,6,6144]{2,1,0:T(8,128)(2,1)}, u32[]{:S(2)}, u32[]{:S(2)}) async-start(bf16[16,6,6144]{2,1,0:T(8,128)(2,1)} %bitcast.331), calls=%async_computation.4 | async-start | bytes 3145728 | tf_op jit(solution)/shard_map/all_to_all | solution.py:200
  163.6 1.7 fusion.75
  165.2 2.2 %fusion.28 = f32[384,1,128]{2,0,1:T(8,128)} fusion(bf16[3,384,384]{1,2,0:T(8,128)(2,1)} %get-tuple-element.54, bf16[384,3,128]{0,2,1:T(8,128)(2,1)S(1)} %bitcast.321), kind=kOutput, calls=%fused_computation.61 | convolution fusion | flops 113295360 | bytes 1376256 | tf_op jit(solution)/shard_map/hgqt,qhgd->thd/dot_general | solution.py:90
  167.5 1.3 collective-permute-start.9
  170.1 18.0 %collective-permute-done.9 = f32[384,1,128]{2,0,1:T(8,128)} collective-permute-done((f32[384,1,128]{2,0,1:T(8,128)}, f32[384,1,128]{2,0,1:T(8,128)}, u32[]{:S(2)}, u32[]{:S(2)}) %collective-permute-start.9) | collective-permute-done | bytes 196640 | tf_op jit(solution)/shard_map/ppermute | solution.py:21
  188.0 2.4 %fusion.40 = bf16[384,128]{1,0:T(8,128)(2,1)} fusion(f32[384,1,128]{2,0,1:T(8,128)} %collective-permute-done.11, f32[384,1,128]{2,0,1:T(8,128)} %collective-permute-done.10, f32[384,1,128]{2,0,1:T(8,128)} %collective-permute-done.9, bf16[3,384,384]{1,2,0:T(8,128)(2,1)} %get-tuple-element.56, bf16[384,3,128]{0,2,1:T(8,128)(2,1)S(1)} %bitcast.322), kind=kOutput, calls=%fused_computation.73 | convolution fusion | flops 113491968 | bytes 1867776 | tf_op jit(solution)/shard_map/hgqt,qhgd->thd/dot_general | solution.py:90
  190.5 2.2 %fusion.39 = bf16[384,128]{1,0:T(8,128)(2,1)} fusion(f32[384,1,128]{2,0,1:T(8,128)} %collective-permute-done.14, f32[384,1,128]{2,0,1:T(8,128)} %collective-permute-done.13, f32[384,1,128]{2,0,1:T(8,128)} %collective-permute-done.12, bf16[384,3,128]{0,2,1:T(8,128)(2,1)S(1)} %bitcast.330, f32[1,3,384,384]{2,3,1,0:T(8,128)S(1)} %get-tuple-element.69, ...), kind=kOutput, calls=%fused_computation.72 | convolution fusion | flops 114769920 | bytes 2904576 | tf_op jit(solution)/shard_map/hgqt,qhgd->thd/dot_general | solution.py:78
  194.0 3.1 %copy.171 = bf16[16,6,6144]{2,0,1:T(8,128)(2,1)} copy(bf16[16,6,6144]{2,1,0:T(8,128)(2,1)} %all-to-all-done.4) | data formatting | bytes 2359296
  (86 shorter events, 16.8 us)
Async XLA Ops:
  0.6 28.0 %copy-start = (bf16[24,2,6144]{2,1,0:T(2,128)(2,1)S(1)}, bf16[24,2,6144]{2,1,0:T(2,128)(2,1)}, u32[]{:S(2)}) copy-start(bf16[24,2,6144]{2,1,0:T(2,128)(2,1)} %param.16) | copy-start | bytes 1769476
  0.6 48.8 %collective-permute-start = (s32[384]{0:T(512)}, s32[384]{0:T(512)S(1)}, u32[]{:S(2)}, u32[]{:S(2)}) collective-permute-start(s32[384]{0:T(512)} %param.14), channel_id=1, source_target_pairs={{0,16},{16,32},{32,48},{48,64},{64,80},{80,96},{96,112},{112,128},... | collective-permute-start | bytes 4616 | tf_op jit(solution)/shard_map/ppermute | solution.py:21
  6.4 46.0 %collective-permute-start.2 = (s32[384]{0:T(512)}, s32[384]{0:T(512)S(1)}, u32[]{:S(2)}, u32[]{:S(2)}) collective-permute-start(s32[384]{0:T(512)} %param.14), channel_id=1, source_target_pairs={{0,32},{16,48},{32,64},{48,80},{64,96},{80,112},{96,128},{112,144}... | collective-permute-start | bytes 4616 | tf_op jit(solution)/shard_map/ppermute | solution.py:21
  10.0 47.0 %collective-permute-start.4 = (s32[384]{0:T(512)}, s32[384]{0:T(512)S(1)}, u32[]{:S(2)}, u32[]{:S(2)}) collective-permute-start(s32[384]{0:T(512)} %param.14), channel_id=1, source_target_pairs={{0,48},{16,64},{32,80},{48,96},{64,112},{80,128},{96,144},{112,160... | collective-permute-start | bytes 4616 | tf_op jit(solution)/shard_map/ppermute | solution.py:21
  14.7 50.7 %collective-permute-start.5 = (bf16[384,1,128]{2,0,1:T(8,128)(2,1)}, bf16[384,1,128]{2,0,1:T(8,128)(2,1)}, u32[]{:S(2)}, u32[]{:S(2)}) collective-permute-start(bf16[384,1,128]{2,0,1:T(8,128)(2,1)} %bitcast.4), channel_id=1, source_target_pairs={{0,48},{16,64},{32,80},{48,96},{64,112},{80,128},{96,144},{112,160... | collective-permute-start | bytes 294920 | tf_op jit(solution)/shard_map/ppermute | solution.py:21
  22.7 46.7 %collective-permute-start.1 = (bf16[384,1,128]{2,0,1:T(8,128)(2,1)}, bf16[384,1,128]{2,0,1:T(8,128)(2,1)S(1)}, u32[]{:S(2)}, u32[]{:S(2)}) collective-permute-start(bf16[384,1,128]{2,0,1:T(8,128)(2,1)} %bitcast.4), channel_id=1, source_target_pairs={{0,16},{16,32},{32,48},{48,64},{64,80},{80,96},{96,112},{112,128},... | collective-permute-start | bytes 294920 | tf_op jit(solution)/shard_map/ppermute | solution.py:21
  28.6 2.6 %copy-start.4 = (bf16[24,6144]{1,0:T(8,128)(2,1)S(1)}, bf16[24,6144]{1,0:T(8,128)(2,1)}, u32[]{:S(2)}) copy-start(bf16[24,6144]{1,0:T(8,128)(2,1)} %param.17) | copy-start | bytes 884740
  28.6 11.2 %copy-start.10 = (s32[24,2]{0,1:T(2,128)S(1)}, s32[24,2]{0,1:T(2,128)}, u32[]{:S(2)}) copy-start(s32[24,2]{0,1:T(2,128)} %param.19) | copy-start | bytes 580
  28.6 11.3 %copy-start.7 = (bf16[8,6144]{1,0:T(8,128)(2,1)S(1)}, bf16[8,6144]{1,0:T(8,128)(2,1)}, u32[]{:S(2)}) copy-start(bf16[8,6144]{1,0:T(8,128)(2,1)} %param.18) | copy-start | bytes 294916
  31.1 12.7 %copy-start.9 = (bf16[24,6144]{1,0:T(8,128)(2,1)S(1)}, bf16[24,6144]{1,0:T(8,128)(2,1)}, u32[]{:S(2)}) copy-start(bf16[24,6144]{1,0:T(8,128)(2,1)} %param.15) | copy-start | bytes 884740
  32.4 55.3 %all-to-all-start = ((f32[16,1,3072]{2,1,0:T(1,128)}), f32[16,1,3072]{2,1,0:T(1,128)S(1)}, u32[]{:S(2)}, u32[]{:S(2)}) async-start(f32[16,1,3072]{2,1,0:T(1,128)} %all_to_all.30), calls=%async_computation | async-start | bytes 393216 | tf_op jit(solution)/shard_map/all_to_all | solution.py:26
  45.1 1.0 copy-start.8
  47.4 15.7 %copy-start.11 = (s32[384]{0:T(512)S(1)}, s32[384]{0:T(512)}, u32[]{:S(2)}) copy-start(s32[384]{0:T(512)} %param.14) | copy-start | bytes 4612
  49.5 20.4 %collective-permute-start.3 = (bf16[384,1,128]{2,0,1:T(8,128)(2,1)}, bf16[384,1,128]{2,0,1:T(8,128)(2,1)S(1)}, u32[]{:S(2)}, u32[]{:S(2)}) collective-permute-start(bf16[384,1,128]{2,0,1:T(8,128)(2,1)} %bitcast.4), channel_id=1, source_target_pairs={{0,32},{16,48},{32,64},{48,80},{64,96},{80,112},{96,128},{112,144}... | collective-permute-start | bytes 294920 | tf_op jit(solution)/shard_map/ppermute | solution.py:21
  52.4 19.5 %collective-permute-start.6 = (bf16[384,1,128]{2,0,1:T(8,128)(2,1)}, bf16[384,1,128]{2,0,1:T(8,128)(2,1)S(1)}, u32[]{:S(2)}, u32[]{:S(2)}) collective-permute-start(bf16[384,1,128]{2,0,1:T(8,128)(2,1)} %bitcast.22), channel_id=1, source_target_pairs={{0,16},{16,32},{32,48},{48,64},{64,80},{80,96},{96,112},{112,128},... | collective-permute-start | bytes 294920 | tf_op jit(solution)/shard_map/ppermute | solution.py:21
  57.0 15.6 %collective-permute-start.8 = (bf16[384,1,128]{2,0,1:T(8,128)(2,1)}, bf16[384,1,128]{2,0,1:T(8,128)(2,1)S(1)}, u32[]{:S(2)}, u32[]{:S(2)}) collective-permute-start(bf16[384,1,128]{2,0,1:T(8,128)(2,1)} %bitcast.22), channel_id=1, source_target_pairs={{0,48},{16,64},{32,80},{48,96},{64,112},{80,128},{96,144},{112,160... | collective-permute-start | bytes 294920 | tf_op jit(solution)/shard_map/ppermute | solution.py:21
  65.4 7.9 %collective-permute-start.7 = (bf16[384,1,128]{2,0,1:T(8,128)(2,1)}, bf16[384,1,128]{2,0,1:T(8,128)(2,1)S(1)}, u32[]{:S(2)}, u32[]{:S(2)}) collective-permute-start(bf16[384,1,128]{2,0,1:T(8,128)(2,1)} %bitcast.22), channel_id=1, source_target_pairs={{0,32},{16,48},{32,64},{48,80},{64,96},{80,112},{96,128},{112,144}... | collective-permute-start | bytes 294920 | tf_op jit(solution)/shard_map/ppermute | solution.py:21
  77.3 113.2 %collective-permute-start.12 = (f32[384,1,128]{2,0,1:T(8,128)}, f32[384,1,128]{2,0,1:T(8,128)}, u32[]{:S(2)}, u32[]{:S(2)}) collective-permute-start(f32[384,1,128]{2,0,1:T(8,128)} %convolution_bitcast_fusion.2), channel_id=1, source_target_pairs={{16,0},{32,16},{48,32},{64,48},{80,64},{96,80},{112,96},{128,112},... | collective-permute-start | bytes 589832 | tf_op jit(solution)/shard_map/ppermute | solution.py:21
  78.6 111.9 %collective-permute-start.14 = (f32[384,1,128]{2,0,1:T(8,128)}, f32[384,1,128]{2,0,1:T(8,128)}, u32[]{:S(2)}, u32[]{:S(2)}) collective-permute-start(f32[384,1,128]{2,0,1:T(8,128)} %convolution_bitcast_fusion), channel_id=1, source_target_pairs={{48,0},{64,16},{80,32},{96,48},{112,64},{128,80},{144,96},{160,112... | collective-permute-start | bytes 589832 | tf_op jit(solution)/shard_map/ppermute | solution.py:21
  79.9 110.6 %collective-permute-start.13 = (f32[384,1,128]{2,0,1:T(8,128)}, f32[384,1,128]{2,0,1:T(8,128)}, u32[]{:S(2)}, u32[]{:S(2)}) collective-permute-start(f32[384,1,128]{2,0,1:T(8,128)} %convolution_bitcast_fusion.1), channel_id=1, source_target_pairs={{32,0},{48,16},{64,32},{80,48},{96,64},{112,80},{128,96},{144,112}... | collective-permute-start | bytes 589832 | tf_op jit(solution)/shard_map/ppermute | solution.py:21
  84.4 0.9 copy-start.1
  86.4 81.1 %collective-permute-start.10 = (f32[384,1,128]{2,0,1:T(8,128)}, f32[384,1,128]{2,0,1:T(8,128)}, u32[]{:S(2)}, u32[]{:S(2)}) collective-permute-start(f32[384,1,128]{2,0,1:T(8,128)} %fusion.29), channel_id=1, source_target_pairs={{32,0},{48,16},{64,32},{80,48},{96,64},{112,80},{128,96},{144,112}... | collective-permute-start | bytes 589832 | tf_op jit(solution)/shard_map/ppermute | solution.py:21
  88.5 30.4 %all-to-all-start.1 = ((f32[32,1,96]{2,1,0:T(1,128)}), f32[32,1,96]{2,1,0:T(1,128)S(1)}, u32[]{:S(2)}, u32[]{:S(2)}) async-start(f32[32,1,96]{2,1,0:T(1,128)} %all_to_all.25), calls=%async_computation.1 | async-start | bytes 32768 | tf_op jit(solution)/shard_map/all_to_all | solution.py:26
  107.7 62.4 %collective-permute-start.11 = (f32[384,1,128]{2,0,1:T(8,128)}, f32[384,1,128]{2,0,1:T(8,128)}, u32[]{:S(2)}, u32[]{:S(2)}) collective-permute-start(f32[384,1,128]{2,0,1:T(8,128)} %fusion.30), channel_id=1, source_target_pairs={{48,0},{64,16},{80,32},{96,48},{112,64},{128,80},{144,96},{160,112... | collective-permute-start | bytes 589832 | tf_op jit(solution)/shard_map/ppermute | solution.py:21
  119.6 18.5 %all-to-all-start.2 = ((f32[32,1,96]{2,1,0:T(1,128)}), f32[32,1,96]{2,1,0:T(1,128)S(1)}, u32[]{:S(2)}, u32[]{:S(2)}) async-start(f32[32,1,96]{2,1,0:T(1,128)} %broadcast_in_dim.110), calls=%async_computation.2 | async-start | bytes 32768 | tf_op jit(solution)/shard_map/all_to_all | solution.py:31
  140.1 16.4 %all-to-all-start.3 = ((f32[16,1,3072]{2,1,0:T(1,128)}), f32[16,1,3072]{2,1,0:T(1,128)S(1)}, u32[]{:S(2)}, u32[]{:S(2)}) async-start(f32[16,1,3072]{2,1,0:T(1,128)} %broadcast_in_dim.112), calls=%async_computation.3 | async-start | bytes 393216 | tf_op jit(solution)/shard_map/all_to_all | solution.py:31
  156.5 2.5 %copy-start.5 = (f32[16,1,3072]{2,1,0:T(1,128)}, f32[16,1,3072]{2,1,0:T(1,128)S(1)}, u32[]{:S(2)}) copy-start(f32[16,1,3072]{2,1,0:T(1,128)S(1)} %all-to-all-done.3) | copy-start | bytes 589828
  159.0 35.0 %all-to-all-start.4 = ((bf16[16,6,6144]{2,1,0:T(8,128)(2,1)}), bf16[16,6,6144]{2,1,0:T(8,128)(2,1)}, u32[]{:S(2)}, u32[]{:S(2)}) async-start(bf16[16,6,6144]{2,1,0:T(8,128)(2,1)} %bitcast.331), calls=%async_computation.4 | async-start | bytes 3145728 | tf_op jit(solution)/shard_map/all_to_all | solution.py:200
  163.6 5.2 %copy-start.2 = (bf16[3,384,384]{1,2,0:T(8,128)(2,1)S(1)}, bf16[3,384,384]{1,2,0:T(8,128)(2,1)}, u32[]{:S(2)}) copy-start(bf16[3,384,384]{1,2,0:T(8,128)(2,1)} %copy-done.1) | copy-start | bytes 2654212
  163.6 5.2 %copy-start.3 = (f32[3,384,128]{1,2,0:T(8,128)S(1)}, f32[3,384,128]{1,2,0:T(8,128)}, u32[]{:S(2)}) copy-start(f32[3,384,128]{1,2,0:T(8,128)} %convolution_add_fusion.1) | copy-start | bytes 1769476
  167.5 20.6 %collective-permute-start.9 = (f32[384,1,128]{2,0,1:T(8,128)}, f32[384,1,128]{2,0,1:T(8,128)}, u32[]{:S(2)}, u32[]{:S(2)}) collective-permute-start(f32[384,1,128]{2,0,1:T(8,128)} %fusion.28), channel_id=1, source_target_pairs={{16,0},{32,16},{48,32},{64,48},{80,64},{96,80},{112,96},{128,112},... | collective-permute-start | bytes 589832 | tf_op jit(solution)/shard_map/ppermute | solution.py:21
  190.4 2.3 %copy-start.6 = (f32[16,1,3072]{2,1,0:T(1,128)S(1)}, f32[16,1,3072]{2,1,0:T(1,128)}, u32[]{:S(2)}) copy-start(f32[16,1,3072]{2,1,0:T(1,128)} %copy-done.5) | copy-start | bytes 589828

commit v2 on v1

--- a/solution.py
+++ b/solution.py
@@ -19,6 +19,21 @@
     devices = lax.axis_size(axis)
     pairs = [(i, i + by) for i in range(devices) if 0 <= i + by < devices]
     return lax.ppermute(value, axis, pairs)
+
+
+def pack_block(key_block, value_block, segments):
+    tok_rows = key_block.shape[0]
+    width = 2 * key_block.shape[1] * HD
+    rows = jnp.concatenate([key_block, value_block], axis=-1).reshape(tok_rows, width)
+    segs = segments.astype(jnp.bfloat16).reshape(-1, HD)
+    segs = jnp.pad(segs, ((0, 8 - segs.shape[0] % 8), (0, width - HD)))
+    return jnp.concatenate([rows, segs], axis=0)
+
+
+def unpack_block(packed, tok_rows, kv_heads):
+    rows = packed[:tok_rows].reshape(tok_rows, kv_heads, 2 * HD)
+    segs = packed[tok_rows : tok_rows + tok_rows // HD, :HD].reshape(tok_rows)
+    return rows[..., :HD], rows[..., HD:], segs.astype(jnp.int32)
 
 
 def scatter_sum(flat, axis):
@@ -116,8 +131,9 @@
     seq_index = lax.axis_index("seq")
     ep_size = lax.axis_size("ep")
     gathered = [(key_block, value_block, segments)]
+    packed = pack_block(key_block, value_block, segments)
     for offset in range(1, REACH + 1):
-        gathered.append(from_behind((key_block, value_block, segments), "seq", offset))
+        gathered.append(unpack_block(from_behind(packed, "seq", offset), tok_rows, kv_heads))
     stat_shape = (kv_heads, group_size, tok_rows)
     running = (
         jnp.full(stat_shape, MASKED, jnp.float32),
@@ -161,7 +177,9 @@
     key_total = parts[0][1]
     value_total = parts[0][2]
     for offset in range(1, REACH + 1):
-        key_back, value_back = from_behind((parts[offset][1], parts[offset][2]), "seq", -offset)
+        both = jnp.concatenate([parts[offset][1], parts[offset][2]], axis=-1)
+        both = from_behind(both, "seq", -offset)
+        key_back, value_back = both[..., :HD], both[..., HD:]
         key_total = key_total + key_back
         value_total = value_total + value_back
     query_grad = query_total.reshape(tok_rows, -1).astype(jnp.bfloat16)

time: 198 us -> 163 us (0.82); the launches traced: 197 us -> 160 us
  starting transfers between devices: 92.9 us -> 67.8 us
  waiting for transfers between devices: 43.4 us -> 24.9 us
  matrix products: 32.7 us -> 24.2 us
  other arithmetic: 9.25 us -> 17.5 us
  local copies, waits for them, and re-layouts: 17.8 us -> 24.2 us
    ppermute x15 -> x6, starting transfers between devices: 49.5 us -> 18.4 us  [from_behind(): return lax.ppermute(value, axis, pairs)]
    ppermute x15 -> x6, waiting for transfers between devices: 18 us -> 0.02 us  [from_behind(): return lax.ppermute(value, axis, pairs)]
    all_to_all x2, waiting for transfers between devices: 9.99 us -> 0.01 us  [scatter_sum(): return lax.all_to_all(parts, axis, 0, 0, tiled=True).sum(axis=0)]
    all_to_all x2, starting transfers between devices: 14.6 us -> 23.5 us  [gather_back(): return lax.all_to_all(copies, axis, 0, 0, tiled=True).reshape(-1)]
    all_to_all x1, waiting for transfers between devices: 0.01 us -> 7.61 us  [on_device(): lax.all_to_all(outgoing, 'ep', split_axis=0, concat_axis=0, tiled=True)]
    dot_general x4, matrix products: 7.95 us -> 4.08 us  [block_grads(): jnp.einsum('hgqt,qhgd->thd', score_low, query_rows, preferred_element_typ...]
    concatenate x0 -> x4, other arithmetic: none -> 3.34 us  [the longest x3 3.32 us: on_device(): both = jnp.concatenate([parts[offset][1], parts[offset][2]], axis=-1)]
    all_to_all x2, starting transfers between devices: 24.3 us -> 21.3 us  [scatter_sum(): return lax.all_to_all(parts, axis, 0, 0, tiled=True).sum(axis=0)]
  transfers between devices with their start and end apart: 20 -> 11, of which waited for: 4 -> 3; matrix products, arithmetic and copies ran while one was open for 27% -> 37% of each run, Pallas kernels for 0% -> 0%
where the time goes in v2:
time: 163 us; the launch traced here: 160 us
  starting transfers between devices  67.8 us (42%)
  waiting for transfers between devices  24.9 us (15%)
  local copies, waits for them, and re-layouts  24.2 us (15%)
  matrix products  24.2 us (15%)
  other arithmetic  17.5 us (11%)
    all_to_all x2, starting transfers between devices, gather_back(): return lax.all_to_all(copies, axis, 0, 0, tiled=True).reshape(-1)  23.5 us
    all_to_all x2, starting transfers between devices, scatter_sum(): return lax.all_to_all(parts, axis, 0, 0, tiled=True).sum(axis=0)  21.3 us
    ppermute x6, starting transfers between devices, from_behind(): return lax.ppermute(value, axis, pairs)  18.4 us
    all_to_all x2, waiting for transfers between devices, gather_back(): return lax.all_to_all(copies, axis, 0, 0, tiled=True).reshape(-1)  17.3 us
    all_to_all x1, waiting for transfers between devices, on_device(): lax.all_to_all(outgoing, 'ep', split_axis=0, concat_axis=0, tiled=True)  7.61 us
    dot_general x4, matrix products, block_grads(): jnp.einsum('hgqt,thd->qhgd', score_low, key_block, preferred_element_type...  7.37 us
    unnamed x53, local copies, waits for them, and re-layouts  6.38 us
    all_to_all x1, starting transfers between devices, on_device(): lax.all_to_all(outgoing, 'ep', split_axis=0, concat_axis=0, tiled=True)  4.52 us
  transfers between devices with their start and end apart: 11, of which 3 were waited for; matrix products, arithmetic and copies ran while one was open for 37% of the time, Pallas kernels for 0%

profile of v2, /device:TPU:1, one launch (start us, length us, event | category | flops | bytes accessed | tf_op | source)
XLA Modules:
  0.0 159.8 jit_solution(5420341848070060009)
XLA Ops:
  0.6 0.7 convert_bitcast_fusion
  1.4 1.0 maximum_bitcast_fusion
  2.4 6.3 %collective-permute-start = (bf16[392,256]{1,0:T(8,128)(2,1)S(1)}, bf16[392,256]{1,0:T(8,128)(2,1)}, u32[]{:S(2)}, u32[]{:S(2)}) collective-permute-start(bf16[392,256]{1,0:T(8,128)(2,1)S(1)} %fusion.60), channel_id=1, source_target_pairs={{0,16},{16,32},{32,48},{48,64},{64,80},{80,96},{96,112},{112,128},... | collective-permute-start | bytes 602120 | tf_op jit(solution)/shard_map/ppermute | solution.py:21
  8.7 3.5 %collective-permute-start.1 = (bf16[392,256]{1,0:T(8,128)(2,1)S(1)}, bf16[392,256]{1,0:T(8,128)(2,1)}, u32[]{:S(2)}, u32[]{:S(2)}) collective-permute-start(bf16[392,256]{1,0:T(8,128)(2,1)S(1)} %fusion.60), channel_id=1, source_target_pairs={{0,32},{16,48},{32,64},{48,80},{64,96},{80,112},{96,128},{112,144}... | collective-permute-start | bytes 602120 | tf_op jit(solution)/shard_map/ppermute | solution.py:21
  12.3 4.7 %collective-permute-start.2 = (bf16[392,256]{1,0:T(8,128)(2,1)S(1)}, bf16[392,256]{1,0:T(8,128)(2,1)}, u32[]{:S(2)}, u32[]{:S(2)}) collective-permute-start(bf16[392,256]{1,0:T(8,128)(2,1)S(1)} %fusion.60), channel_id=1, source_target_pairs={{0,48},{16,64},{32,80},{48,96},{64,112},{80,128},{96,144},{112,160... | collective-permute-start | bytes 602120 | tf_op jit(solution)/shard_map/ppermute | solution.py:21
  17.6 2.4 %fusion.57 = f32[24,1,2]{2,1,0:T(1,128)S(1)} fusion(bf16[24,2,6144]{2,1,0:T(2,128)(2,1)S(1)} %copy-done, bf16[24,6144,1]{1,0,2:T(8,128)(2,1)} %bitcast.335), kind=kOutput, calls=%fused_computation.92 | convolution fusion | flops 589824 | bytes 884928 | tf_op jit(solution)/shard_map/td,tkd->tk/dot_general | solution.py:197
  20.7 0.9 all_to_all.30
  21.7 6.8 %all-to-all-start = ((f32[16,1,3072]{2,1,0:T(1,128)}), f32[16,1,3072]{2,1,0:T(1,128)S(1)}, u32[]{:S(2)}, u32[]{:S(2)}) async-start(f32[16,1,3072]{2,1,0:T(1,128)} %all_to_all.30), calls=%async_computation | async-start | bytes 393216 | tf_op jit(solution)/shard_map/all_to_all | solution.py:41
  29.1 1.5 mul.333
  30.6 2.1 %mul.334 = f32[48,6144]{1,0:T(8,128)S(1)} reshape(f32[24,2,6144]{2,1,0:T(2,128)} %mul.333) | data formatting | bytes 2359296 | tf_op jit(solution)/shard_map/mul | solution.py:209
  33.3 2.0 %sort.17 = (s32[48]{0:T(128)}, s32[48]{0:T(128)S(1)}) sort(s32[48]{0:T(128)S(1)} %multiply_add_fusion.1, s32[48]{0:T(128)S(1)} %iota.37), dimensions={0}, to_apply=%region_17.18 | sort | flops 288 | bytes 768 | tf_op jit(solution)/shard_map/jit(argsort)/sort | solution.py:215
  35.5 0.9 gather_fusion
  36.4 1.1 reshape.482
  37.6 1.1 convolution_convert_fusion
  39.5 14.5 %all-to-all-start.1 = ((f32[32,1,96]{2,1,0:T(1,128)}), f32[32,1,96]{2,1,0:T(1,128)}, u32[]{:S(2)}, u32[]{:S(2)}) async-start(f32[32,1,96]{2,1,0:T(1,128)} %all_to_all.25), calls=%async_computation.1 | async-start | bytes 32768 | tf_op jit(solution)/shard_map/all_to_all | solution.py:41
  56.0 0.8 and_and_fusion.3
  57.3 0.9 slice_bitcast_fusion.2
  58.8 0.9 slice_bitcast_fusion
  60.2 0.9 slice_bitcast_fusion.1
  65.1 1.9 %fusion.42 = (bf16[3,384,384]{1,2,0:T(8,128)(2,1)S(1)}, bf16[3,384,384]{1,2,0:T(8,128)(2,1)S(1)}, bf16[3,384,384]{1,2,0:T(8,128)(2,1)S(1)}, bf16[3,384,384]{1,2,0:T(8,128)(2,1)S(1)}) fusion(f32[384,384,3]{1,0,2:T(8,128)S(1)} %get-tuple-element.72, f32[1,3,384,384]{2,3,1,0:T(8,128)S(1)} %get-tuple-element.67, f32[3,384]{1,0:T(4,128)S(1)} %add_divide_fusion, ...), kind=kLoop, calls=%fused_computation.73 | loop fusion | flops 8847360 | bytes 18293760 | tf_op jit(solution)/shard_map/reshape.62
  67.0 1.4 convolution_multiply_fusion
  69.2 1.1 convolution_bitcast_fusion.5
  70.3 0.8 pad_maximum_fusion.2
  71.1 1.3 collective-permute-start.5
  72.8 0.8 pad_maximum_fusion.1
  73.6 1.3 collective-permute-start.4
  74.9 1.1 fusion.30
  75.9 0.7 reduce_sum.118
  77.3 15.6 %all-to-all-start.2 = ((f32[32,1,96]{2,1,0:T(1,128)}), f32[32,1,96]{2,1,0:T(1,128)S(1)}, u32[]{:S(2)}, u32[]{:S(2)}) async-start(f32[32,1,96]{2,1,0:T(1,128)} %broadcast_in_dim.110), calls=%async_computation.2 | async-start | bytes 32768 | tf_op jit(solution)/shard_map/all_to_all | solution.py:46
  92.9 1.8 %pad_maximum_fusion = f32[384,1,256]{2,0,1:T(8,128)} fusion(f32[384,1,128]{2,0,1:T(8,128)} %convolution_bitcast_fusion.5, f32[384,1,128]{2,0,1:T(8,128)} %fusion.30), kind=kLoop, calls=%fused_computation.96 | loop fusion | flops 98304 | bytes 786432 | tf_op jit(solution)/shard_map/concatenate | solution.py:180
  94.7 1.3 collective-permute-start.3
  96.0 12.9 %all-to-all-done.2 = f32[32,1,96]{2,1,0:T(1,128)S(1)} async-done(((f32[32,1,96]{2,1,0:T(1,128)}), f32[32,1,96]{2,1,0:T(1,128)S(1)}, u32[]{:S(2)}, u32[]{:S(2)}) %all-to-all-start.2) | async-done | bytes 12320 | tf_op jit(solution)/shard_map/all_to_all | solution.py:46
  110.0 1.4 reduce.19
  112.0 1.5 broadcast_in_dim.112
  113.5 7.9 %all-to-all-start.3 = ((f32[16,1,3072]{2,1,0:T(1,128)}), f32[16,1,3072]{2,1,0:T(1,128)}, u32[]{:S(2)}, u32[]{:S(2)}) async-start(f32[16,1,3072]{2,1,0:T(1,128)} %broadcast_in_dim.112), calls=%async_computation.3 | async-start | bytes 393216 | tf_op jit(solution)/shard_map/all_to_all | solution.py:46
  121.5 2.4 %convolution_multiply_fusion.1 = f32[128,3,384]{2,0,1:T(8,128)} fusion(bf16[3,384,384]{1,2,0:T(8,128)(2,1)} %copy-done.3, bf16[384,1,256]{2,0,1:T(8,128)(2,1)} %copy-done.11), kind=kOutput, calls=%fused_computation.43 | convolution fusion | flops 113393664 | bytes 1572864 | tf_op jit(solution)/shard_map/hgqt,thd->qhgd/dot_general | solution.py:101
  123.9 4.4 %all-to-all-done.3 = f32[16,1,3072]{2,1,0:T(1,128)} async-done(((f32[16,1,3072]{2,1,0:T(1,128)}), f32[16,1,3072]{2,1,0:T(1,128)}, u32[]{:S(2)}, u32[]{:S(2)}) %all-to-all-start.3) | async-done | bytes 196640 | tf_op jit(solution)/shard_map/all_to_all | solution.py:46
  128.3 2.5 %broadcast_in_dim.114 = bf16[8,2,6,6144]{3,2,1,0:T(8,128)(2,1)} broadcast(bf16[8,6,6144]{2,1,0:T(8,128)(2,1)} %reshape.482), dimensions={0,2,3} | broadcast | bytes 1769472 | tf_op jit(solution)/shard_map/broadcast_in_dim | solution.py:217
  130.8 4.5 %all-to-all-start.4 = ((bf16[16,6,6144]{2,1,0:T(8,128)(2,1)}), bf16[16,6,6144]{2,1,0:T(8,128)(2,1)}, u32[]{:S(2)}, u32[]{:S(2)}) async-start(bf16[16,6,6144]{2,1,0:T(8,128)(2,1)} %bitcast.331), calls=%async_computation.4 | async-start | bytes 3145728 | tf_op jit(solution)/shard_map/all_to_all | solution.py:218
  135.3 1.4 fusion.20
  136.7 2.2 %fusion.24 = bf16[128,3,384]{2,0,1:T(8,128)(2,1)} fusion(f32[128,3,384]{2,0,1:T(8,128)S(1)} %copy-done.9, f32[128,3,384]{2,0,1:T(8,128)} %convolution_multiply_fusion.1, f32[128,3,384]{2,0,1:T(8,128)S(1)} %fusion.20, bf16[3,384,384]{1,2,0:T(8,128)(2,1)S(1)} %copy-done.2, bf16[384,1,256]{2,0,1:T(8,128)(2,1)} %copy-done.10), kind=kOutput, calls=%fused_computation.50 | convolution fusion | flops 113983488 | bytes 3047424 | tf_op jit(solution)/shard_map/hgqt,thd->qhgd/dot_general | solution.py:101
  139.0 1.9 %copy.206 = bf16[384,384]{1,0:T(8,128)(2,1)} copy(bf16[384,384]{0,1:T(8,128)(2,1)} %bitcast.332) | data formatting | bytes 589824
  140.8 2.2 %multiply_reduce_fusion = f32[16,3072]{1,0:T(8,128)} fusion(f32[16,1,3072]{2,1,0:T(1,128)} %all-to-all-done.3), kind=kLoop, calls=%fused_computation.112 | loop fusion | flops 49152 | bytes 393216 | tf_op jit(solution)/shard_map/div | solution.py:207
  143.0 1.7 %div.27 = f32[8,6144]{1,0:T(8,128)} reshape(f32[16,3072]{1,0:T(8,128)} %multiply_reduce_fusion) | data formatting | bytes 393216 | tf_op jit(solution)/shard_map/div | solution.py:207
  144.7 2.2 %fusion.63 = bf16[384,128]{1,0:T(8,128)(2,1)} fusion(f32[384,1,256]{2,0,1:T(8,128)} %collective-permute-done.5, f32[384,1,256]{2,0,1:T(8,128)} %collective-permute-done.4, f32[384,1,256]{2,0,1:T(8,128)} %collective-permute-done.3, bf16[3,384,384]{1,2,0:T(8,128)(2,1)S(1)} %get-tuple-element.56, bf16[384,3,128]{0,2,1:T(8,128)(2,1)S(1)} %bitcast.322), kind=kOutput, calls=%fused_computation.113 | convolution fusion | flops 113491968 | bytes 1867776 | tf_op jit(solution)/shard_map/hgqt,qhgd->thd/dot_general | solution.py:105
  146.9 2.2 %fusion.64 = bf16[384,128]{1,0:T(8,128)(2,1)} fusion(f32[384,1,256]{2,0,1:T(8,128)} %collective-permute-done.5, f32[384,1,256]{2,0,1:T(8,128)} %collective-permute-done.4, f32[384,1,256]{2,0,1:T(8,128)} %collective-permute-done.3, bf16[384,3,128]{0,2,1:T(8,128)(2,1)S(1)} %bitcast.330, f32[1,3,384,384]{2,3,1,0:T(8,128)S(1)} %get-tuple-element.69, ...), kind=kOutput, calls=%fused_computation.114 | convolution fusion | flops 114769920 | bytes 2904576 | tf_op jit(solution)/shard_map/hgqt,qhgd->thd/dot_general | solution.py:93
  149.1 7.6 %all-to-all-done.4 = bf16[16,6,6144]{2,1,0:T(8,128)(2,1)} async-done(((bf16[16,6,6144]{2,1,0:T(8,128)(2,1)}), bf16[16,6,6144]{2,1,0:T(8,128)(2,1)}, u32[]{:S(2)}, u32[]{:S(2)}) %all-to-all-start.4) | async-done | bytes 1179680 | tf_op jit(solution)/shard_map/all_to_all | solution.py:218
  156.7 3.1 %copy.207 = bf16[16,6,6144]{2,0,1:T(8,128)(2,1)} copy(bf16[16,6,6144]{2,1,0:T(8,128)(2,1)} %all-to-all-done.4) | data formatting | bytes 2359296
  (104 shorter events, 14.4 us)
Async XLA Ops:
  0.6 17.0 %copy-start = (bf16[24,2,6144]{2,1,0:T(2,128)(2,1)S(1)}, bf16[24,2,6144]{2,1,0:T(2,128)(2,1)}, u32[]{:S(2)}) copy-start(bf16[24,2,6144]{2,1,0:T(2,128)(2,1)} %param.16) | copy-start | bytes 1769476
  2.4 53.0 %collective-permute-start = (bf16[392,256]{1,0:T(8,128)(2,1)S(1)}, bf16[392,256]{1,0:T(8,128)(2,1)}, u32[]{:S(2)}, u32[]{:S(2)}) collective-permute-start(bf16[392,256]{1,0:T(8,128)(2,1)S(1)} %fusion.60), channel_id=1, source_target_pairs={{0,16},{16,32},{32,48},{48,64},{64,80},{80,96},{96,112},{112,128},... | collective-permute-start | bytes 602120 | tf_op jit(solution)/shard_map/ppermute | solution.py:21
  8.7 45.3 %collective-permute-start.1 = (bf16[392,256]{1,0:T(8,128)(2,1)S(1)}, bf16[392,256]{1,0:T(8,128)(2,1)}, u32[]{:S(2)}, u32[]{:S(2)}) collective-permute-start(bf16[392,256]{1,0:T(8,128)(2,1)S(1)} %fusion.60), channel_id=1, source_target_pairs={{0,32},{16,48},{32,64},{48,80},{64,96},{80,112},{96,128},{112,144}... | collective-permute-start | bytes 602120 | tf_op jit(solution)/shard_map/ppermute | solution.py:21
  12.3 42.5 %collective-permute-start.2 = (bf16[392,256]{1,0:T(8,128)(2,1)S(1)}, bf16[392,256]{1,0:T(8,128)(2,1)}, u32[]{:S(2)}, u32[]{:S(2)}) collective-permute-start(bf16[392,256]{1,0:T(8,128)(2,1)S(1)} %fusion.60), channel_id=1, source_target_pairs={{0,48},{16,64},{32,80},{48,96},{64,112},{80,128},{96,144},{112,160... | collective-permute-start | bytes 602120 | tf_op jit(solution)/shard_map/ppermute | solution.py:21
  17.6 2.6 %copy-start.12 = (bf16[24,6144]{1,0:T(8,128)(2,1)S(1)}, bf16[24,6144]{1,0:T(8,128)(2,1)}, u32[]{:S(2)}) copy-start(bf16[24,6144]{1,0:T(8,128)(2,1)} %param.17) | copy-start | bytes 884740
  17.6 2.6 %copy-start.14 = (bf16[8,6144]{1,0:T(8,128)(2,1)S(1)}, bf16[8,6144]{1,0:T(8,128)(2,1)}, u32[]{:S(2)}) copy-start(bf16[8,6144]{1,0:T(8,128)(2,1)} %param.18) | copy-start | bytes 294916
  17.6 2.7 %copy-start.23 = (s32[24,2]{0,1:T(2,128)S(1)}, s32[24,2]{0,1:T(2,128)}, u32[]{:S(2)}) copy-start(s32[24,2]{0,1:T(2,128)} %param.19) | copy-start | bytes 580
  20.1 8.5 %copy-start.16 = (bf16[384,384]{1,0:T(8,128)(2,1)S(1)}, bf16[384,384]{1,0:T(8,128)(2,1)}, u32[]{:S(2)}) copy-start(bf16[384,384]{1,0:T(8,128)(2,1)} %param.10) | copy-start | bytes 884740
  20.1 8.7 %copy-start.17 = (bf16[384,384]{1,0:T(8,128)(2,1)S(1)}, bf16[384,384]{1,0:T(8,128)(2,1)}, u32[]{:S(2)}) copy-start(bf16[384,384]{1,0:T(8,128)(2,1)} %param.13) | copy-start | bytes 884740
  20.1 9.0 %copy-start.18 = (bf16[24,6144]{1,0:T(8,128)(2,1)S(1)}, bf16[24,6144]{1,0:T(8,128)(2,1)}, u32[]{:S(2)}) copy-start(bf16[24,6144]{1,0:T(8,128)(2,1)} %param.15) | copy-start | bytes 884740
  21.7 17.0 %all-to-all-start = ((f32[16,1,3072]{2,1,0:T(1,128)}), f32[16,1,3072]{2,1,0:T(1,128)S(1)}, u32[]{:S(2)}, u32[]{:S(2)}) async-start(f32[16,1,3072]{2,1,0:T(1,128)} %all_to_all.30), calls=%async_computation | async-start | bytes 393216 | tf_op jit(solution)/shard_map/all_to_all | solution.py:41
  29.0 35.5 %copy-start.4 = (bf16[384,384]{0,1:T(8,128)(2,1)}, bf16[384,384]{0,1:T(8,128)(2,1)S(1)}, u32[]{:S(2)}) copy-start(bf16[384,384]{0,1:T(8,128)(2,1)S(1)} %copy.175) | copy-start | bytes 884740
  36.4 19.6 %copy-start.22 = (s32[384]{0:T(512)S(1)}, s32[384]{0:T(512)}, u32[]{:S(2)}) copy-start(s32[384]{0:T(512)} %param.14) | copy-start | bytes 4612
  36.4 20.4 %copy-start.13 = (bf16[384,128]{1,0:T(8,128)(2,1)S(1)}, bf16[384,128]{1,0:T(8,128)(2,1)}, u32[]{:S(2)}) copy-start(bf16[384,128]{1,0:T(8,128)(2,1)} %param.11) | copy-start | bytes 294916
  39.5 36.4 %all-to-all-start.1 = ((f32[32,1,96]{2,1,0:T(1,128)}), f32[32,1,96]{2,1,0:T(1,128)}, u32[]{:S(2)}, u32[]{:S(2)}) async-start(f32[32,1,96]{2,1,0:T(1,128)} %all_to_all.25), calls=%async_computation.1 | async-start | bytes 32768 | tf_op jit(solution)/shard_map/all_to_all | solution.py:41
  56.9 8.2 %copy-start.7 = (pred[384,384]{0,1:T(8,128)(4,1)}, pred[384,384]{0,1:T(8,128)(4,1)S(1)}, u32[]{:S(2)}) copy-start(pred[384,384]{0,1:T(8,128)(4,1)S(1)} %get-tuple-element.58) | copy-start | bytes 442372
  58.3 3.3 %copy-start.10 = (bf16[384,1,256]{2,0,1:T(8,128)(2,1)}, bf16[384,1,256]{2,0,1:T(8,128)(2,1)S(1)}, u32[]{:S(2)}) copy-start(bf16[384,1,256]{2,0,1:T(8,128)(2,1)S(1)} %slice_bitcast_fusion.2) | copy-start | bytes 589828
  61.1 1.8 %copy-start.11 = (bf16[384,1,256]{2,0,1:T(8,128)(2,1)}, bf16[384,1,256]{2,0,1:T(8,128)(2,1)S(1)}, u32[]{:S(2)}) copy-start(bf16[384,1,256]{2,0,1:T(8,128)(2,1)S(1)} %slice_bitcast_fusion.1) | copy-start | bytes 589828
  63.0 0.9 copy-start.15
  64.6 4.7 %copy-start.20 = (f32[3,384]{1,0:T(4,128)}, f32[3,384]{1,0:T(4,128)S(1)}, u32[]{:S(2)}) copy-start(f32[3,384]{1,0:T(4,128)S(1)} %get-tuple-element.48) | copy-start | bytes 13828
  67.0 5.4 %copy-start.3 = (bf16[3,384,384]{1,2,0:T(8,128)(2,1)}, bf16[3,384,384]{1,2,0:T(8,128)(2,1)S(1)}, u32[]{:S(2)}) copy-start(bf16[3,384,384]{1,2,0:T(8,128)(2,1)S(1)} %get-tuple-element.54) | copy-start | bytes 2654212
  67.0 7.9 %copy-start.1 = (bf16[3,384,384]{1,2,0:T(8,128)(2,1)}, bf16[3,384,384]{1,2,0:T(8,128)(2,1)S(1)}, u32[]{:S(2)}) copy-start(bf16[3,384,384]{1,2,0:T(8,128)(2,1)S(1)} %get-tuple-element.53) | copy-start | bytes 2654212
  67.0 1.8 %copy-start.5 = (bf16[384,384]{0,1:T(8,128)(2,1)S(1)}, bf16[384,384]{0,1:T(8,128)(2,1)}, u32[]{:S(2)}) copy-start(bf16[384,384]{0,1:T(8,128)(2,1)} %copy-done.4) | copy-start | bytes 884740
  71.1 73.6 %collective-permute-start.5 = (f32[384,1,256]{2,0,1:T(8,128)}, f32[384,1,256]{2,0,1:T(8,128)}, u32[]{:S(2)}, u32[]{:S(2)}) collective-permute-start(f32[384,1,256]{2,0,1:T(8,128)} %pad_maximum_fusion.2), channel_id=1, source_target_pairs={{48,0},{64,16},{80,32},{96,48},{112,64},{128,80},{144,96},{160,112... | collective-permute-start | bytes 1179656 | tf_op jit(solution)/shard_map/ppermute | solution.py:21
  73.6 71.1 %collective-permute-start.4 = (f32[384,1,256]{2,0,1:T(8,128)}, f32[384,1,256]{2,0,1:T(8,128)}, u32[]{:S(2)}, u32[]{:S(2)}) collective-permute-start(f32[384,1,256]{2,0,1:T(8,128)} %pad_maximum_fusion.1), channel_id=1, source_target_pairs={{32,0},{48,16},{64,32},{80,48},{96,64},{112,80},{128,96},{144,112}... | collective-permute-start | bytes 1179656 | tf_op jit(solution)/shard_map/ppermute | solution.py:21
  77.3 31.5 %all-to-all-start.2 = ((f32[32,1,96]{2,1,0:T(1,128)}), f32[32,1,96]{2,1,0:T(1,128)S(1)}, u32[]{:S(2)}, u32[]{:S(2)}) async-start(f32[32,1,96]{2,1,0:T(1,128)} %broadcast_in_dim.110), calls=%async_computation.2 | async-start | bytes 32768 | tf_op jit(solution)/shard_map/all_to_all | solution.py:46
  94.7 50.0 %collective-permute-start.3 = (f32[384,1,256]{2,0,1:T(8,128)}, f32[384,1,256]{2,0,1:T(8,128)}, u32[]{:S(2)}, u32[]{:S(2)}) collective-permute-start(f32[384,1,256]{2,0,1:T(8,128)} %pad_maximum_fusion), channel_id=1, source_target_pairs={{16,0},{32,16},{48,32},{64,48},{80,64},{96,80},{112,96},{128,112},... | collective-permute-start | bytes 1179656 | tf_op jit(solution)/shard_map/ppermute | solution.py:21
  108.8 0.6 copy-start.19
  113.5 14.8 %all-to-all-start.3 = ((f32[16,1,3072]{2,1,0:T(1,128)}), f32[16,1,3072]{2,1,0:T(1,128)}, u32[]{:S(2)}, u32[]{:S(2)}) async-start(f32[16,1,3072]{2,1,0:T(1,128)} %broadcast_in_dim.112), calls=%async_computation.3 | async-start | bytes 393216 | tf_op jit(solution)/shard_map/all_to_all | solution.py:46
  130.8 25.9 %all-to-all-start.4 = ((bf16[16,6,6144]{2,1,0:T(8,128)(2,1)}), bf16[16,6,6144]{2,1,0:T(8,128)(2,1)}, u32[]{:S(2)}, u32[]{:S(2)}) async-start(bf16[16,6,6144]{2,1,0:T(8,128)(2,1)} %bitcast.331), calls=%async_computation.4 | async-start | bytes 3145728 | tf_op jit(solution)/shard_map/all_to_all | solution.py:218
  135.3 1.4 copy-start.2
  135.3 1.4 copy-start.9
  139.0 7.9 %copy-start.21 = (f32[3,384]{1,0:T(4,128)S(1)}, f32[3,384]{1,0:T(4,128)}, u32[]{:S(2)}) copy-start(f32[3,384]{1,0:T(4,128)} %copy-done.20) | copy-start | bytes 13828
  144.7 2.2 %copy-start.6 = (bf16[384,384]{0,1:T(8,128)(2,1)S(1)}, bf16[384,384]{0,1:T(8,128)(2,1)}, u32[]{:S(2)}) copy-start(bf16[384,384]{0,1:T(8,128)(2,1)} %copy-done.4) | copy-start | bytes 884740
  144.7 2.2 %copy-start.8 = (pred[384,384]{0,1:T(8,128)(4,1)S(1)}, pred[384,384]{0,1:T(8,128)(4,1)}, u32[]{:S(2)}) copy-start(pred[384,384]{0,1:T(8,128)(4,1)} %copy-done.7) | copy-start | bytes 442372

commit v3 on v2

--- a/solution.py
+++ b/solution.py
@@ -46,9 +46,14 @@
     return lax.all_to_all(copies, axis, 0, 0, tiled=True).reshape(-1)
 
 
+def broadcast_sum(flat, axis):
+    copies = jnp.broadcast_to(flat[None], (lax.axis_size(axis),) + flat.shape)
+    return lax.all_to_all(copies, axis, 0, 0, tiled=True).sum(axis=0)
+
+
 def sum_everywhere(value):
-    flat = scatter_sum(scatter_sum(value.reshape(-1), "ep"), "seq")
-    return gather_back(gather_back(flat, "seq"), "ep").reshape(value.shape)
+    flat = broadcast_sum(scatter_sum(value.reshape(-1), "ep"), "seq")
+    return gather_back(flat, "ep").reshape(value.shape)
 
 
 def allowed_pairs(seg_rows, seg_keys, seq_index, offset, tok_rows):
@@ -215,6 +220,7 @@
     order = jnp.argsort(flat_routes * capacity + ranks)
     outgoing = expert_rows.reshape(-1, expert_rows.shape[2])[order]
     outgoing = jnp.repeat(outgoing.reshape(EXPERTS, capacity, -1), copies, axis=0)
+    router_grad, outgoing = lax.optimization_barrier((router_grad, outgoing))
     routed_grads = lax.all_to_all(outgoing, "ep", split_axis=0, concat_axis=0, tiled=True)
     return (query_grad, key_grad, value_grad, normed_grad, router_grad, routed_grads)
 

time: 163 us -> 146 us (0.90); the launches traced: 160 us -> 145 us
  starting transfers between devices: 67.8 us -> 51.6 us
  waiting for transfers between devices: 24.9 us -> 28 us
  local copies, waits for them, and re-layouts: 24.2 us -> 21.4 us
    ppermute x6, waiting for transfers between devices: 0.02 us -> 20.9 us  [from_behind(): return lax.ppermute(value, axis, pairs)]
    all_to_all x2 -> x1, starting transfers between devices: 23.5 us -> 6.64 us  [gather_back(): return lax.all_to_all(copies, axis, 0, 0, tiled=True).reshape(-1)]
    all_to_all x2 -> x1, waiting for transfers between devices: 17.3 us -> 2.59 us  [gather_back(): return lax.all_to_all(copies, axis, 0, 0, tiled=True).reshape(-1)]
    all_to_all x2 -> x1, starting transfers between devices: 21.3 us -> 6.84 us  [scatter_sum(): return lax.all_to_all(parts, axis, 0, 0, tiled=True).sum(axis=0)]
    all_to_all x0 -> x1, starting transfers between devices: none -> 14.3 us  [broadcast_sum(): return lax.all_to_all(copies, axis, 0, 0, tiled=True).sum(axis=0)]
    all_to_all x1, waiting for transfers between devices: 7.61 us -> 0.01 us  [on_device(): lax.all_to_all(outgoing, 'ep', split_axis=0, concat_axis=0, tiled=True)]
    all_to_all x0 -> x1, waiting for transfers between devices: none -> 4.47 us  [broadcast_sum(): return lax.all_to_all(copies, axis, 0, 0, tiled=True).sum(axis=0)]
    dot_general x4, matrix products: 7.37 us -> 4.7 us  [block_grads(): jnp.einsum('hgqt,thd->qhgd', score_low, key_block, preferred_element_type...]
  transfers between devices with their start and end apart: 11 -> 10, of which waited for: 3 -> 3; matrix products, arithmetic and copies ran while one was open for 37% -> 40% of each run, Pallas kernels for 0% -> 0%
where the time goes in v3:
time: 146 us; the launch traced here: 145 us
  starting transfers between devices  51.6 us (35%)
  waiting for transfers between devices  28 us (19%)
  matrix products  24 us (16%)
  local copies, waits for them, and re-layouts  21.4 us (15%)
  other arithmetic  18.6 us (13%)
    ppermute x6, waiting for transfers between devices, from_behind(): return lax.ppermute(value, axis, pairs)  20.9 us
    ppermute x6, starting transfers between devices, from_behind(): return lax.ppermute(value, axis, pairs)  18.6 us
    all_to_all x1, starting transfers between devices, broadcast_sum(): return lax.all_to_all(copies, axis, 0, 0, tiled=True).sum(axis=0)  14.3 us
    all_to_all x1, starting transfers between devices, scatter_sum(): return lax.all_to_all(parts, axis, 0, 0, tiled=True).sum(axis=0)  6.84 us
    all_to_all x1, starting transfers between devices, gather_back(): return lax.all_to_all(copies, axis, 0, 0, tiled=True).reshape(-1)  6.64 us
    dot_general x4, matrix products, block_grads(): jnp.einsum('hgqt,qhgd->thd', score_low, query_rows, preferred_element_typ...  5.89 us
    unnamed x49, local copies, waits for them, and re-layouts  5.77 us
    all_to_all x1, starting transfers between devices, on_device(): lax.all_to_all(outgoing, 'ep', split_axis=0, concat_axis=0, tiled=True)  5.26 us
  transfers between devices with their start and end apart: 10, of which 3 were waited for; matrix products, arithmetic and copies ran while one was open for 40% of the time, Pallas kernels for 0%

profile of v3, /device:TPU:1, one launch (start us, length us, event | category | flops | bytes accessed | tf_op | source)
XLA Modules:
  0.0 144.6 jit_solution(3277266557209873166)
XLA Ops:
  1.4 1.0 maximum_bitcast_fusion
  2.4 6.3 %collective-permute-start = (bf16[392,256]{1,0:T(8,128)(2,1)S(1)}, bf16[392,256]{1,0:T(8,128)(2,1)}, u32[]{:S(2)}, u32[]{:S(2)}) collective-permute-start(bf16[392,256]{1,0:T(8,128)(2,1)S(1)} %fusion.60), channel_id=1, source_target_pairs={{0,16},{16,32},{32,48},{48,64},{64,80},{80,96},{96,112},{112,128},... | collective-permute-start | bytes 602120 | tf_op jit(solution)/shard_map/ppermute | solution.py:21
  8.7 3.5 %collective-permute-start.1 = (bf16[392,256]{1,0:T(8,128)(2,1)S(1)}, bf16[392,256]{1,0:T(8,128)(2,1)}, u32[]{:S(2)}, u32[]{:S(2)}) collective-permute-start(bf16[392,256]{1,0:T(8,128)(2,1)S(1)} %fusion.60), channel_id=1, source_target_pairs={{0,32},{16,48},{32,64},{48,80},{64,96},{80,112},{96,128},{112,144}... | collective-permute-start | bytes 602120 | tf_op jit(solution)/shard_map/ppermute | solution.py:21
  12.3 4.7 %collective-permute-start.2 = (bf16[392,256]{1,0:T(8,128)(2,1)S(1)}, bf16[392,256]{1,0:T(8,128)(2,1)}, u32[]{:S(2)}, u32[]{:S(2)}) collective-permute-start(bf16[392,256]{1,0:T(8,128)(2,1)S(1)} %fusion.60), channel_id=1, source_target_pairs={{0,48},{16,64},{32,80},{48,96},{64,112},{80,128},{96,144},{112,160... | collective-permute-start | bytes 602120 | tf_op jit(solution)/shard_map/ppermute | solution.py:21
  17.6 2.4 %fusion.57 = f32[24,1,2]{2,1,0:T(1,128)S(1)} fusion(bf16[24,2,6144]{2,1,0:T(2,128)(2,1)S(1)} %copy-done, bf16[24,6144,1]{1,0,2:T(8,128)(2,1)} %bitcast.334), kind=kOutput, calls=%fused_computation.92 | convolution fusion | flops 589824 | bytes 884928 | tf_op jit(solution)/shard_map/td,tkd->tk/dot_general | solution.py:202
  20.7 0.9 all_to_all.22
  21.7 6.8 %all-to-all-start = ((f32[16,1,3072]{2,1,0:T(1,128)}), f32[16,1,3072]{2,1,0:T(1,128)S(1)}, u32[]{:S(2)}, u32[]{:S(2)}) async-start(f32[16,1,3072]{2,1,0:T(1,128)} %all_to_all.22), calls=%async_computation | async-start | bytes 393216 | tf_op jit(solution)/shard_map/all_to_all | solution.py:41
  29.1 1.5 %mul.333 = f32[24,2,6144]{2,1,0:T(2,128)} broadcast(bf16[24,6144]{1,0:T(8,128)(2,1)S(1)} %copy-done.17), dimensions={0,2} | broadcast | bytes 1474560 | tf_op jit(solution)/shard_map/mul | solution.py:214
  30.6 2.1 %mul.334 = f32[48,6144]{1,0:T(8,128)S(1)} reshape(f32[24,2,6144]{2,1,0:T(2,128)} %mul.333) | data formatting | bytes 2359296 | tf_op jit(solution)/shard_map/mul | solution.py:214
  33.3 2.0 %sort.17 = (s32[48]{0:T(128)}, s32[48]{0:T(128)S(1)}) sort(s32[48]{0:T(128)S(1)} %multiply_add_fusion.1, s32[48]{0:T(128)S(1)} %iota.37), dimensions={0}, to_apply=%region_17.18 | sort | flops 288 | bytes 768 | tf_op jit(solution)/shard_map/jit(argsort)/sort | solution.py:220
  35.5 0.9 gather_fusion
  36.4 1.1 reshape.475
  37.6 1.2 convolution_convert_fusion
  38.8 1.0 broadcast_in_dim.109
  39.8 14.3 %all-to-all-start.1 = ((f32[32,1,3072]{2,1,0:T(1,128)}), f32[32,1,3072]{2,1,0:T(1,128)}, u32[]{:S(2)}, u32[]{:S(2)}) async-start(f32[32,1,3072]{2,1,0:T(1,128)} %broadcast_in_dim.109), calls=%async_computation.1 | async-start | bytes 786432 | tf_op jit(solution)/shard_map/all_to_all | solution.py:51
  56.1 0.8 and_and_fusion.3
  57.4 0.9 slice_bitcast_fusion.2
  58.8 0.9 slice_bitcast_fusion
  60.2 0.9 slice_bitcast_fusion.1
  65.1 2.7 %fusion.42 = (bf16[3,384,384]{1,2,0:T(8,128)(2,1)}, bf16[3,384,384]{1,2,0:T(8,128)(2,1)S(1)}, bf16[3,384,384]{1,2,0:T(8,128)(2,1)S(1)}, bf16[3,384,384]{1,2,0:T(8,128)(2,1)S(1)}) fusion(f32[384,384,3]{1,0,2:T(8,128)S(1)} %get-tuple-element.76, f32[1,3,384,384]{2,3,1,0:T(8,128)S(1)} %get-tuple-element.71, f32[3,384]{1,0:T(4,128)S(1)} %add_divide_fusion, ...), kind=kLoop, calls=%fused_computation.73 | loop fusion | flops 8847360 | bytes 18293760 | tf_op jit(solution)/shard_map/reshape.61
  68.2 0.8 pad_maximum_fusion.2
  69.0 1.5 %collective-permute-start.5 = (f32[384,1,256]{2,0,1:T(8,128)}, f32[384,1,256]{2,0,1:T(8,128)}, u32[]{:S(2)}, u32[]{:S(2)}) collective-permute-start(f32[384,1,256]{2,0,1:T(8,128)} %pad_maximum_fusion.2), channel_id=1, source_target_pairs={{48,0},{64,16},{80,32},{96,48},{112,64},{128,80},{144,96},{160,112... | collective-permute-start | bytes 1179656 | tf_op jit(solution)/shard_map/ppermute | solution.py:21
  70.4 1.1 fusion.31
  71.5 1.2 convolution_multiply_fusion
  72.7 1.2 convolution_multiply_fusion.1
  73.9 1.1 convolution_bitcast_fusion.3
  75.0 1.1 convolution_bitcast_fusion.5
  76.1 4.5 %all-to-all-done.1 = f32[32,1,3072]{2,1,0:T(1,128)} async-done(((f32[32,1,3072]{2,1,0:T(1,128)}), f32[32,1,3072]{2,1,0:T(1,128)}, u32[]{:S(2)}, u32[]{:S(2)}) %all-to-all-start.1) | async-done | bytes 393248 | tf_op jit(solution)/shard_map/all_to_all | solution.py:51
  80.6 1.2 reduce_sum.118
  81.8 0.8 broadcast_in_dim.110
  82.6 6.6 %all-to-all-start.2 = ((f32[16,1,3072]{2,1,0:T(1,128)}), f32[16,1,3072]{2,1,0:T(1,128)}, u32[]{:S(2)}, u32[]{:S(2)}) async-start(f32[16,1,3072]{2,1,0:T(1,128)} %broadcast_in_dim.110), calls=%async_computation.2 | async-start | bytes 393216 | tf_op jit(solution)/shard_map/all_to_all | solution.py:46
  89.2 1.8 %pad_maximum_fusion.1 = f32[384,1,256]{2,0,1:T(8,128)} fusion(f32[384,1,128]{2,0,1:T(8,128)} %convolution_bitcast_fusion.3, f32[384,1,128]{2,0,1:T(8,128)} %fusion.31), kind=kLoop, calls=%fused_computation.97 | loop fusion | flops 98304 | bytes 786432 | tf_op jit(solution)/shard_map/concatenate | solution.py:185
  91.0 1.3 collective-permute-start.4
  92.3 2.2 %fusion.30 = f32[384,1,128]{2,0,1:T(8,128)} fusion(bf16[3,384,384]{1,2,0:T(8,128)(2,1)} %get-tuple-element.57, bf16[384,3,128]{0,2,1:T(8,128)(2,1)S(1)} %bitcast.320), kind=kOutput, calls=%fused_computation.65 | convolution fusion | flops 113295360 | bytes 1376256 | tf_op jit(solution)/shard_map/hgqt,qhgd->thd/dot_general | solution.py:110
  94.6 2.6 %all-to-all-done.2 = f32[16,1,3072]{2,1,0:T(1,128)} async-done(((f32[16,1,3072]{2,1,0:T(1,128)}), f32[16,1,3072]{2,1,0:T(1,128)}, u32[]{:S(2)}, u32[]{:S(2)}) %all-to-all-start.2) | async-done | bytes 196640 | tf_op jit(solution)/shard_map/all_to_all | solution.py:46
  97.2 2.2 %multiply_reduce_fusion = f32[16,3072]{1,0:T(8,128)} fusion(f32[16,1,3072]{2,1,0:T(1,128)} %all-to-all-done.2), kind=kLoop, calls=%fused_computation.112 | loop fusion | flops 49152 | bytes 393216 | tf_op jit(solution)/shard_map/div | solution.py:212
  99.3 1.7 %div.27 = f32[8,6144]{1,0:T(8,128)} reshape(f32[16,3072]{1,0:T(8,128)} %multiply_reduce_fusion) | data formatting | bytes 393216 | tf_op jit(solution)/shard_map/div | solution.py:212
  101.0 2.5 %broadcast_in_dim.112 = bf16[8,2,6,6144]{3,2,1,0:T(8,128)(2,1)} broadcast(bf16[8,6,6144]{2,1,0:T(8,128)(2,1)} %reshape.475), dimensions={0,2,3} | broadcast | bytes 1769472 | tf_op jit(solution)/shard_map/broadcast_in_dim | solution.py:222
  103.5 5.3 %all-to-all-start.3 = ((bf16[16,6,6144]{2,1,0:T(8,128)(2,1)}), bf16[16,6,6144]{2,1,0:T(8,128)(2,1)}, u32[]{:S(2)}, u32[]{:S(2)}) async-start(bf16[16,6,6144]{2,1,0:T(8,128)(2,1)} %bitcast.330), calls=%async_computation.3 | async-start | bytes 3145728 | tf_op jit(solution)/shard_map/all_to_all | solution.py:224
  108.8 2.0 %pad_maximum_fusion = f32[384,1,256]{2,0,1:T(8,128)} fusion(f32[384,1,128]{2,0,1:T(8,128)} %convolution_bitcast_fusion.5, f32[384,1,128]{2,0,1:T(8,128)} %fusion.30), kind=kLoop, calls=%fused_computation.96 | loop fusion | flops 98304 | bytes 786432 | tf_op jit(solution)/shard_map/concatenate | solution.py:185
  110.7 1.3 collective-permute-start.3
  112.0 1.3 fusion.20
  113.3 1.1 fusion.24
  114.4 1.9 %copy.206 = bf16[384,384]{1,0:T(8,128)(2,1)} copy(bf16[384,384]{0,1:T(8,128)(2,1)} %bitcast.331) | data formatting | bytes 589824
  116.3 20.9 %collective-permute-done.3 = f32[384,1,256]{2,0,1:T(8,128)} collective-permute-done((f32[384,1,256]{2,0,1:T(8,128)}, f32[384,1,256]{2,0,1:T(8,128)}, u32[]{:S(2)}, u32[]{:S(2)}) %collective-permute-start.3) | collective-permute-done | bytes 393248 | tf_op jit(solution)/shard_map/ppermute | solution.py:21
  137.2 2.2 %fusion.63 = bf16[384,128]{1,0:T(8,128)(2,1)} fusion(f32[384,1,256]{2,0,1:T(8,128)} %collective-permute-done.5, f32[384,1,256]{2,0,1:T(8,128)} %collective-permute-done.4, f32[384,1,256]{2,0,1:T(8,128)} %collective-permute-done.3, bf16[3,384,384]{1,2,0:T(8,128)(2,1)S(1)} %get-tuple-element.60, bf16[384,3,128]{0,2,1:T(8,128)(2,1)S(1)} %bitcast.321), kind=kOutput, calls=%fused_computation.113 | convolution fusion | flops 113491968 | bytes 1867776 | tf_op jit(solution)/shard_map/hgqt,qhgd->thd/dot_general | solution.py:110
  139.4 2.2 %fusion.64 = bf16[384,128]{1,0:T(8,128)(2,1)} fusion(f32[384,1,256]{2,0,1:T(8,128)} %collective-permute-done.5, f32[384,1,256]{2,0,1:T(8,128)} %collective-permute-done.4, f32[384,1,256]{2,0,1:T(8,128)} %collective-permute-done.3, bf16[384,3,128]{0,2,1:T(8,128)(2,1)S(1)} %bitcast.329, f32[1,3,384,384]{2,3,1,0:T(8,128)S(1)} %get-tuple-element.73, ...), kind=kOutput, calls=%fused_computation.114 | convolution fusion | flops 114769920 | bytes 2904576 | tf_op jit(solution)/shard_map/hgqt,qhgd->thd/dot_general | solution.py:98
  141.6 3.1 %copy.207 = bf16[16,6,6144]{2,0,1:T(8,128)(2,1)} copy(bf16[16,6,6144]{2,1,0:T(8,128)(2,1)} %all-to-all-done.3) | data formatting | bytes 2359296
  (94 shorter events, 11.2 us)
Async XLA Ops:
  0.6 17.0 %copy-start = (bf16[24,2,6144]{2,1,0:T(2,128)(2,1)S(1)}, bf16[24,2,6144]{2,1,0:T(2,128)(2,1)}, u32[]{:S(2)}) copy-start(bf16[24,2,6144]{2,1,0:T(2,128)(2,1)} %param.16) | copy-start | bytes 1769476
  2.4 53.1 %collective-permute-start = (bf16[392,256]{1,0:T(8,128)(2,1)S(1)}, bf16[392,256]{1,0:T(8,128)(2,1)}, u32[]{:S(2)}, u32[]{:S(2)}) collective-permute-start(bf16[392,256]{1,0:T(8,128)(2,1)S(1)} %fusion.60), channel_id=1, source_target_pairs={{0,16},{16,32},{32,48},{48,64},{64,80},{80,96},{96,112},{112,128},... | collective-permute-start | bytes 602120 | tf_op jit(solution)/shard_map/ppermute | solution.py:21
  8.7 45.4 %collective-permute-start.1 = (bf16[392,256]{1,0:T(8,128)(2,1)S(1)}, bf16[392,256]{1,0:T(8,128)(2,1)}, u32[]{:S(2)}, u32[]{:S(2)}) collective-permute-start(bf16[392,256]{1,0:T(8,128)(2,1)S(1)} %fusion.60), channel_id=1, source_target_pairs={{0,32},{16,48},{32,64},{48,80},{64,96},{80,112},{96,128},{112,144}... | collective-permute-start | bytes 602120 | tf_op jit(solution)/shard_map/ppermute | solution.py:21
  12.3 42.5 %collective-permute-start.2 = (bf16[392,256]{1,0:T(8,128)(2,1)S(1)}, bf16[392,256]{1,0:T(8,128)(2,1)}, u32[]{:S(2)}, u32[]{:S(2)}) collective-permute-start(bf16[392,256]{1,0:T(8,128)(2,1)S(1)} %fusion.60), channel_id=1, source_target_pairs={{0,48},{16,64},{32,80},{48,96},{64,112},{80,128},{96,144},{112,160... | collective-permute-start | bytes 602120 | tf_op jit(solution)/shard_map/ppermute | solution.py:21
  17.6 2.6 %copy-start.11 = (bf16[24,6144]{1,0:T(8,128)(2,1)S(1)}, bf16[24,6144]{1,0:T(8,128)(2,1)}, u32[]{:S(2)}) copy-start(bf16[24,6144]{1,0:T(8,128)(2,1)} %param.17) | copy-start | bytes 884740
  17.6 2.6 %copy-start.13 = (bf16[8,6144]{1,0:T(8,128)(2,1)S(1)}, bf16[8,6144]{1,0:T(8,128)(2,1)}, u32[]{:S(2)}) copy-start(bf16[8,6144]{1,0:T(8,128)(2,1)} %param.18) | copy-start | bytes 294916
  17.6 2.7 %copy-start.21 = (s32[24,2]{0,1:T(2,128)S(1)}, s32[24,2]{0,1:T(2,128)}, u32[]{:S(2)}) copy-start(s32[24,2]{0,1:T(2,128)} %param.19) | copy-start | bytes 580
  20.1 8.5 %copy-start.15 = (bf16[384,384]{1,0:T(8,128)(2,1)S(1)}, bf16[384,384]{1,0:T(8,128)(2,1)}, u32[]{:S(2)}) copy-start(bf16[384,384]{1,0:T(8,128)(2,1)} %param.10) | copy-start | bytes 884740
  20.1 8.7 %copy-start.16 = (bf16[384,384]{1,0:T(8,128)(2,1)S(1)}, bf16[384,384]{1,0:T(8,128)(2,1)}, u32[]{:S(2)}) copy-start(bf16[384,384]{1,0:T(8,128)(2,1)} %param.13) | copy-start | bytes 884740
  20.1 9.0 %copy-start.17 = (bf16[24,6144]{1,0:T(8,128)(2,1)S(1)}, bf16[24,6144]{1,0:T(8,128)(2,1)}, u32[]{:S(2)}) copy-start(bf16[24,6144]{1,0:T(8,128)(2,1)} %param.15) | copy-start | bytes 884740
  21.7 17.0 %all-to-all-start = ((f32[16,1,3072]{2,1,0:T(1,128)}), f32[16,1,3072]{2,1,0:T(1,128)S(1)}, u32[]{:S(2)}, u32[]{:S(2)}) async-start(f32[16,1,3072]{2,1,0:T(1,128)} %all_to_all.22), calls=%async_computation | async-start | bytes 393216 | tf_op jit(solution)/shard_map/all_to_all | solution.py:41
  29.0 35.6 %copy-start.2 = (bf16[384,384]{0,1:T(8,128)(2,1)}, bf16[384,384]{0,1:T(8,128)(2,1)S(1)}, u32[]{:S(2)}) copy-start(bf16[384,384]{0,1:T(8,128)(2,1)S(1)} %copy.175) | copy-start | bytes 884740
  36.4 19.7 %copy-start.20 = (s32[384]{0:T(512)S(1)}, s32[384]{0:T(512)}, u32[]{:S(2)}) copy-start(s32[384]{0:T(512)} %param.14) | copy-start | bytes 4612
  36.4 20.5 %copy-start.12 = (bf16[384,128]{1,0:T(8,128)(2,1)S(1)}, bf16[384,128]{1,0:T(8,128)(2,1)}, u32[]{:S(2)}) copy-start(bf16[384,128]{1,0:T(8,128)(2,1)} %param.11) | copy-start | bytes 294916
  39.8 40.8 %all-to-all-start.1 = ((f32[32,1,3072]{2,1,0:T(1,128)}), f32[32,1,3072]{2,1,0:T(1,128)}, u32[]{:S(2)}, u32[]{:S(2)}) async-start(f32[32,1,3072]{2,1,0:T(1,128)} %broadcast_in_dim.109), calls=%async_computation.1 | async-start | bytes 786432 | tf_op jit(solution)/shard_map/all_to_all | solution.py:51
  56.9 8.2 %copy-start.5 = (pred[384,384]{0,1:T(8,128)(4,1)}, pred[384,384]{0,1:T(8,128)(4,1)S(1)}, u32[]{:S(2)}) copy-start(pred[384,384]{0,1:T(8,128)(4,1)S(1)} %get-tuple-element.62) | copy-start | bytes 442372
  58.4 3.3 %copy-start.9 = (bf16[384,1,256]{2,0,1:T(8,128)(2,1)}, bf16[384,1,256]{2,0,1:T(8,128)(2,1)S(1)}, u32[]{:S(2)}) copy-start(bf16[384,1,256]{2,0,1:T(8,128)(2,1)S(1)} %slice_bitcast_fusion.2) | copy-start | bytes 589828
  63.0 0.9 copy-start.14
  64.6 10.4 %copy-start.18 = (f32[3,384]{1,0:T(4,128)}, f32[3,384]{1,0:T(4,128)S(1)}, u32[]{:S(2)}) copy-start(f32[3,384]{1,0:T(4,128)S(1)} %get-tuple-element.52) | copy-start | bytes 13828
  69.0 47.3 %collective-permute-start.5 = (f32[384,1,256]{2,0,1:T(8,128)}, f32[384,1,256]{2,0,1:T(8,128)}, u32[]{:S(2)}, u32[]{:S(2)}) collective-permute-start(f32[384,1,256]{2,0,1:T(8,128)} %pad_maximum_fusion.2), channel_id=1, source_target_pairs={{48,0},{64,16},{80,32},{96,48},{112,64},{128,80},{144,96},{160,112... | collective-permute-start | bytes 1179656 | tf_op jit(solution)/shard_map/ppermute | solution.py:21
  71.5 2.3 %copy-start.3 = (bf16[384,384]{0,1:T(8,128)(2,1)S(1)}, bf16[384,384]{0,1:T(8,128)(2,1)}, u32[]{:S(2)}) copy-start(bf16[384,384]{0,1:T(8,128)(2,1)} %copy-done.2) | copy-start | bytes 884740
  82.6 14.6 %all-to-all-start.2 = ((f32[16,1,3072]{2,1,0:T(1,128)}), f32[16,1,3072]{2,1,0:T(1,128)}, u32[]{:S(2)}, u32[]{:S(2)}) async-start(f32[16,1,3072]{2,1,0:T(1,128)} %broadcast_in_dim.110), calls=%async_computation.2 | async-start | bytes 393216 | tf_op jit(solution)/shard_map/all_to_all | solution.py:46
  91.0 25.3 %collective-permute-start.4 = (f32[384,1,256]{2,0,1:T(8,128)}, f32[384,1,256]{2,0,1:T(8,128)}, u32[]{:S(2)}, u32[]{:S(2)}) collective-permute-start(f32[384,1,256]{2,0,1:T(8,128)} %pad_maximum_fusion.1), channel_id=1, source_target_pairs={{32,0},{48,16},{64,32},{80,48},{96,64},{112,80},{128,96},{144,112}... | collective-permute-start | bytes 1179656 | tf_op jit(solution)/shard_map/ppermute | solution.py:21
  103.5 38.1 %all-to-all-start.3 = ((bf16[16,6,6144]{2,1,0:T(8,128)(2,1)}), bf16[16,6,6144]{2,1,0:T(8,128)(2,1)}, u32[]{:S(2)}, u32[]{:S(2)}) async-start(bf16[16,6,6144]{2,1,0:T(8,128)(2,1)} %bitcast.330), calls=%async_computation.3 | async-start | bytes 3145728 | tf_op jit(solution)/shard_map/all_to_all | solution.py:224
  108.7 4.6 %copy-start.1 = (bf16[3,384,384]{1,2,0:T(8,128)(2,1)S(1)}, bf16[3,384,384]{1,2,0:T(8,128)(2,1)}, u32[]{:S(2)}) copy-start(bf16[3,384,384]{1,2,0:T(8,128)(2,1)} %get-tuple-element.57) | copy-start | bytes 2654212
  108.7 4.6 %copy-start.7 = (f32[128,3,384]{2,0,1:T(8,128)S(1)}, f32[128,3,384]{2,0,1:T(8,128)}, u32[]{:S(2)}) copy-start(f32[128,3,384]{2,0,1:T(8,128)} %convolution_multiply_fusion) | copy-start | bytes 1769476
  108.7 4.6 %copy-start.8 = (f32[128,3,384]{2,0,1:T(8,128)S(1)}, f32[128,3,384]{2,0,1:T(8,128)}, u32[]{:S(2)}) copy-start(f32[128,3,384]{2,0,1:T(8,128)} %convolution_multiply_fusion.1) | copy-start | bytes 1769476
  108.7 4.6 %copy-start.10 = (bf16[384,1,256]{2,0,1:T(8,128)(2,1)S(1)}, bf16[384,1,256]{2,0,1:T(8,128)(2,1)}, u32[]{:S(2)}) copy-start(bf16[384,1,256]{2,0,1:T(8,128)(2,1)} %copy-done.9) | copy-start | bytes 589828
  110.7 26.5 %collective-permute-start.3 = (f32[384,1,256]{2,0,1:T(8,128)}, f32[384,1,256]{2,0,1:T(8,128)}, u32[]{:S(2)}, u32[]{:S(2)}) collective-permute-start(f32[384,1,256]{2,0,1:T(8,128)} %pad_maximum_fusion), channel_id=1, source_target_pairs={{16,0},{32,16},{48,32},{64,48},{80,64},{96,80},{112,96},{128,112},... | collective-permute-start | bytes 1179656 | tf_op jit(solution)/shard_map/ppermute | solution.py:21
  114.4 24.9 %copy-start.19 = (f32[3,384]{1,0:T(4,128)S(1)}, f32[3,384]{1,0:T(4,128)}, u32[]{:S(2)}) copy-start(f32[3,384]{1,0:T(4,128)} %copy-done.18) | copy-start | bytes 13828
  116.3 23.1 %copy-start.4 = (bf16[384,384]{0,1:T(8,128)(2,1)S(1)}, bf16[384,384]{0,1:T(8,128)(2,1)}, u32[]{:S(2)}) copy-start(bf16[384,384]{0,1:T(8,128)(2,1)} %copy-done.2) | copy-start | bytes 884740
  116.3 23.1 %copy-start.6 = (pred[384,384]{0,1:T(8,128)(4,1)S(1)}, pred[384,384]{0,1:T(8,128)(4,1)}, u32[]{:S(2)}) copy-start(pred[384,384]{0,1:T(8,128)(4,1)} %copy-done.5) | copy-start | bytes 442372

commit v4 on v3

--- a/solution.py
+++ b/solution.py
@@ -159,31 +159,30 @@
     row_peak, row_total, weighted = running
     log_total = row_peak + jnp.log(row_total)
     delta = weighted / row_total
-    parts = []
-    for offset, (keys_now, values_now, segs_now) in enumerate(gathered):
-        compute = functools.partial(
-            block_grads,
-            query_rows,
-            grad_rows,
-            keys_now,
-            values_now,
-            masks[offset],
-            log_total,
-            delta,
-            score_scale,
+    def grads_at(offset, rows_q, rows_g, keys_now, values_now):
+        return block_grads(
+            rows_q, rows_g, keys_now, values_now, masks[offset], log_total, delta, score_scale
         )
-        if offset == 0:
-            parts.append(compute())
-        else:
-            parts.append(compute())
+
+    parts = {}
+    returned = {}
+    for offset in range(REACH, 0, -1):
+        keys_now, values_now, _ = gathered[offset]
+        parts[offset] = grads_at(offset, query_rows, grad_rows, keys_now, values_now)
+        both = jnp.concatenate([parts[offset][1], parts[offset][2]], axis=-1)
+        returned[offset] = from_behind(both, "seq", -offset)
+    sent = [parts[offset][1:] for offset in range(1, REACH + 1)]
+    local_in, _ = lax.optimization_barrier(
+        ((query_rows, grad_rows, key_block, value_block), sent)
+    )
+    parts[0] = grads_at(0, *local_in)
     query_total = parts[0][0]
     for offset in range(1, REACH + 1):
         query_total = query_total + parts[offset][0]
     key_total = parts[0][1]
     value_total = parts[0][2]
     for offset in range(1, REACH + 1):
-        both = jnp.concatenate([parts[offset][1], parts[offset][2]], axis=-1)
-        both = from_behind(both, "seq", -offset)
+        both = returned[offset]
         key_back, value_back = both[..., :HD], both[..., HD:]
         key_total = key_total + key_back
         value_total = value_total + value_back

time: 146 us -> 142 us (0.973)
  matrix products: 24 us -> 19.3 us
  waiting for transfers between devices: 28 us -> 30.8 us
    ppermute x6, waiting for transfers between devices: 20.9 us -> 0.02 us  [from_behind(): return lax.ppermute(value, axis, pairs)]
    all_to_all x1, waiting for transfers between devices: 0.01 us -> 12.8 us  [on_device(): lax.all_to_all(outgoing, 'ep', split_axis=0, concat_axis=0, tiled=True)]
    all_to_all x1, waiting for transfers between devices: 2.59 us -> 15.1 us  [gather_back(): return lax.all_to_all(copies, axis, 0, 0, tiled=True).reshape(-1)]
    dot_general x4, matrix products: 5.89 us -> 2.73 us  [block_grads(): jnp.einsum('hgqt,qhgd->thd', score_low, query_rows, preferred_element_typ...]
    mul x3, local copies, waits for them, and re-layouts: 3.7 us -> 1.41 us  [on_device(): gates[:, :, None] * moe_grad.astype(jnp.float32)[:, None, :]]
    concatenate x3, other arithmetic: 4.58 us -> 2.34 us  [on_device(): both = jnp.concatenate([parts[offset][1], parts[offset][2]], axis=-1)]
    unnamed x49 -> x53, local copies, waits for them, and re-layouts: 5.77 us -> 7.32 us
    all_to_all x1, waiting for transfers between devices: 4.47 us -> 2.93 us  [broadcast_sum(): return lax.all_to_all(copies, axis, 0, 0, tiled=True).sum(axis=0)]
  transfers between devices with their start and end apart: 10 -> 10, of which waited for: 3 -> 3; matrix products, arithmetic and copies ran while one was open for 40% -> 35% of each run, Pallas kernels for 0% -> 0%
where the time goes in v4:
time: 142 us; the launch traced here: 141 us
  starting transfers between devices  51.5 us (36%)
  waiting for transfers between devices  30.8 us (22%)
  local copies, waits for them, and re-layouts  20.6 us (15%)
  matrix products  19.3 us (14%)
  other arithmetic  17.3 us (12%)
    ppermute x6, starting transfers between devices, from_behind(): return lax.ppermute(value, axis, pairs)  19 us
    all_to_all x1, waiting for transfers between devices, gather_back(): return lax.all_to_all(copies, axis, 0, 0, tiled=True).reshape(-1)  15.1 us
    all_to_all x1, starting transfers between devices, broadcast_sum(): return lax.all_to_all(copies, axis, 0, 0, tiled=True).sum(axis=0)  13.7 us
    all_to_all x1, waiting for transfers between devices, on_device(): lax.all_to_all(outgoing, 'ep', split_axis=0, concat_axis=0, tiled=True)  12.8 us
    unnamed x53, local copies, waits for them, and re-layouts  7.32 us
    all_to_all x1, starting transfers between devices, scatter_sum(): return lax.all_to_all(parts, axis, 0, 0, tiled=True).sum(axis=0)  6.84 us
    all_to_all x1, starting transfers between devices, gather_back(): return lax.all_to_all(copies, axis, 0, 0, tiled=True).reshape(-1)  6.71 us
    all_to_all x1, starting transfers between devices, on_device(): lax.all_to_all(outgoing, 'ep', split_axis=0, concat_axis=0, tiled=True)  5.2 us
  transfers between devices with their start and end apart: 10, of which 3 were waited for; matrix products, arithmetic and copies ran while one was open for 35% of the time, Pallas kernels for 0%

profile of v4, /device:TPU:1, one launch (start us, length us, event | category | flops | bytes accessed | tf_op | source)
XLA Modules:
  0.0 140.7 jit_solution(709191576728386568)
XLA Ops:
  0.6 0.7 convert_bitcast_fusion
  1.4 1.0 maximum_bitcast_fusion
  2.4 0.7 fusion.61
  3.1 7.7 %collective-permute-start.2 = (bf16[392,256]{1,0:T(8,128)(2,1)}, bf16[392,256]{1,0:T(8,128)(2,1)}, u32[]{:S(2)}, u32[]{:S(2)}) collective-permute-start(bf16[392,256]{1,0:T(8,128)(2,1)} %fusion.61), channel_id=1, source_target_pairs={{0,48},{16,64},{32,80},{48,96},{64,112},{80,128},{96,144},{112,160... | collective-permute-start | bytes 602120 | tf_op jit(solution)/shard_map/ppermute | solution.py:21
  10.7 4.2 %collective-permute-start.1 = (bf16[392,256]{1,0:T(8,128)(2,1)}, bf16[392,256]{1,0:T(8,128)(2,1)}, u32[]{:S(2)}, u32[]{:S(2)}) collective-permute-start(bf16[392,256]{1,0:T(8,128)(2,1)} %fusion.61), channel_id=1, source_target_pairs={{0,32},{16,48},{32,64},{48,80},{64,96},{80,112},{96,128},{112,144}... | collective-permute-start | bytes 602120 | tf_op jit(solution)/shard_map/ppermute | solution.py:21
  14.9 3.3 %collective-permute-start = (bf16[392,256]{1,0:T(8,128)(2,1)}, bf16[392,256]{1,0:T(8,128)(2,1)}, u32[]{:S(2)}, u32[]{:S(2)}) collective-permute-start(bf16[392,256]{1,0:T(8,128)(2,1)} %fusion.61), channel_id=1, source_target_pairs={{0,16},{16,32},{32,48},{48,64},{64,80},{80,96},{96,112},{112,128},... | collective-permute-start | bytes 602120 | tf_op jit(solution)/shard_map/ppermute | solution.py:21
  19.0 2.4 %fusion.54 = f32[24,1,2]{2,1,0:T(1,128)S(1)} fusion(bf16[24,2,6144]{2,1,0:T(2,128)(2,1)S(1)} %copy-done, bf16[24,6144,1]{1,0,2:T(8,128)(2,1)} %bitcast.374), kind=kOutput, calls=%fused_computation.89 | convolution fusion | flops 589824 | bytes 884928 | tf_op jit(solution)/shard_map/td,tkd->tk/dot_general | solution.py:201
  22.6 0.9 all_to_all.22
  23.5 6.8 %all-to-all-start = ((f32[16,1,3072]{2,1,0:T(1,128)}), f32[16,1,3072]{2,1,0:T(1,128)}, u32[]{:S(2)}, u32[]{:S(2)}) async-start(f32[16,1,3072]{2,1,0:T(1,128)} %all_to_all.22), calls=%async_computation | async-start | bytes 393216 | tf_op jit(solution)/shard_map/all_to_all | solution.py:41
  31.4 0.8 mul.337
  32.2 0.7 pad_maximum_fusion.3
  33.5 2.0 %sort.17 = (s32[48]{0:T(128)}, s32[48]{0:T(128)S(1)}) sort(s32[48]{0:T(128)S(1)} %multiply_add_fusion.1, s32[48]{0:T(128)S(1)} %iota.37), dimensions={0}, to_apply=%region_17.18 | sort | flops 288 | bytes 768 | tf_op jit(solution)/shard_map/jit(argsort)/sort | solution.py:219
  35.8 0.9 gather_fusion
  36.7 1.1 reshape.494
  37.8 1.2 convolution_convert_fusion
  39.0 1.1 reduce_sum.117
  40.0 0.9 broadcast_in_dim.109
  41.0 13.7 %all-to-all-start.1 = ((f32[32,1,3072]{2,1,0:T(1,128)}), f32[32,1,3072]{2,1,0:T(1,128)S(1)}, u32[]{:S(2)}, u32[]{:S(2)}) async-start(f32[32,1,3072]{2,1,0:T(1,128)} %broadcast_in_dim.109), calls=%async_computation.1 | async-start | bytes 786432 | tf_op jit(solution)/shard_map/all_to_all | solution.py:51
  56.7 0.8 and_and_fusion.2
  58.0 0.9 slice_bitcast_fusion
  59.4 0.9 slice_bitcast_fusion.1
  60.8 0.9 slice_bitcast_fusion.2
  62.8 0.7 fusion.5
  65.9 1.3 fusion.42
  69.4 0.8 pad_maximum_fusion.2
  70.2 1.3 collective-permute-start.5
  71.5 0.8 pad_maximum_fusion.1
  72.3 1.3 collective-permute-start.4
  73.6 0.8 pad_maximum_fusion
  74.3 1.3 collective-permute-start.3
  76.3 1.2 copy-done.4
  77.9 2.9 %all-to-all-done.1 = f32[32,1,3072]{2,1,0:T(1,128)S(1)} async-done(((f32[32,1,3072]{2,1,0:T(1,128)}), f32[32,1,3072]{2,1,0:T(1,128)S(1)}, u32[]{:S(2)}, u32[]{:S(2)}) %all-to-all-start.1) | async-done | bytes 393248 | tf_op jit(solution)/shard_map/all_to_all | solution.py:51
  81.0 0.8 broadcast_in_dim.110
  81.8 6.7 %all-to-all-start.2 = ((f32[16,1,3072]{2,1,0:T(1,128)}), f32[16,1,3072]{2,1,0:T(1,128)}, u32[]{:S(2)}, u32[]{:S(2)}) async-start(f32[16,1,3072]{2,1,0:T(1,128)} %broadcast_in_dim.110), calls=%async_computation.2 | async-start | bytes 393216 | tf_op jit(solution)/shard_map/all_to_all | solution.py:46
  88.5 1.2 fusion.70
  89.8 15.1 %all-to-all-done.2 = f32[16,1,3072]{2,1,0:T(1,128)} async-done(((f32[16,1,3072]{2,1,0:T(1,128)}), f32[16,1,3072]{2,1,0:T(1,128)}, u32[]{:S(2)}, u32[]{:S(2)}) %all-to-all-start.2) | async-done | bytes 196640 | tf_op jit(solution)/shard_map/all_to_all | solution.py:46
  104.8 2.2 %multiply_reduce_fusion = f32[16,3072]{1,0:T(8,128)} fusion(f32[16,1,3072]{2,1,0:T(1,128)} %all-to-all-done.2), kind=kLoop, calls=%fused_computation.113 | loop fusion | flops 49152 | bytes 393216 | tf_op jit(solution)/shard_map/div | solution.py:211
  107.0 1.7 %div.27 = f32[8,6144]{1,0:T(8,128)} reshape(f32[16,3072]{1,0:T(8,128)} %multiply_reduce_fusion) | data formatting | bytes 393216 | tf_op jit(solution)/shard_map/div | solution.py:211
  108.6 2.5 %broadcast_in_dim.112 = bf16[8,2,6,6144]{3,2,1,0:T(8,128)(2,1)} broadcast(bf16[8,6,6144]{2,1,0:T(8,128)(2,1)} %reshape.494), dimensions={0,2,3} | broadcast | bytes 1769472 | tf_op jit(solution)/shard_map/broadcast_in_dim | solution.py:221
  111.1 5.2 %all-to-all-start.3 = ((bf16[16,6,6144]{2,1,0:T(8,128)(2,1)}), bf16[16,6,6144]{2,1,0:T(8,128)(2,1)}, u32[]{:S(2)}, u32[]{:S(2)}) async-start(bf16[16,6,6144]{2,1,0:T(8,128)(2,1)} %bitcast.367), calls=%async_computation.3 | async-start | bytes 3145728 | tf_op jit(solution)/shard_map/all_to_all | solution.py:223
  116.3 1.7 %convolution_add_fusion.2 = f32[128,3,384]{2,0,1:T(8,128)S(1)} fusion(f32[128,3,384]{2,0,1:T(8,128)S(1)} %fusion.70, bf16[3,384,384]{1,2,0:T(8,128)(2,1)} %copy-done.3, bf16[384,1,256]{2,0,1:T(8,128)(2,1)} %copy-done.9), kind=kOutput, calls=%fused_computation.47 | convolution fusion | flops 113393664 | bytes 2162688 | tf_op jit(solution)/shard_map/hgqt,thd->qhgd/dot_general | solution.py:106
  118.8 0.9 copy.204
  119.7 1.5 %fusion.64 = bf16[384,128]{0,1:T(8,128)(2,1)S(1)} fusion(f32[384,1,256]{0,2,1:T(8,128)} %collective-permute-done.5, f32[384,1,256]{0,2,1:T(8,128)} %collective-permute-done.4, f32[384,1,256]{0,2,1:T(8,128)} %collective-permute-done.3, bf16[3,384,384]{1,2,0:T(8,128)(2,1)S(1)} %fusion.22, bf16[384,1,3,128]{0,3,2,1:T(8,128)(2,1)S(1)} %bitcast.357), kind=kOutput, calls=%fused_computation.114 | convolution fusion | flops 113491968 | bytes 1867776 | tf_op jit(solution)/shard_map/hgqt,qhgd->thd/dot_general | solution.py:110
  121.2 0.8 copy.205
  122.0 2.0 %fusion.65 = bf16[384,128]{0,1:T(8,128)(2,1)S(1)} fusion(f32[384,1,256]{0,2,1:T(8,128)} %collective-permute-done.5, f32[384,1,256]{0,2,1:T(8,128)} %collective-permute-done.4, f32[384,1,256]{0,2,1:T(8,128)} %collective-permute-done.3, f32[1,3,384,384]{2,3,1,0:T(8,128)} %copy-done.4, bf16[384,1,3,128]{0,3,2,1:T(8,128)(2,1)S(1)} %bitcast.366), kind=kOutput, calls=%fused_computation.115 | convolution fusion | flops 113885184 | bytes 2752512 | tf_op jit(solution)/shard_map/hgqt,qhgd->thd/dot_general | solution.py:98
  124.0 0.8 copy.206
  124.8 12.8 %all-to-all-done.3 = bf16[16,6,6144]{2,1,0:T(8,128)(2,1)} async-done(((bf16[16,6,6144]{2,1,0:T(8,128)(2,1)}), bf16[16,6,6144]{2,1,0:T(8,128)(2,1)}, u32[]{:S(2)}, u32[]{:S(2)}) %all-to-all-start.3) | async-done | bytes 1179680 | tf_op jit(solution)/shard_map/all_to_all | solution.py:223
  137.6 3.1 %copy.207 = bf16[16,6,6144]{2,0,1:T(8,128)(2,1)} copy(bf16[16,6,6144]{2,1,0:T(8,128)(2,1)} %all-to-all-done.3) | data formatting | bytes 2359296
  (101 shorter events, 14.6 us)
Async XLA Ops:
  0.6 18.3 %copy-start = (bf16[24,2,6144]{2,1,0:T(2,128)(2,1)S(1)}, bf16[24,2,6144]{2,1,0:T(2,128)(2,1)}, u32[]{:S(2)}) copy-start(bf16[24,2,6144]{2,1,0:T(2,128)(2,1)} %param.16) | copy-start | bytes 1769476
  3.1 52.3 %collective-permute-start.2 = (bf16[392,256]{1,0:T(8,128)(2,1)}, bf16[392,256]{1,0:T(8,128)(2,1)}, u32[]{:S(2)}, u32[]{:S(2)}) collective-permute-start(bf16[392,256]{1,0:T(8,128)(2,1)} %fusion.61), channel_id=1, source_target_pairs={{0,48},{16,64},{32,80},{48,96},{64,112},{80,128},{96,144},{112,160... | collective-permute-start | bytes 602120 | tf_op jit(solution)/shard_map/ppermute | solution.py:21
  10.7 44.0 %collective-permute-start.1 = (bf16[392,256]{1,0:T(8,128)(2,1)}, bf16[392,256]{1,0:T(8,128)(2,1)}, u32[]{:S(2)}, u32[]{:S(2)}) collective-permute-start(bf16[392,256]{1,0:T(8,128)(2,1)} %fusion.61), channel_id=1, source_target_pairs={{0,32},{16,48},{32,64},{48,80},{64,96},{80,112},{96,128},{112,144}... | collective-permute-start | bytes 602120 | tf_op jit(solution)/shard_map/ppermute | solution.py:21
  14.9 41.1 %collective-permute-start = (bf16[392,256]{1,0:T(8,128)(2,1)}, bf16[392,256]{1,0:T(8,128)(2,1)}, u32[]{:S(2)}, u32[]{:S(2)}) collective-permute-start(bf16[392,256]{1,0:T(8,128)(2,1)} %fusion.61), channel_id=1, source_target_pairs={{0,16},{16,32},{32,48},{48,64},{64,80},{80,96},{96,112},{112,128},... | collective-permute-start | bytes 602120 | tf_op jit(solution)/shard_map/ppermute | solution.py:21
  18.9 3.3 %copy-start.18 = (f32[24,2,8]{0,2,1:T(8,128)}, f32[24,2,8]{0,2,1:T(8,128)S(1)}, u32[]{:S(2)}) copy-start(f32[24,2,8]{0,2,1:T(8,128)S(1)} %fusion.79) | copy-start | bytes 4612
  18.9 2.6 %copy-start.10 = (bf16[24,6144]{1,0:T(8,128)(2,1)S(1)}, bf16[24,6144]{1,0:T(8,128)(2,1)}, u32[]{:S(2)}) copy-start(bf16[24,6144]{1,0:T(8,128)(2,1)} %param.17) | copy-start | bytes 884740
  18.9 2.6 %copy-start.12 = (bf16[8,6144]{1,0:T(8,128)(2,1)S(1)}, bf16[8,6144]{1,0:T(8,128)(2,1)}, u32[]{:S(2)}) copy-start(bf16[8,6144]{1,0:T(8,128)(2,1)} %param.18) | copy-start | bytes 294916
  19.0 2.7 %copy-start.21 = (s32[24,2]{0,1:T(2,128)S(1)}, s32[24,2]{0,1:T(2,128)}, u32[]{:S(2)}) copy-start(s32[24,2]{0,1:T(2,128)} %param.19) | copy-start | bytes 580
  21.4 9.0 %copy-start.15 = (bf16[384,384]{1,0:T(8,128)(2,1)S(1)}, bf16[384,384]{1,0:T(8,128)(2,1)}, u32[]{:S(2)}) copy-start(bf16[384,384]{1,0:T(8,128)(2,1)} %param.10) | copy-start | bytes 884740
  21.4 9.2 %copy-start.16 = (bf16[384,384]{1,0:T(8,128)(2,1)S(1)}, bf16[384,384]{1,0:T(8,128)(2,1)}, u32[]{:S(2)}) copy-start(bf16[384,384]{1,0:T(8,128)(2,1)} %param.13) | copy-start | bytes 884740
  21.4 9.5 %copy-start.17 = (bf16[24,6144]{1,0:T(8,128)(2,1)S(1)}, bf16[24,6144]{1,0:T(8,128)(2,1)}, u32[]{:S(2)}) copy-start(bf16[24,6144]{1,0:T(8,128)(2,1)} %param.15) | copy-start | bytes 884740
  22.3 8.1 %copy-start.22 = (f32[24,1]{0,1:T(1,128)}, f32[24,1]{0,1:T(1,128)S(1)}, u32[]{:S(2)}) copy-start(f32[24,1]{0,1:T(1,128)S(1)} %get-tuple-element.57) | copy-start | bytes 292
  23.5 15.5 %all-to-all-start = ((f32[16,1,3072]{2,1,0:T(1,128)}), f32[16,1,3072]{2,1,0:T(1,128)}, u32[]{:S(2)}, u32[]{:S(2)}) async-start(f32[16,1,3072]{2,1,0:T(1,128)} %all_to_all.22), calls=%async_computation | async-start | bytes 393216 | tf_op jit(solution)/shard_map/all_to_all | solution.py:41
  35.7 2.1 %copy-start.13 = (bf16[8,6144]{1,0:T(8,128)(2,1)S(1)}, bf16[8,6144]{1,0:T(8,128)(2,1)}, u32[]{:S(2)}) copy-start(bf16[8,6144]{1,0:T(8,128)(2,1)} %param.18) | copy-start | bytes 294916
  35.7 2.1 %copy-start.19 = (f32[24,2,8]{0,2,1:T(8,128)S(1)}, f32[24,2,8]{0,2,1:T(8,128)}, u32[]{:S(2)}) copy-start(f32[24,2,8]{0,2,1:T(8,128)} %copy-done.18) | copy-start | bytes 4612
  36.7 20.0 %copy-start.20 = (s32[384]{0:T(512)S(1)}, s32[384]{0:T(512)}, u32[]{:S(2)}) copy-start(s32[384]{0:T(512)} %param.14) | copy-start | bytes 4612
  36.7 20.8 %copy-start.11 = (bf16[384,128]{1,0:T(8,128)(2,1)S(1)}, bf16[384,128]{1,0:T(8,128)(2,1)}, u32[]{:S(2)}) copy-start(bf16[384,128]{1,0:T(8,128)(2,1)} %param.11) | copy-start | bytes 294916
  41.0 39.8 %all-to-all-start.1 = ((f32[32,1,3072]{2,1,0:T(1,128)}), f32[32,1,3072]{2,1,0:T(1,128)S(1)}, u32[]{:S(2)}, u32[]{:S(2)}) async-start(f32[32,1,3072]{2,1,0:T(1,128)} %broadcast_in_dim.109), calls=%async_computation.1 | async-start | bytes 786432 | tf_op jit(solution)/shard_map/all_to_all | solution.py:51
  58.9 4.5 %copy-start.5 = (bf16[384,1,256]{2,0,1:T(8,128)(2,1)}, bf16[384,1,256]{2,0,1:T(8,128)(2,1)S(1)}, u32[]{:S(2)}) copy-start(bf16[384,1,256]{2,0,1:T(8,128)(2,1)S(1)} %slice_bitcast_fusion) | copy-start | bytes 589828
  60.4 3.7 %copy-start.7 = (bf16[384,1,256]{2,0,1:T(8,128)(2,1)}, bf16[384,1,256]{2,0,1:T(8,128)(2,1)S(1)}, u32[]{:S(2)}) copy-start(bf16[384,1,256]{2,0,1:T(8,128)(2,1)S(1)} %slice_bitcast_fusion.1) | copy-start | bytes 589828
  61.8 3.0 %copy-start.9 = (bf16[384,1,256]{2,0,1:T(8,128)(2,1)}, bf16[384,1,256]{2,0,1:T(8,128)(2,1)S(1)}, u32[]{:S(2)}) copy-start(bf16[384,1,256]{2,0,1:T(8,128)(2,1)S(1)} %slice_bitcast_fusion.2) | copy-start | bytes 589828
  61.8 1.0 copy-start.14
  67.2 1.3 copy-start.1
  67.2 1.3 copy-start.3
  70.2 49.5 %collective-permute-start.5 = (f32[384,1,256]{0,2,1:T(8,128)}, f32[384,1,256]{0,2,1:T(8,128)}, u32[]{:S(2)}, u32[]{:S(2)}) collective-permute-start(f32[384,1,256]{0,2,1:T(8,128)} %pad_maximum_fusion.2), channel_id=1, source_target_pairs={{48,0},{64,16},{80,32},{96,48},{112,64},{128,80},{144,96},{160,112... | collective-permute-start | bytes 1179656 | tf_op jit(solution)/shard_map/ppermute | solution.py:21
  72.3 47.4 %collective-permute-start.4 = (f32[384,1,256]{0,2,1:T(8,128)}, f32[384,1,256]{0,2,1:T(8,128)}, u32[]{:S(2)}, u32[]{:S(2)}) collective-permute-start(f32[384,1,256]{0,2,1:T(8,128)} %pad_maximum_fusion.1), channel_id=1, source_target_pairs={{32,0},{48,16},{64,32},{80,48},{96,64},{112,80},{128,96},{144,112}... | collective-permute-start | bytes 1179656 | tf_op jit(solution)/shard_map/ppermute | solution.py:21
  74.3 45.4 %collective-permute-start.3 = (f32[384,1,256]{0,2,1:T(8,128)}, f32[384,1,256]{0,2,1:T(8,128)}, u32[]{:S(2)}, u32[]{:S(2)}) collective-permute-start(f32[384,1,256]{0,2,1:T(8,128)} %pad_maximum_fusion), channel_id=1, source_target_pairs={{16,0},{32,16},{48,32},{64,48},{80,64},{96,80},{112,96},{128,112},... | collective-permute-start | bytes 1179656 | tf_op jit(solution)/shard_map/ppermute | solution.py:21
  76.3 1.2 copy-start.4
  81.8 23.0 %all-to-all-start.2 = ((f32[16,1,3072]{2,1,0:T(1,128)}), f32[16,1,3072]{2,1,0:T(1,128)}, u32[]{:S(2)}, u32[]{:S(2)}) async-start(f32[16,1,3072]{2,1,0:T(1,128)} %broadcast_in_dim.110), calls=%async_computation.2 | async-start | bytes 393216 | tf_op jit(solution)/shard_map/all_to_all | solution.py:46
  111.1 26.5 %all-to-all-start.3 = ((bf16[16,6,6144]{2,1,0:T(8,128)(2,1)}), bf16[16,6,6144]{2,1,0:T(8,128)(2,1)}, u32[]{:S(2)}, u32[]{:S(2)}) async-start(bf16[16,6,6144]{2,1,0:T(8,128)(2,1)} %bitcast.367), calls=%async_computation.3 | async-start | bytes 3145728 | tf_op jit(solution)/shard_map/all_to_all | solution.py:223
  116.3 1.7 %copy-start.2 = (bf16[3,384,384]{1,2,0:T(8,128)(2,1)S(1)}, bf16[3,384,384]{1,2,0:T(8,128)(2,1)}, u32[]{:S(2)}) copy-start(bf16[3,384,384]{1,2,0:T(8,128)(2,1)} %copy-done.1) | copy-start | bytes 2654212
  116.3 1.7 %copy-start.8 = (bf16[384,1,256]{2,0,1:T(8,128)(2,1)S(1)}, bf16[384,1,256]{2,0,1:T(8,128)(2,1)}, u32[]{:S(2)}) copy-start(bf16[384,1,256]{2,0,1:T(8,128)(2,1)} %copy-done.7) | copy-start | bytes 589828
  116.3 2.1 %copy-start.6 = (bf16[384,1,256]{2,0,1:T(8,128)(2,1)S(1)}, bf16[384,1,256]{2,0,1:T(8,128)(2,1)}, u32[]{:S(2)}) copy-start(bf16[384,1,256]{2,0,1:T(8,128)(2,1)} %copy-done.5) | copy-start | bytes 589828

commit v5 on v4

--- a/solution.py
+++ b/solution.py
@@ -208,7 +208,6 @@
         logit_grad.T, normed.astype(jnp.float32), precision=lax.Precision.HIGHEST
     )
     all_tokens = moe_rows * lax.axis_size("seq") * ep_size
-    router_grad = sum_everywhere(local_router) / all_tokens
     gates = jnp.stack([first_gate, second_gate], axis=1)
     expert_rows = (gates[:, :, None] * moe_grad.astype(jnp.float32)[:, None, :]).astype(
         jnp.bfloat16
@@ -219,8 +218,16 @@
     order = jnp.argsort(flat_routes * capacity + ranks)
     outgoing = expert_rows.reshape(-1, expert_rows.shape[2])[order]
     outgoing = jnp.repeat(outgoing.reshape(EXPERTS, capacity, -1), copies, axis=0)
-    router_grad, outgoing = lax.optimization_barrier((router_grad, outgoing))
-    routed_grads = lax.all_to_all(outgoing, "ep", split_axis=0, concat_axis=0, tiled=True)
+    slots = outgoing.shape[0]
+    router_parts = local_router.reshape(slots, -1)
+    merged = jnp.concatenate(
+        [outgoing.reshape(slots, -1).astype(jnp.float32), router_parts], axis=1
+    )
+    merged = lax.all_to_all(merged, "ep", split_axis=0, concat_axis=0, tiled=True)
+    split_at = merged.shape[1] - router_parts.shape[1]
+    routed_grads = merged[:, :split_at].reshape(outgoing.shape).astype(jnp.bfloat16)
+    router_flat = broadcast_sum(merged[:, split_at:].sum(axis=0), "seq")
+    router_grad = gather_back(router_flat, "ep").reshape(local_router.shape) / all_tokens
     return (query_grad, key_grad, value_grad, normed_grad, router_grad, routed_grads)
 
 

time: 142 us -> 143 us (level)
  local copies, waits for them, and re-layouts: 20.6 us -> 27.6 us
  starting transfers between devices: 51.5 us -> 47.3 us
  other arithmetic: 17.3 us -> 14.1 us
  waiting for transfers between devices: 30.8 us -> 33.7 us
  matrix products: 19.3 us -> 17.8 us
    all_to_all x1, waiting for transfers between devices: 2.93 us -> 18 us  [broadcast_sum(): return lax.all_to_all(copies, axis, 0, 0, tiled=True).sum(axis=0)]
    all_to_all x1, waiting for transfers between devices: 15.1 us -> 1.09 us  [gather_back(): return lax.all_to_all(copies, axis, 0, 0, tiled=True).reshape(-1)]
    all_to_all x2 -> x1, starting transfers between devices: 12 us -> 6.98 us  [on_device(): lax.all_to_all(merged, 'ep', split_axis=0, concat_axis=0, tiled=True)]
    unnamed x53 -> x66, local copies, waits for them, and re-layouts: 7.32 us -> 11.6 us
    all_to_all x1, local copies, waits for them, and re-layouts: 0.94 us -> 4.12 us  [on_device(): lax.all_to_all(merged, 'ep', split_axis=0, concat_axis=0, tiled=True)]
    broadcast_in_dim x1, local copies, waits for them, and re-layouts: 2.46 us -> 0.3 us  [on_device(): jnp.repeat(outgoing.reshape(EXPERTS, capacity, -1), copies, axis=0)]
    slice x0 -> x1, local copies, waits for them, and re-layouts: none -> 1.78 us  [on_device(): merged[:, :split_at].reshape(outgoing.shape).astype(jnp.bfloat16)]
    all_to_all x2 -> x1, waiting for transfers between devices: 12.8 us -> 14.6 us  [on_device(): lax.all_to_all(merged, 'ep', split_axis=0, concat_axis=0, tiled=True)]
  transfers between devices with their start and end apart: 10 -> 9, of which waited for: 3 -> 3; matrix products, arithmetic and copies ran while one was open for 35% -> 36% of each run, Pallas kernels for 0% -> 0%
where the time goes in v5:
time: 143 us; the launch traced here: 142 us
  starting transfers between devices  47.3 us (33%)
  waiting for transfers between devices  33.7 us (24%)
  local copies, waits for them, and re-layouts  27.6 us (19%)
  matrix products  17.8 us (12%)
  other arithmetic  14.1 us (10%)
    ppermute x6, starting transfers between devices, from_behind(): return lax.ppermute(value, axis, pairs)  19.1 us
    all_to_all x1, waiting for transfers between devices, broadcast_sum(): return lax.all_to_all(copies, axis, 0, 0, tiled=True).sum(axis=0)  18 us
    all_to_all x1, waiting for transfers between devices, on_device(): lax.all_to_all(merged, 'ep', split_axis=0, concat_axis=0, tiled=True)  14.6 us
    all_to_all x1, starting transfers between devices, broadcast_sum(): return lax.all_to_all(copies, axis, 0, 0, tiled=True).sum(axis=0)  14.5 us
    unnamed x66, local copies, waits for them, and re-layouts  11.6 us
    all_to_all x1, starting transfers between devices, on_device(): lax.all_to_all(merged, 'ep', split_axis=0, concat_axis=0, tiled=True)  6.98 us
    all_to_all x1, starting transfers between devices, gather_back(): return lax.all_to_all(copies, axis, 0, 0, tiled=True).reshape(-1)  6.78 us
    all_to_all x1, local copies, waits for them, and re-layouts, on_device(): lax.all_to_all(merged, 'ep', split_axis=0, concat_axis=0, tiled=True)  4.12 us
  transfers between devices with their start and end apart: 9, of which 3 were waited for; matrix products, arithmetic and copies ran while one was open for 36% of the time, Pallas kernels for 0%

profile of v5, /device:TPU:1, one launch (start us, length us, event | category | flops | bytes accessed | tf_op | source)
XLA Modules:
  0.0 141.8 jit_solution(17692996780176918238)
XLA Ops:
  0.6 0.7 convert_bitcast_fusion
  1.4 1.0 maximum_bitcast_fusion.1
  2.4 0.7 fusion.61
  3.1 7.7 %collective-permute-start.2 = (bf16[392,256]{1,0:T(8,128)(2,1)}, bf16[392,256]{1,0:T(8,128)(2,1)}, u32[]{:S(2)}, u32[]{:S(2)}) collective-permute-start(bf16[392,256]{1,0:T(8,128)(2,1)} %fusion.61), channel_id=1, source_target_pairs={{0,48},{16,64},{32,80},{48,96},{64,112},{80,128},{96,144},{112,160... | collective-permute-start | bytes 602120 | tf_op jit(solution)/shard_map/ppermute | solution.py:21
  10.7 4.2 %collective-permute-start.1 = (bf16[392,256]{1,0:T(8,128)(2,1)}, bf16[392,256]{1,0:T(8,128)(2,1)}, u32[]{:S(2)}, u32[]{:S(2)}) collective-permute-start(bf16[392,256]{1,0:T(8,128)(2,1)} %fusion.61), channel_id=1, source_target_pairs={{0,32},{16,48},{32,64},{48,80},{64,96},{80,112},{96,128},{112,144}... | collective-permute-start | bytes 602120 | tf_op jit(solution)/shard_map/ppermute | solution.py:21
  15.0 3.3 %collective-permute-start = (bf16[392,256]{1,0:T(8,128)(2,1)}, bf16[392,256]{1,0:T(8,128)(2,1)}, u32[]{:S(2)}, u32[]{:S(2)}) collective-permute-start(bf16[392,256]{1,0:T(8,128)(2,1)} %fusion.61), channel_id=1, source_target_pairs={{0,16},{16,32},{32,48},{48,64},{64,80},{80,96},{96,112},{112,128},... | collective-permute-start | bytes 602120 | tf_op jit(solution)/shard_map/ppermute | solution.py:21
  18.3 0.7 fusion.79
  19.0 0.8 copy.200
  19.8 2.5 %fusion.54 = f32[24,1,2]{2,1,0:T(1,128)S(1)} fusion(bf16[24,2,6144]{2,1,0:T(2,128)(2,1)S(1)} %copy-done, bf16[24,6144,1]{1,0,2:T(8,128)(2,1)} %bitcast.390), kind=kOutput, calls=%fused_computation.93 | convolution fusion | flops 589824 | bytes 884928 | tf_op jit(solution)/shard_map/td,tkd->tk/dot_general | solution.py:201
  23.9 0.7 reshape.496
  25.1 0.8 mul.337
  26.6 2.0 %sort.17 = (s32[48]{0:T(128)}, s32[48]{0:T(128)S(1)}) sort(s32[48]{0:T(128)S(1)} %multiply_add_fusion.1, s32[48]{0:T(128)S(1)} %iota.37), dimensions={0}, to_apply=%region_15.16 | sort | flops 288 | bytes 768 | tf_op jit(solution)/shard_map/jit(argsort)/sort | solution.py:218
  28.8 0.9 gather_fusion
  30.2 1.4 copy.242
  31.7 4.1 %copy.201 = f32[16,1,39936]{2,1,0:T(1,128)} copy(f32[16,1,39936]{2,0,1:T(8,128)S(1)} %maximum_bitcast_fusion) | data formatting | bytes 5111808 | tf_op jit(solution)/shard_map/all_to_all | solution.py:226
  35.9 7.0 %all-to-all-start = ((f32[16,1,39936]{2,1,0:T(1,128)}), f32[16,1,39936]{2,1,0:T(1,128)}, u32[]{:S(2)}, u32[]{:S(2)}) async-start(f32[16,1,39936]{2,1,0:T(1,128)} %copy.201), calls=%async_computation | async-start | bytes 5111808 | tf_op jit(solution)/shard_map/all_to_all | solution.py:226
  43.4 1.2 convolution_convert_fusion
  44.6 0.7 fusion.83
  46.6 0.8 and_and_fusion.2
  47.9 0.9 slice_bitcast_fusion
  49.3 0.9 slice_bitcast_fusion.1
  50.7 0.9 slice_bitcast_fusion.2
  52.6 0.7 fusion.5
  55.3 1.3 fusion.42
  59.3 0.8 pad_maximum_fusion.2
  60.0 1.3 collective-permute-start.5
  61.3 0.8 pad_maximum_fusion.1
  62.1 1.3 collective-permute-start.4
  63.4 0.8 pad_maximum_fusion
  64.2 1.3 collective-permute-start.3
  65.5 14.6 %all-to-all-done = f32[16,1,39936]{2,1,0:T(1,128)} async-done(((f32[16,1,39936]{2,1,0:T(1,128)}), f32[16,1,39936]{2,1,0:T(1,128)}, u32[]{:S(2)}, u32[]{:S(2)}) %all-to-all-start) | async-done | bytes 2555936 | tf_op jit(solution)/shard_map/all_to_all | solution.py:226
  80.0 2.2 %copy.247 = f32[16,1,39936]{2,0,1:T(8,128)S(1)} copy(f32[16,1,39936]{2,1,0:T(1,128)} %all-to-all-done) | data formatting | bytes 5111808
  82.3 1.5 %copy-done.6 = f32[16,1,39936]{2,0,1:T(8,128)} copy-done((f32[16,1,39936]{2,0,1:T(8,128)}, f32[16,1,39936]{2,0,1:T(8,128)S(1)}, u32[]{:S(2)}) %copy-start.6) | copy-done | bytes 2555928
  83.7 0.9 broadcast_in_dim.111
  84.7 14.5 %all-to-all-start.1 = ((f32[32,1,3072]{2,1,0:T(1,128)}), f32[32,1,3072]{2,1,0:T(1,128)S(1)}, u32[]{:S(2)}, u32[]{:S(2)}) async-start(f32[32,1,3072]{2,1,0:T(1,128)} %broadcast_in_dim.111), calls=%async_computation.1 | async-start | bytes 786432 | tf_op jit(solution)/shard_map/all_to_all | solution.py:51
  102.7 1.1 fusion.25
  103.8 1.8 %copy.203 = bf16[384,384]{1,0:T(8,128)(2,1)} copy(bf16[384,384]{0,1:T(8,128)(2,1)} %bitcast.383) | data formatting | bytes 589824
  105.7 1.5 %fusion.64 = bf16[384,128]{0,1:T(8,128)(2,1)S(1)} fusion(f32[384,1,256]{0,2,1:T(8,128)} %collective-permute-done.5, f32[384,1,256]{0,2,1:T(8,128)} %collective-permute-done.4, f32[384,1,256]{0,2,1:T(8,128)} %collective-permute-done.3, bf16[3,384,384]{1,2,0:T(8,128)(2,1)S(1)} %fusion.22, bf16[384,1,3,128]{0,3,2,1:T(8,128)(2,1)S(1)} %bitcast.368), kind=kOutput, calls=%fused_computation.119 | convolution fusion | flops 113491968 | bytes 1867776 | tf_op jit(solution)/shard_map/hgqt,qhgd->thd/dot_general | solution.py:110
  107.2 0.8 copy.204
  108.0 18.0 %all-to-all-done.1 = f32[32,1,3072]{2,1,0:T(1,128)S(1)} async-done(((f32[32,1,3072]{2,1,0:T(1,128)}), f32[32,1,3072]{2,1,0:T(1,128)S(1)}, u32[]{:S(2)}, u32[]{:S(2)}) %all-to-all-start.1) | async-done | bytes 393248 | tf_op jit(solution)/shard_map/all_to_all | solution.py:51
  126.2 0.8 broadcast_in_dim.112
  126.9 6.8 %all-to-all-start.2 = ((f32[16,1,3072]{2,1,0:T(1,128)}), f32[16,1,3072]{2,1,0:T(1,128)S(1)}, u32[]{:S(2)}, u32[]{:S(2)}) async-start(f32[16,1,3072]{2,1,0:T(1,128)} %broadcast_in_dim.112), calls=%async_computation.2 | async-start | bytes 393216 | tf_op jit(solution)/shard_map/all_to_all | solution.py:46
  133.7 2.0 %fusion.65 = bf16[384,128]{0,1:T(8,128)(2,1)S(1)} fusion(f32[384,1,256]{0,2,1:T(8,128)} %collective-permute-done.5, f32[384,1,256]{0,2,1:T(8,128)} %collective-permute-done.4, f32[384,1,256]{0,2,1:T(8,128)} %collective-permute-done.3, f32[1,3,384,384]{2,3,1,0:T(8,128)} %copy-done.5, bf16[384,1,3,128]{0,3,2,1:T(8,128)(2,1)S(1)} %bitcast.378), kind=kOutput, calls=%fused_computation.120 | convolution fusion | flops 113885184 | bytes 2752512 | tf_op jit(solution)/shard_map/hgqt,qhgd->thd/dot_general | solution.py:98
  135.8 0.8 copy.205
  136.5 1.8 %slice.202 = bf16[16,36864]{1,0:T(8,128)(2,1)S(1)} slice(f32[16,39936]{1,0:T(8,128)} %bitcast.381), slice={[0:16], [0:36864]} | slice | bytes 2359296 | tf_op jit(solution)/shard_map/slice | solution.py:228
  138.3 1.1 copy.248
  139.4 1.1 all-to-all-done.2
  141.0 0.7 div.27
  (116 shorter events, 16.6 us)
Async XLA Ops:
  0.6 19.1 %copy-start = (bf16[24,2,6144]{2,1,0:T(2,128)(2,1)S(1)}, bf16[24,2,6144]{2,1,0:T(2,128)(2,1)}, u32[]{:S(2)}) copy-start(bf16[24,2,6144]{2,1,0:T(2,128)(2,1)} %param.16) | copy-start | bytes 1769476
  3.1 42.2 %collective-permute-start.2 = (bf16[392,256]{1,0:T(8,128)(2,1)}, bf16[392,256]{1,0:T(8,128)(2,1)}, u32[]{:S(2)}, u32[]{:S(2)}) collective-permute-start(bf16[392,256]{1,0:T(8,128)(2,1)} %fusion.61), channel_id=1, source_target_pairs={{0,48},{16,64},{32,80},{48,96},{64,112},{80,128},{96,144},{112,160... | collective-permute-start | bytes 602120 | tf_op jit(solution)/shard_map/ppermute | solution.py:21
  10.7 33.8 %collective-permute-start.1 = (bf16[392,256]{1,0:T(8,128)(2,1)}, bf16[392,256]{1,0:T(8,128)(2,1)}, u32[]{:S(2)}, u32[]{:S(2)}) collective-permute-start(bf16[392,256]{1,0:T(8,128)(2,1)} %fusion.61), channel_id=1, source_target_pairs={{0,32},{16,48},{32,64},{48,80},{64,96},{80,112},{96,128},{112,144}... | collective-permute-start | bytes 602120 | tf_op jit(solution)/shard_map/ppermute | solution.py:21
  15.0 31.0 %collective-permute-start = (bf16[392,256]{1,0:T(8,128)(2,1)}, bf16[392,256]{1,0:T(8,128)(2,1)}, u32[]{:S(2)}, u32[]{:S(2)}) collective-permute-start(bf16[392,256]{1,0:T(8,128)(2,1)} %fusion.61), channel_id=1, source_target_pairs={{0,16},{16,32},{32,48},{48,64},{64,80},{80,96},{96,112},{112,128},... | collective-permute-start | bytes 602120 | tf_op jit(solution)/shard_map/ppermute | solution.py:21
  19.0 4.6 %copy-start.22 = (f32[24,2,8]{0,2,1:T(8,128)}, f32[24,2,8]{0,2,1:T(8,128)S(1)}, u32[]{:S(2)}) copy-start(f32[24,2,8]{0,2,1:T(8,128)S(1)} %fusion.79) | copy-start | bytes 4612
  19.7 2.6 %copy-start.11 = (bf16[24,6144]{1,0:T(8,128)(2,1)S(1)}, bf16[24,6144]{1,0:T(8,128)(2,1)}, u32[]{:S(2)}) copy-start(bf16[24,6144]{1,0:T(8,128)(2,1)} %param.17) | copy-start | bytes 884740
  19.7 2.6 %copy-start.15 = (bf16[8,6144]{1,0:T(8,128)(2,1)S(1)}, bf16[8,6144]{1,0:T(8,128)(2,1)}, u32[]{:S(2)}) copy-start(bf16[8,6144]{1,0:T(8,128)(2,1)} %param.18) | copy-start | bytes 294916
  19.7 2.8 %copy-start.25 = (s32[24,2]{0,1:T(2,128)S(1)}, s32[24,2]{0,1:T(2,128)}, u32[]{:S(2)}) copy-start(s32[24,2]{0,1:T(2,128)} %param.19) | copy-start | bytes 580
  19.8 4.8 %copy-start.21 = (bf16[24,6144]{1,0:T(8,128)(2,1)S(1)}, bf16[24,6144]{1,0:T(8,128)(2,1)}, u32[]{:S(2)}) copy-start(bf16[24,6144]{1,0:T(8,128)(2,1)} %param.15) | copy-start | bytes 884740
  23.1 0.5 copy-start.26
  24.6 1.3 copy-start.27
  24.6 1.3 copy-start.28
  30.2 1.4 copy-start.14
  35.9 7.0 %copy-start.19 = (bf16[384,384]{1,0:T(8,128)(2,1)S(1)}, bf16[384,384]{1,0:T(8,128)(2,1)}, u32[]{:S(2)}) copy-start(bf16[384,384]{1,0:T(8,128)(2,1)} %param.10) | copy-start | bytes 884740
  35.9 7.3 %copy-start.20 = (bf16[384,384]{1,0:T(8,128)(2,1)S(1)}, bf16[384,384]{1,0:T(8,128)(2,1)}, u32[]{:S(2)}) copy-start(bf16[384,384]{1,0:T(8,128)(2,1)} %param.13) | copy-start | bytes 884740
  35.9 7.5 %copy-start.16 = (bf16[8,6144]{1,0:T(8,128)(2,1)S(1)}, bf16[8,6144]{1,0:T(8,128)(2,1)}, u32[]{:S(2)}) copy-start(bf16[8,6144]{1,0:T(8,128)(2,1)} %param.18) | copy-start | bytes 294916
  35.9 7.5 %copy-start.23 = (f32[24,2,8]{0,2,1:T(8,128)S(1)}, f32[24,2,8]{0,2,1:T(8,128)}, u32[]{:S(2)}) copy-start(f32[24,2,8]{0,2,1:T(8,128)} %copy-done.22) | copy-start | bytes 4612
  35.9 10.7 %copy-start.24 = (s32[384]{0:T(512)S(1)}, s32[384]{0:T(512)}, u32[]{:S(2)}) copy-start(s32[384]{0:T(512)} %param.14) | copy-start | bytes 4612
  35.9 44.1 %all-to-all-start = ((f32[16,1,39936]{2,1,0:T(1,128)}), f32[16,1,39936]{2,1,0:T(1,128)}, u32[]{:S(2)}, u32[]{:S(2)}) async-start(f32[16,1,39936]{2,1,0:T(1,128)} %copy.201), calls=%async_computation | async-start | bytes 5111808 | tf_op jit(solution)/shard_map/all_to_all | solution.py:226
  42.9 4.5 %copy-start.12 = (bf16[384,128]{1,0:T(8,128)(2,1)S(1)}, bf16[384,128]{1,0:T(8,128)(2,1)}, u32[]{:S(2)}) copy-start(bf16[384,128]{1,0:T(8,128)(2,1)} %param.11) | copy-start | bytes 294916
  50.2 3.7 %copy-start.7 = (bf16[384,1,256]{2,0,1:T(8,128)(2,1)}, bf16[384,1,256]{2,0,1:T(8,128)(2,1)S(1)}, u32[]{:S(2)}) copy-start(bf16[384,1,256]{2,0,1:T(8,128)(2,1)S(1)} %slice_bitcast_fusion.1) | copy-start | bytes 589828
  51.6 2.9 %copy-start.9 = (bf16[384,1,256]{2,0,1:T(8,128)(2,1)}, bf16[384,1,256]{2,0,1:T(8,128)(2,1)S(1)}, u32[]{:S(2)}) copy-start(bf16[384,1,256]{2,0,1:T(8,128)(2,1)S(1)} %slice_bitcast_fusion.2) | copy-start | bytes 589828
  51.7 1.0 copy-start.17
  56.6 1.3 copy-start.1
  56.6 1.3 copy-start.3
  60.0 45.6 %collective-permute-start.5 = (f32[384,1,256]{0,2,1:T(8,128)}, f32[384,1,256]{0,2,1:T(8,128)}, u32[]{:S(2)}, u32[]{:S(2)}) collective-permute-start(f32[384,1,256]{0,2,1:T(8,128)} %pad_maximum_fusion.2), channel_id=1, source_target_pairs={{48,0},{64,16},{80,32},{96,48},{112,64},{128,80},{144,96},{160,112... | collective-permute-start | bytes 1179656 | tf_op jit(solution)/shard_map/ppermute | solution.py:21
  62.1 43.6 %collective-permute-start.4 = (f32[384,1,256]{0,2,1:T(8,128)}, f32[384,1,256]{0,2,1:T(8,128)}, u32[]{:S(2)}, u32[]{:S(2)}) collective-permute-start(f32[384,1,256]{0,2,1:T(8,128)} %pad_maximum_fusion.1), channel_id=1, source_target_pairs={{32,0},{48,16},{64,32},{80,48},{96,64},{112,80},{128,96},{144,112}... | collective-permute-start | bytes 1179656 | tf_op jit(solution)/shard_map/ppermute | solution.py:21
  64.2 41.5 %collective-permute-start.3 = (f32[384,1,256]{0,2,1:T(8,128)}, f32[384,1,256]{0,2,1:T(8,128)}, u32[]{:S(2)}, u32[]{:S(2)}) collective-permute-start(f32[384,1,256]{0,2,1:T(8,128)} %pad_maximum_fusion), channel_id=1, source_target_pairs={{16,0},{32,16},{48,32},{64,48},{80,64},{96,80},{112,96},{128,112},... | collective-permute-start | bytes 1179656 | tf_op jit(solution)/shard_map/ppermute | solution.py:21
  82.2 1.5 %copy-start.6 = (f32[16,1,39936]{2,0,1:T(8,128)}, f32[16,1,39936]{2,0,1:T(8,128)S(1)}, u32[]{:S(2)}) copy-start(f32[16,1,39936]{2,0,1:T(8,128)S(1)} %copy.247) | copy-start | bytes 7667716
  84.7 41.2 %all-to-all-start.1 = ((f32[32,1,3072]{2,1,0:T(1,128)}), f32[32,1,3072]{2,1,0:T(1,128)S(1)}, u32[]{:S(2)}, u32[]{:S(2)}) async-start(f32[32,1,3072]{2,1,0:T(1,128)} %broadcast_in_dim.111), calls=%async_computation.1 | async-start | bytes 786432 | tf_op jit(solution)/shard_map/all_to_all | solution.py:51
  99.2 0.9 copy-start.18
  100.1 1.3 copy-start.5
  100.1 1.0 copy-start.13
  100.1 1.9 %copy-start.4 = (bf16[3,384,384]{1,2,0:T(8,128)(2,1)S(1)}, bf16[3,384,384]{1,2,0:T(8,128)(2,1)}, u32[]{:S(2)}) copy-start(bf16[3,384,384]{1,2,0:T(8,128)(2,1)} %copy-done.3) | copy-start | bytes 2654212
  100.1 1.9 %copy-start.10 = (bf16[384,1,256]{2,0,1:T(8,128)(2,1)S(1)}, bf16[384,1,256]{2,0,1:T(8,128)(2,1)}, u32[]{:S(2)}) copy-start(bf16[384,1,256]{2,0,1:T(8,128)(2,1)} %copy-done.9) | copy-start | bytes 589828
  101.1 1.3 copy-start.2
  101.1 1.3 copy-start.8
  126.9 13.5 %all-to-all-start.2 = ((f32[16,1,3072]{2,1,0:T(1,128)}), f32[16,1,3072]{2,1,0:T(1,128)S(1)}, u32[]{:S(2)}, u32[]{:S(2)}) async-start(f32[16,1,3072]{2,1,0:T(1,128)} %broadcast_in_dim.112), calls=%async_computation.2 | async-start | bytes 393216 | tf_op jit(solution)/shard_map/all_to_all | solution.py:46

commit v6 on v4

--- a/solution.py
+++ b/solution.py
@@ -136,7 +136,26 @@
     seq_index = lax.axis_index("seq")
     ep_size = lax.axis_size("ep")
     gathered = [(key_block, value_block, segments)]
+    moe_rows = moe_grad.shape[0]
+    capacity = moe_rows * TOP // EXPERTS
+    copies = max(1, ep_size // EXPERTS)
+    logits = jnp.einsum("td,ed->te", normed, router, preferred_element_type=jnp.float32)
+    expert_ids = jnp.arange(EXPERTS, dtype=jnp.int32)
+    onehot = (routes[:, :, None] == expert_ids[None, None, :]).astype(jnp.float32)
+    chosen = jnp.sum(onehot * logits[:, None, :], axis=2)
+    first_gate = 1.0 / (1.0 + jnp.exp(chosen[:, 1] - chosen[:, 0]))
+    second_gate = 1.0 - first_gate
+    gate_grad = jnp.einsum("td,tkd->tk", moe_grad, expert_out, preferred_element_type=jnp.float32)
+    logit_step = first_gate * second_gate * (gate_grad[:, 0] - gate_grad[:, 1])
+    logit_grad = (onehot[:, 0, :] - onehot[:, 1, :]) * logit_step[:, None]
+    normed_grad = jnp.dot(
+        logit_grad, router.astype(jnp.float32), precision=lax.Precision.HIGHEST
+    ).astype(jnp.bfloat16)
+    local_router = jnp.dot(
+        logit_grad.T, normed.astype(jnp.float32), precision=lax.Precision.HIGHEST
+    )
     packed = pack_block(key_block, value_block, segments)
+    local_router, packed = lax.optimization_barrier((local_router, packed))
     for offset in range(1, REACH + 1):
         gathered.append(unpack_block(from_behind(packed, "seq", offset), tok_rows, kv_heads))
     stat_shape = (kv_heads, group_size, tok_rows)
@@ -189,24 +208,6 @@
     query_grad = query_total.reshape(tok_rows, -1).astype(jnp.bfloat16)
     key_grad = key_total.reshape(tok_rows, -1).astype(jnp.bfloat16)
     value_grad = value_total.reshape(tok_rows, -1).astype(jnp.bfloat16)
-    moe_rows = moe_grad.shape[0]
-    capacity = moe_rows * TOP // EXPERTS
-    copies = max(1, ep_size // EXPERTS)
-    logits = jnp.einsum("td,ed->te", normed, router, preferred_element_type=jnp.float32)
-    expert_ids = jnp.arange(EXPERTS, dtype=jnp.int32)
-    onehot = (routes[:, :, None] == expert_ids[None, None, :]).astype(jnp.float32)
-    chosen = jnp.sum(onehot * logits[:, None, :], axis=2)
-    first_gate = 1.0 / (1.0 + jnp.exp(chosen[:, 1] - chosen[:, 0]))
-    second_gate = 1.0 - first_gate
-    gate_grad = jnp.einsum("td,tkd->tk", moe_grad, expert_out, preferred_element_type=jnp.float32)
-    logit_step = first_gate * second_gate * (gate_grad[:, 0] - gate_grad[:, 1])
-    logit_grad = (onehot[:, 0, :] - onehot[:, 1, :]) * logit_step[:, None]
-    normed_grad = jnp.dot(
-        logit_grad, router.astype(jnp.float32), precision=lax.Precision.HIGHEST
-    ).astype(jnp.bfloat16)
-    local_router = jnp.dot(
-        logit_grad.T, normed.astype(jnp.float32), precision=lax.Precision.HIGHEST
-    )
     all_tokens = moe_rows * lax.axis_size("seq") * ep_size
     router_grad = sum_everywhere(local_router) / all_tokens
     gates = jnp.stack([first_gate, second_gate], axis=1)

time: 142 us -> 141 us (level)
  other arithmetic: 17.3 us -> 15.7 us
    unnamed x53 -> x61, local copies, waits for them, and re-layouts: 7.32 us -> 8.16 us
  transfers between devices with their start and end apart: 10 -> 10, of which waited for: 3 -> 3; matrix products, arithmetic and copies ran while one was open for 35% -> 32% of each run, Pallas kernels for 0% -> 0%
where the time goes in v6:
time: 141 us; the launch traced here: 140 us
  starting transfers between devices  51.5 us (37%)
  waiting for transfers between devices  30.9 us (22%)
  local copies, waits for them, and re-layouts  21.5 us (15%)
  matrix products  19.3 us (14%)
  other arithmetic  15.7 us (11%)
    ppermute x6, starting transfers between devices, from_behind(): return lax.ppermute(value, axis, pairs)  19 us
    all_to_all x1, waiting for transfers between devices, gather_back(): return lax.all_to_all(copies, axis, 0, 0, tiled=True).reshape(-1)  15 us
    all_to_all x1, starting transfers between devices, broadcast_sum(): return lax.all_to_all(copies, axis, 0, 0, tiled=True).sum(axis=0)  13.7 us
    all_to_all x1, waiting for transfers between devices, on_device(): lax.all_to_all(outgoing, 'ep', split_axis=0, concat_axis=0, tiled=True)  12.8 us
    unnamed x61, local copies, waits for them, and re-layouts  8.16 us
    all_to_all x1, starting transfers between devices, scatter_sum(): return lax.all_to_all(parts, axis, 0, 0, tiled=True).sum(axis=0)  6.84 us
    all_to_all x1, starting transfers between devices, gather_back(): return lax.all_to_all(copies, axis, 0, 0, tiled=True).reshape(-1)  6.69 us
    all_to_all x1, starting transfers between devices, on_device(): lax.all_to_all(outgoing, 'ep', split_axis=0, concat_axis=0, tiled=True)  5.25 us
  transfers between devices with their start and end apart: 10, of which 3 were waited for; matrix products, arithmetic and copies ran while one was open for 32% of the time, Pallas kernels for 0%

profile of v6, /device:TPU:1, one launch (start us, length us, event | category | flops | bytes accessed | tf_op | source)
XLA Modules:
  0.0 140.0 jit_solution(3787815649613972065)
XLA Ops:
  0.6 0.7 fusion.79
  1.8 2.4 %fusion.54 = f32[24,1,2]{2,1,0:T(1,128)S(1)} fusion(bf16[24,2,6144]{2,1,0:T(2,128)(2,1)S(1)} %copy-done, bf16[24,6144,1]{1,0,2:T(8,128)(2,1)} %bitcast.374), kind=kOutput, calls=%fused_computation.89 | convolution fusion | flops 589824 | bytes 884928 | tf_op jit(solution)/shard_map/td,tkd->tk/dot_general | solution.py:148
  5.9 0.7 fusion.61
  6.6 7.7 %collective-permute-start.2 = (bf16[392,256]{1,0:T(8,128)(2,1)}, bf16[392,256]{1,0:T(8,128)(2,1)}, u32[]{:S(2)}, u32[]{:S(2)}) collective-permute-start(bf16[392,256]{1,0:T(8,128)(2,1)} %fusion.61), channel_id=1, source_target_pairs={{0,48},{16,64},{32,80},{48,96},{64,112},{80,128},{96,144},{112,160... | collective-permute-start | bytes 602120 | tf_op jit(solution)/shard_map/ppermute | solution.py:21
  14.3 4.2 %collective-permute-start.1 = (bf16[392,256]{1,0:T(8,128)(2,1)}, bf16[392,256]{1,0:T(8,128)(2,1)}, u32[]{:S(2)}, u32[]{:S(2)}) collective-permute-start(bf16[392,256]{1,0:T(8,128)(2,1)} %fusion.61), channel_id=1, source_target_pairs={{0,32},{16,48},{32,64},{48,80},{64,96},{80,112},{96,128},{112,144}... | collective-permute-start | bytes 602120 | tf_op jit(solution)/shard_map/ppermute | solution.py:21
  18.5 3.3 %collective-permute-start = (bf16[392,256]{1,0:T(8,128)(2,1)}, bf16[392,256]{1,0:T(8,128)(2,1)}, u32[]{:S(2)}, u32[]{:S(2)}) collective-permute-start(bf16[392,256]{1,0:T(8,128)(2,1)} %fusion.61), channel_id=1, source_target_pairs={{0,16},{16,32},{32,48},{48,64},{64,80},{80,96},{96,112},{112,128},... | collective-permute-start | bytes 602120 | tf_op jit(solution)/shard_map/ppermute | solution.py:21
  21.8 0.9 all_to_all.22
  22.8 6.8 %all-to-all-start = ((f32[16,1,3072]{2,1,0:T(1,128)}), f32[16,1,3072]{2,1,0:T(1,128)}, u32[]{:S(2)}, u32[]{:S(2)}) async-start(f32[16,1,3072]{2,1,0:T(1,128)} %all_to_all.22), calls=%async_computation | async-start | bytes 393216 | tf_op jit(solution)/shard_map/all_to_all | solution.py:41
  30.7 0.8 mul.337
  31.5 0.7 pad_maximum_fusion.3
  32.8 2.0 %sort.17 = (s32[48]{0:T(128)}, s32[48]{0:T(128)S(1)}) sort(s32[48]{0:T(128)S(1)} %multiply_add_fusion.1, s32[48]{0:T(128)S(1)} %iota.37), dimensions={0}, to_apply=%region_17.18 | sort | flops 288 | bytes 768 | tf_op jit(solution)/shard_map/jit(argsort)/sort | solution.py:220
  35.0 0.9 gather_fusion
  36.0 1.1 reshape.494
  37.1 1.2 convolution_convert_fusion
  38.2 1.1 reduce_sum.117
  39.3 0.9 broadcast_in_dim.109
  40.2 13.7 %all-to-all-start.1 = ((f32[32,1,3072]{2,1,0:T(1,128)}), f32[32,1,3072]{2,1,0:T(1,128)S(1)}, u32[]{:S(2)}, u32[]{:S(2)}) async-start(f32[32,1,3072]{2,1,0:T(1,128)} %broadcast_in_dim.109), calls=%async_computation.1 | async-start | bytes 786432 | tf_op jit(solution)/shard_map/all_to_all | solution.py:51
  54.6 0.7 fusion.82
  56.0 0.8 and_and_fusion.2
  57.2 0.9 slice_bitcast_fusion
  58.7 0.9 slice_bitcast_fusion.1
  60.1 0.9 slice_bitcast_fusion.2
  62.0 0.7 fusion.5
  65.1 1.3 fusion.42
  68.7 0.8 pad_maximum_fusion.2
  69.5 1.3 collective-permute-start.5
  70.8 0.8 pad_maximum_fusion.1
  71.5 1.3 collective-permute-start.4
  72.8 0.8 pad_maximum_fusion
  73.6 1.3 collective-permute-start.3
  75.5 1.2 copy-done.4
  77.1 3.0 %all-to-all-done.1 = f32[32,1,3072]{2,1,0:T(1,128)S(1)} async-done(((f32[32,1,3072]{2,1,0:T(1,128)}), f32[32,1,3072]{2,1,0:T(1,128)S(1)}, u32[]{:S(2)}, u32[]{:S(2)}) %all-to-all-start.1) | async-done | bytes 393248 | tf_op jit(solution)/shard_map/all_to_all | solution.py:51
  80.3 0.8 broadcast_in_dim.110
  81.1 6.7 %all-to-all-start.2 = ((f32[16,1,3072]{2,1,0:T(1,128)}), f32[16,1,3072]{2,1,0:T(1,128)}, u32[]{:S(2)}, u32[]{:S(2)}) async-start(f32[16,1,3072]{2,1,0:T(1,128)} %broadcast_in_dim.110), calls=%async_computation.2 | async-start | bytes 393216 | tf_op jit(solution)/shard_map/all_to_all | solution.py:46
  87.8 1.2 fusion.70
  89.0 15.0 %all-to-all-done.2 = f32[16,1,3072]{2,1,0:T(1,128)} async-done(((f32[16,1,3072]{2,1,0:T(1,128)}), f32[16,1,3072]{2,1,0:T(1,128)}, u32[]{:S(2)}, u32[]{:S(2)}) %all-to-all-start.2) | async-done | bytes 196640 | tf_op jit(solution)/shard_map/all_to_all | solution.py:46
  104.1 2.2 %multiply_reduce_fusion = f32[16,3072]{1,0:T(8,128)} fusion(f32[16,1,3072]{2,1,0:T(1,128)} %all-to-all-done.2), kind=kLoop, calls=%fused_computation.113 | loop fusion | flops 49152 | bytes 393216 | tf_op jit(solution)/shard_map/div | solution.py:212
  106.2 1.7 %div.27 = f32[8,6144]{1,0:T(8,128)} reshape(f32[16,3072]{1,0:T(8,128)} %multiply_reduce_fusion) | data formatting | bytes 393216 | tf_op jit(solution)/shard_map/div | solution.py:212
  107.9 2.5 %broadcast_in_dim.112 = bf16[8,2,6,6144]{3,2,1,0:T(8,128)(2,1)} broadcast(bf16[8,6,6144]{2,1,0:T(8,128)(2,1)} %reshape.494), dimensions={0,2,3} | broadcast | bytes 1769472 | tf_op jit(solution)/shard_map/broadcast_in_dim | solution.py:222
  110.4 5.2 %all-to-all-start.3 = ((bf16[16,6,6144]{2,1,0:T(8,128)(2,1)}), bf16[16,6,6144]{2,1,0:T(8,128)(2,1)}, u32[]{:S(2)}, u32[]{:S(2)}) async-start(bf16[16,6,6144]{2,1,0:T(8,128)(2,1)} %bitcast.367), calls=%async_computation.3 | async-start | bytes 3145728 | tf_op jit(solution)/shard_map/all_to_all | solution.py:224
  115.6 1.7 %convolution_add_fusion.2 = f32[128,3,384]{2,0,1:T(8,128)S(1)} fusion(f32[128,3,384]{2,0,1:T(8,128)S(1)} %fusion.70, bf16[3,384,384]{1,2,0:T(8,128)(2,1)} %copy-done.3, bf16[384,1,256]{2,0,1:T(8,128)(2,1)} %copy-done.9), kind=kOutput, calls=%fused_computation.47 | convolution fusion | flops 113393664 | bytes 2162688 | tf_op jit(solution)/shard_map/hgqt,thd->qhgd/dot_general | solution.py:106
  118.1 0.9 copy.204
  119.0 1.5 %fusion.64 = bf16[384,128]{0,1:T(8,128)(2,1)S(1)} fusion(f32[384,1,256]{0,2,1:T(8,128)} %collective-permute-done.5, f32[384,1,256]{0,2,1:T(8,128)} %collective-permute-done.4, f32[384,1,256]{0,2,1:T(8,128)} %collective-permute-done.3, bf16[3,384,384]{1,2,0:T(8,128)(2,1)S(1)} %fusion.22, bf16[384,1,3,128]{0,3,2,1:T(8,128)(2,1)S(1)} %bitcast.357), kind=kOutput, calls=%fused_computation.114 | convolution fusion | flops 113491968 | bytes 1867776 | tf_op jit(solution)/shard_map/hgqt,qhgd->thd/dot_general | solution.py:110
  120.5 0.8 copy.205
  121.3 2.0 %fusion.65 = bf16[384,128]{0,1:T(8,128)(2,1)S(1)} fusion(f32[384,1,256]{0,2,1:T(8,128)} %collective-permute-done.5, f32[384,1,256]{0,2,1:T(8,128)} %collective-permute-done.4, f32[384,1,256]{0,2,1:T(8,128)} %collective-permute-done.3, f32[1,3,384,384]{2,3,1,0:T(8,128)} %copy-done.4, bf16[384,1,3,128]{0,3,2,1:T(8,128)(2,1)S(1)} %bitcast.366), kind=kOutput, calls=%fused_computation.115 | convolution fusion | flops 113885184 | bytes 2752512 | tf_op jit(solution)/shard_map/hgqt,qhgd->thd/dot_general | solution.py:98
  123.3 0.8 copy.206
  124.1 12.8 %all-to-all-done.3 = bf16[16,6,6144]{2,1,0:T(8,128)(2,1)} async-done(((bf16[16,6,6144]{2,1,0:T(8,128)(2,1)}), bf16[16,6,6144]{2,1,0:T(8,128)(2,1)}, u32[]{:S(2)}, u32[]{:S(2)}) %all-to-all-start.3) | async-done | bytes 1179680 | tf_op jit(solution)/shard_map/all_to_all | solution.py:224
  136.9 3.1 %copy.207 = bf16[16,6,6144]{2,0,1:T(8,128)(2,1)} copy(bf16[16,6,6144]{2,1,0:T(8,128)(2,1)} %all-to-all-done.3) | data formatting | bytes 2359296
  (109 shorter events, 14.1 us)
Async XLA Ops:
  0.6 1.1 copy-start
  1.4 4.2 %copy-start.20 = (f32[24,2,8]{0,2,1:T(8,128)}, f32[24,2,8]{0,2,1:T(8,128)S(1)}, u32[]{:S(2)}) copy-start(f32[24,2,8]{0,2,1:T(8,128)S(1)} %fusion.79) | copy-start | bytes 4612
  1.7 2.6 %copy-start.10 = (bf16[24,6144]{1,0:T(8,128)(2,1)S(1)}, bf16[24,6144]{1,0:T(8,128)(2,1)}, u32[]{:S(2)}) copy-start(bf16[24,6144]{1,0:T(8,128)(2,1)} %param.17) | copy-start | bytes 884740
  1.7 2.6 %copy-start.13 = (bf16[8,6144]{1,0:T(8,128)(2,1)S(1)}, bf16[8,6144]{1,0:T(8,128)(2,1)}, u32[]{:S(2)}) copy-start(bf16[8,6144]{1,0:T(8,128)(2,1)} %param.18) | copy-start | bytes 294916
  1.7 2.8 %copy-start.23 = (s32[24,2]{0,1:T(2,128)S(1)}, s32[24,2]{0,1:T(2,128)}, u32[]{:S(2)}) copy-start(s32[24,2]{0,1:T(2,128)} %param.19) | copy-start | bytes 580
  1.7 3.3 %copy-start.22 = (s32[384]{0:T(512)S(1)}, s32[384]{0:T(512)}, u32[]{:S(2)}) copy-start(s32[384]{0:T(512)} %param.14) | copy-start | bytes 4612
  1.7 4.1 %copy-start.11 = (bf16[384,128]{1,0:T(8,128)(2,1)S(1)}, bf16[384,128]{1,0:T(8,128)(2,1)}, u32[]{:S(2)}) copy-start(bf16[384,128]{1,0:T(8,128)(2,1)} %param.11) | copy-start | bytes 294916
  1.7 4.1 %copy-start.15 = (bf16[384,128]{1,0:T(8,128)(2,1)S(1)}, bf16[384,128]{1,0:T(8,128)(2,1)}, u32[]{:S(2)}) copy-start(bf16[384,128]{1,0:T(8,128)(2,1)} %param.12) | copy-start | bytes 294916
  4.2 25.5 %copy-start.17 = (bf16[384,384]{1,0:T(8,128)(2,1)S(1)}, bf16[384,384]{1,0:T(8,128)(2,1)}, u32[]{:S(2)}) copy-start(bf16[384,384]{1,0:T(8,128)(2,1)} %param.10) | copy-start | bytes 884740
  4.2 25.7 %copy-start.18 = (bf16[384,384]{1,0:T(8,128)(2,1)S(1)}, bf16[384,384]{1,0:T(8,128)(2,1)}, u32[]{:S(2)}) copy-start(bf16[384,384]{1,0:T(8,128)(2,1)} %param.13) | copy-start | bytes 884740
  4.3 25.9 %copy-start.19 = (bf16[24,6144]{1,0:T(8,128)(2,1)S(1)}, bf16[24,6144]{1,0:T(8,128)(2,1)}, u32[]{:S(2)}) copy-start(bf16[24,6144]{1,0:T(8,128)(2,1)} %param.15) | copy-start | bytes 884740
  5.1 0.5 copy-start.26
  5.6 24.5 %copy-start.24 = (f32[24]{0:T(128)}, f32[24]{0:T(128)S(1)}, u32[]{:S(2)}) copy-start(f32[24]{0:T(128)S(1)} %multiply_bitcast_fusion) | copy-start | bytes 292
  6.6 48.0 %collective-permute-start.2 = (bf16[392,256]{1,0:T(8,128)(2,1)}, bf16[392,256]{1,0:T(8,128)(2,1)}, u32[]{:S(2)}, u32[]{:S(2)}) collective-permute-start(bf16[392,256]{1,0:T(8,128)(2,1)} %fusion.61), channel_id=1, source_target_pairs={{0,48},{16,64},{32,80},{48,96},{64,112},{80,128},{96,144},{112,160... | collective-permute-start | bytes 602120 | tf_op jit(solution)/shard_map/ppermute | solution.py:21
  14.3 39.7 %collective-permute-start.1 = (bf16[392,256]{1,0:T(8,128)(2,1)}, bf16[392,256]{1,0:T(8,128)(2,1)}, u32[]{:S(2)}, u32[]{:S(2)}) collective-permute-start(bf16[392,256]{1,0:T(8,128)(2,1)} %fusion.61), channel_id=1, source_target_pairs={{0,32},{16,48},{32,64},{48,80},{64,96},{80,112},{96,128},{112,144}... | collective-permute-start | bytes 602120 | tf_op jit(solution)/shard_map/ppermute | solution.py:21
  18.5 36.8 %collective-permute-start = (bf16[392,256]{1,0:T(8,128)(2,1)}, bf16[392,256]{1,0:T(8,128)(2,1)}, u32[]{:S(2)}, u32[]{:S(2)}) collective-permute-start(bf16[392,256]{1,0:T(8,128)(2,1)} %fusion.61), channel_id=1, source_target_pairs={{0,16},{16,32},{32,48},{48,64},{64,80},{80,96},{96,112},{112,128},... | collective-permute-start | bytes 602120 | tf_op jit(solution)/shard_map/ppermute | solution.py:21
  22.8 15.5 %all-to-all-start = ((f32[16,1,3072]{2,1,0:T(1,128)}), f32[16,1,3072]{2,1,0:T(1,128)}, u32[]{:S(2)}, u32[]{:S(2)}) async-start(f32[16,1,3072]{2,1,0:T(1,128)} %all_to_all.22), calls=%async_computation | async-start | bytes 393216 | tf_op jit(solution)/shard_map/all_to_all | solution.py:41
  35.0 2.1 %copy-start.14 = (bf16[8,6144]{1,0:T(8,128)(2,1)S(1)}, bf16[8,6144]{1,0:T(8,128)(2,1)}, u32[]{:S(2)}) copy-start(bf16[8,6144]{1,0:T(8,128)(2,1)} %param.18) | copy-start | bytes 294916
  35.0 2.1 %copy-start.21 = (f32[24,2,8]{0,2,1:T(8,128)S(1)}, f32[24,2,8]{0,2,1:T(8,128)}, u32[]{:S(2)}) copy-start(f32[24,2,8]{0,2,1:T(8,128)} %copy-done.20) | copy-start | bytes 4612
  35.0 2.1 %copy-start.25 = (f32[24]{0:T(128)S(1)}, f32[24]{0:T(128)}, u32[]{:S(2)}) copy-start(f32[24]{0:T(128)} %copy-done.24) | copy-start | bytes 292
  35.9 20.8 %copy-start.12 = (bf16[384,128]{1,0:T(8,128)(2,1)S(1)}, bf16[384,128]{1,0:T(8,128)(2,1)}, u32[]{:S(2)}) copy-start(bf16[384,128]{1,0:T(8,128)(2,1)} %param.11) | copy-start | bytes 294916
  40.2 39.8 %all-to-all-start.1 = ((f32[32,1,3072]{2,1,0:T(1,128)}), f32[32,1,3072]{2,1,0:T(1,128)S(1)}, u32[]{:S(2)}, u32[]{:S(2)}) async-start(f32[32,1,3072]{2,1,0:T(1,128)} %broadcast_in_dim.109), calls=%async_computation.1 | async-start | bytes 786432 | tf_op jit(solution)/shard_map/all_to_all | solution.py:51
  58.2 4.5 %copy-start.5 = (bf16[384,1,256]{2,0,1:T(8,128)(2,1)}, bf16[384,1,256]{2,0,1:T(8,128)(2,1)S(1)}, u32[]{:S(2)}) copy-start(bf16[384,1,256]{2,0,1:T(8,128)(2,1)S(1)} %slice_bitcast_fusion) | copy-start | bytes 589828
  59.6 3.7 %copy-start.7 = (bf16[384,1,256]{2,0,1:T(8,128)(2,1)}, bf16[384,1,256]{2,0,1:T(8,128)(2,1)S(1)}, u32[]{:S(2)}) copy-start(bf16[384,1,256]{2,0,1:T(8,128)(2,1)S(1)} %slice_bitcast_fusion.1) | copy-start | bytes 589828
  61.0 3.0 %copy-start.9 = (bf16[384,1,256]{2,0,1:T(8,128)(2,1)}, bf16[384,1,256]{2,0,1:T(8,128)(2,1)S(1)}, u32[]{:S(2)}) copy-start(bf16[384,1,256]{2,0,1:T(8,128)(2,1)S(1)} %slice_bitcast_fusion.2) | copy-start | bytes 589828
  61.1 1.0 copy-start.16
  66.5 1.3 copy-start.1
  66.5 1.3 copy-start.3
  69.5 49.5 %collective-permute-start.5 = (f32[384,1,256]{0,2,1:T(8,128)}, f32[384,1,256]{0,2,1:T(8,128)}, u32[]{:S(2)}, u32[]{:S(2)}) collective-permute-start(f32[384,1,256]{0,2,1:T(8,128)} %pad_maximum_fusion.2), channel_id=1, source_target_pairs={{48,0},{64,16},{80,32},{96,48},{112,64},{128,80},{144,96},{160,112... | collective-permute-start | bytes 1179656 | tf_op jit(solution)/shard_map/ppermute | solution.py:21
  71.5 47.5 %collective-permute-start.4 = (f32[384,1,256]{0,2,1:T(8,128)}, f32[384,1,256]{0,2,1:T(8,128)}, u32[]{:S(2)}, u32[]{:S(2)}) collective-permute-start(f32[384,1,256]{0,2,1:T(8,128)} %pad_maximum_fusion.1), channel_id=1, source_target_pairs={{32,0},{48,16},{64,32},{80,48},{96,64},{112,80},{128,96},{144,112}... | collective-permute-start | bytes 1179656 | tf_op jit(solution)/shard_map/ppermute | solution.py:21
  73.6 45.4 %collective-permute-start.3 = (f32[384,1,256]{0,2,1:T(8,128)}, f32[384,1,256]{0,2,1:T(8,128)}, u32[]{:S(2)}, u32[]{:S(2)}) collective-permute-start(f32[384,1,256]{0,2,1:T(8,128)} %pad_maximum_fusion), channel_id=1, source_target_pairs={{16,0},{32,16},{48,32},{64,48},{80,64},{96,80},{112,96},{128,112},... | collective-permute-start | bytes 1179656 | tf_op jit(solution)/shard_map/ppermute | solution.py:21
  75.5 1.2 copy-start.4
  81.1 23.0 %all-to-all-start.2 = ((f32[16,1,3072]{2,1,0:T(1,128)}), f32[16,1,3072]{2,1,0:T(1,128)}, u32[]{:S(2)}, u32[]{:S(2)}) async-start(f32[16,1,3072]{2,1,0:T(1,128)} %broadcast_in_dim.110), calls=%async_computation.2 | async-start | bytes 393216 | tf_op jit(solution)/shard_map/all_to_all | solution.py:46
  110.4 26.5 %all-to-all-start.3 = ((bf16[16,6,6144]{2,1,0:T(8,128)(2,1)}), bf16[16,6,6144]{2,1,0:T(8,128)(2,1)}, u32[]{:S(2)}, u32[]{:S(2)}) async-start(bf16[16,6,6144]{2,1,0:T(8,128)(2,1)} %bitcast.367), calls=%async_computation.3 | async-start | bytes 3145728 | tf_op jit(solution)/shard_map/all_to_all | solution.py:224
  115.6 1.7 %copy-start.2 = (bf16[3,384,384]{1,2,0:T(8,128)(2,1)S(1)}, bf16[3,384,384]{1,2,0:T(8,128)(2,1)}, u32[]{:S(2)}) copy-start(bf16[3,384,384]{1,2,0:T(8,128)(2,1)} %copy-done.1) | copy-start | bytes 2654212
  115.6 1.7 %copy-start.8 = (bf16[384,1,256]{2,0,1:T(8,128)(2,1)S(1)}, bf16[384,1,256]{2,0,1:T(8,128)(2,1)}, u32[]{:S(2)}) copy-start(bf16[384,1,256]{2,0,1:T(8,128)(2,1)} %copy-done.7) | copy-start | bytes 589828
  115.6 2.1 %copy-start.6 = (bf16[384,1,256]{2,0,1:T(8,128)(2,1)S(1)}, bf16[384,1,256]{2,0,1:T(8,128)(2,1)}, u32[]{:S(2)}) copy-start(bf16[384,1,256]{2,0,1:T(8,128)(2,1)} %copy-done.5) | copy-start | bytes 589828

commit v7 on v6

--- a/solution.py
+++ b/solution.py
@@ -209,7 +209,7 @@
     key_grad = key_total.reshape(tok_rows, -1).astype(jnp.bfloat16)
     value_grad = value_total.reshape(tok_rows, -1).astype(jnp.bfloat16)
     all_tokens = moe_rows * lax.axis_size("seq") * ep_size
-    router_grad = sum_everywhere(local_router) / all_tokens
+    router_flat = broadcast_sum(scatter_sum(local_router.reshape(-1), "ep"), "seq")
     gates = jnp.stack([first_gate, second_gate], axis=1)
     expert_rows = (gates[:, :, None] * moe_grad.astype(jnp.float32)[:, None, :]).astype(
         jnp.bfloat16
@@ -220,8 +220,18 @@
     order = jnp.argsort(flat_routes * capacity + ranks)
     outgoing = expert_rows.reshape(-1, expert_rows.shape[2])[order]
     outgoing = jnp.repeat(outgoing.reshape(EXPERTS, capacity, -1), copies, axis=0)
-    router_grad, outgoing = lax.optimization_barrier((router_grad, outgoing))
-    routed_grads = lax.all_to_all(outgoing, "ep", split_axis=0, concat_axis=0, tiled=True)
+    slots = outgoing.shape[0]
+    merged = jnp.concatenate(
+        [
+            outgoing.reshape(slots, -1).astype(jnp.float32),
+            jnp.broadcast_to(router_flat[None], (slots,) + router_flat.shape),
+        ],
+        axis=1,
+    )
+    merged = lax.all_to_all(merged, "ep", split_axis=0, concat_axis=0, tiled=True)
+    split_at = merged.shape[1] - router_flat.shape[0]
+    routed_grads = merged[:, :split_at].reshape(outgoing.shape).astype(jnp.bfloat16)
+    router_grad = merged[:, split_at:].reshape(local_router.shape) / all_tokens
     return (query_grad, key_grad, value_grad, normed_grad, router_grad, routed_grads)
 
 

time: 141 us -> 155 us (1.099)
  waiting for transfers between devices: 30.9 us -> 42.7 us
  starting transfers between devices: 51.5 us -> 46.9 us
  other arithmetic: 15.7 us -> 18.2 us
  matrix products: 19.3 us -> 21.7 us
  local copies, waits for them, and re-layouts: 21.5 us -> 23.4 us
    ppermute x6, waiting for transfers between devices: 0.02 us -> 37.1 us  [from_behind(): return lax.ppermute(value, axis, pairs)]
    all_to_all x2 -> x1, waiting for transfers between devices: 27.9 us -> 0.01 us  [on_device(): lax.all_to_all(merged, 'ep', split_axis=0, concat_axis=0, tiled=True)]
    all_to_all x2 -> x1, starting transfers between devices: 11.9 us -> 6.81 us  [on_device(): lax.all_to_all(merged, 'ep', split_axis=0, concat_axis=0, tiled=True)]
    all_to_all x0 -> x1, local copies, waits for them, and re-layouts: none -> 4.13 us  [on_device(): lax.all_to_all(merged, 'ep', split_axis=0, concat_axis=0, tiled=True)]
    all_to_all x1, waiting for transfers between devices: 2.96 us -> 5.57 us  [broadcast_sum(): return lax.all_to_all(copies, axis, 0, 0, tiled=True).sum(axis=0)]
    dot_general x4, matrix products: 3.65 us -> 1.45 us  [block_grads(): jnp.einsum('hgqt,thd->qhgd', score_low, key_block, preferred_element_type...]
    broadcast_in_dim x1, local copies, waits for them, and re-layouts: 2.46 us -> 0.3 us  [on_device(): jnp.repeat(outgoing.reshape(EXPERTS, capacity, -1), copies, axis=0)]
    div x1, other arithmetic: 2.16 us -> 0.02 us  [on_device(): router_grad = merged[:, split_at:].reshape(local_router.shape) / all_tokens]
  transfers between devices with their start and end apart: 10 -> 9, of which waited for: 3 -> 3; matrix products, arithmetic and copies ran while one was open for 32% -> 28% of each run, Pallas kernels for 0% -> 0%
where the time goes in v7:
time: 155 us; the launch traced here: 154 us
  starting transfers between devices  46.9 us (30%)
  waiting for transfers between devices  42.7 us (28%)
  local copies, waits for them, and re-layouts  23.4 us (15%)
  matrix products  21.7 us (14%)
  other arithmetic  18.2 us (12%)
    ppermute x6, waiting for transfers between devices, from_behind(): return lax.ppermute(value, axis, pairs)  37.1 us
    ppermute x6, starting transfers between devices, from_behind(): return lax.ppermute(value, axis, pairs)  19.4 us
    all_to_all x1, starting transfers between devices, broadcast_sum(): return lax.all_to_all(copies, axis, 0, 0, tiled=True).sum(axis=0)  13.8 us
    unnamed x84, local copies, waits for them, and re-layouts  8.79 us
    all_to_all x1, starting transfers between devices, scatter_sum(): return lax.all_to_all(parts, axis, 0, 0, tiled=True).sum(axis=0)  6.84 us
    all_to_all x1, starting transfers between devices, on_device(): lax.all_to_all(merged, 'ep', split_axis=0, concat_axis=0, tiled=True)  6.81 us
    all_to_all x1, waiting for transfers between devices, broadcast_sum(): return lax.all_to_all(copies, axis, 0, 0, tiled=True).sum(axis=0)  5.57 us
    dot_general x4, matrix products, block_grads(): jnp.einsum('hgqt,qhgd->thd', probs_low, grad_rows, preferred_element_type...  5.45 us
  transfers between devices with their start and end apart: 9, of which 3 were waited for; matrix products, arithmetic and copies ran while one was open for 28% of the time, Pallas kernels for 0%

profile of v7, /device:TPU:1, one launch (start us, length us, event | category | flops | bytes accessed | tf_op | source)
XLA Modules:
  0.0 154.1 jit_solution(17313247691142877272)
XLA Ops:
  0.6 0.7 fusion.79
  1.8 2.4 %fusion.54 = f32[24,1,2]{2,1,0:T(1,128)S(1)} fusion(bf16[24,2,6144]{2,1,0:T(2,128)(2,1)S(1)} %copy-done, bf16[24,6144,1]{1,0,2:T(8,128)(2,1)} %bitcast.390), kind=kOutput, calls=%fused_computation.93 | convolution fusion | flops 589824 | bytes 884928 | tf_op jit(solution)/shard_map/td,tkd->tk/dot_general | solution.py:148
  5.9 0.7 fusion.61
  6.6 7.7 %collective-permute-start.2 = (bf16[392,256]{1,0:T(8,128)(2,1)}, bf16[392,256]{1,0:T(8,128)(2,1)}, u32[]{:S(2)}, u32[]{:S(2)}) collective-permute-start(bf16[392,256]{1,0:T(8,128)(2,1)} %fusion.61), channel_id=1, source_target_pairs={{0,48},{16,64},{32,80},{48,96},{64,112},{80,128},{96,144},{112,160... | collective-permute-start | bytes 602120 | tf_op jit(solution)/shard_map/ppermute | solution.py:21
  14.3 4.2 %collective-permute-start.1 = (bf16[392,256]{1,0:T(8,128)(2,1)}, bf16[392,256]{1,0:T(8,128)(2,1)}, u32[]{:S(2)}, u32[]{:S(2)}) collective-permute-start(bf16[392,256]{1,0:T(8,128)(2,1)} %fusion.61), channel_id=1, source_target_pairs={{0,32},{16,48},{32,64},{48,80},{64,96},{80,112},{96,128},{112,144}... | collective-permute-start | bytes 602120 | tf_op jit(solution)/shard_map/ppermute | solution.py:21
  18.5 3.3 %collective-permute-start = (bf16[392,256]{1,0:T(8,128)(2,1)}, bf16[392,256]{1,0:T(8,128)(2,1)}, u32[]{:S(2)}, u32[]{:S(2)}) collective-permute-start(bf16[392,256]{1,0:T(8,128)(2,1)} %fusion.61), channel_id=1, source_target_pairs={{0,16},{16,32},{32,48},{48,64},{64,80},{80,96},{96,112},{112,128},... | collective-permute-start | bytes 602120 | tf_op jit(solution)/shard_map/ppermute | solution.py:21
  21.8 0.9 all_to_all.24
  22.8 6.8 %all-to-all-start = ((f32[16,1,3072]{2,1,0:T(1,128)}), f32[16,1,3072]{2,1,0:T(1,128)}, u32[]{:S(2)}, u32[]{:S(2)}) async-start(f32[16,1,3072]{2,1,0:T(1,128)} %all_to_all.24), calls=%async_computation | async-start | bytes 393216 | tf_op jit(solution)/shard_map/all_to_all | solution.py:41
  30.7 0.8 mul.337
  32.8 2.0 %sort.17 = (s32[48]{0:T(128)}, s32[48]{0:T(128)S(1)}) sort(s32[48]{0:T(128)S(1)} %multiply_add_fusion.1, s32[48]{0:T(128)S(1)} %iota.37), dimensions={0}, to_apply=%region_15.16 | sort | flops 288 | bytes 768 | tf_op jit(solution)/shard_map/jit(argsort)/sort | solution.py:220
  35.0 0.9 gather_fusion
  36.4 1.4 copy.245
  39.0 1.2 convolution_convert_fusion
  40.1 1.1 reduce_sum.118
  41.2 1.0 broadcast_in_dim.111
  42.2 13.8 %all-to-all-start.1 = ((f32[32,1,3072]{2,1,0:T(1,128)}), f32[32,1,3072]{2,1,0:T(1,128)}, u32[]{:S(2)}, u32[]{:S(2)}) async-start(f32[32,1,3072]{2,1,0:T(1,128)} %broadcast_in_dim.111), calls=%async_computation.1 | async-start | bytes 786432 | tf_op jit(solution)/shard_map/all_to_all | solution.py:51
  58.0 1.6 %and_and_fusion.2 = (pred[384,384]{0,1:T(8,128)(4,1)S(1)}, pred[384,384]{0,1:T(8,128)(4,1)S(1)}, pred[384,384]{0,1:T(8,128)(4,1)S(1)}, pred[384,384]{0,1:T(8,128)(4,1)S(1)}) fusion(s32[384]{0:T(512)} %get-tuple-element.84, s32[384]{0:T(512)S(1)} %copy-done.33, pred[]{:T(512)S(6)} %ge.13, pred[]{:T(512)S(6)} %ge.14, s32[384]{0:T(512)} %get-tuple-element.83, ...), kind=kLoop, calls=%fused_computation.91 | loop fusion | flops 2359296 | bytes 602116 | tf_op jit(solution)/shard_map/and | solution.py:65
  59.6 1.4 fusion.15
  61.0 0.9 slice_bitcast_fusion
  62.4 0.9 slice_bitcast_fusion.1
  63.9 0.9 slice_bitcast_fusion.2
  68.5 2.2 %fusion.42 = (bf16[3,384,384]{1,2,0:T(8,128)(2,1)}, bf16[3,384,384]{1,2,0:T(8,128)(2,1)S(1)}, bf16[3,384,384]{1,2,0:T(8,128)(2,1)S(1)}) fusion(f32[384,384,3]{1,0,2:T(8,128)S(1)} %get-tuple-element.79, f32[1,3,384,384]{2,3,1,0:T(8,128)S(1)} %get-tuple-element.72, f32[3,384]{1,0:T(4,128)S(1)} %get-tuple-element.58, f32[3,384]{1,0:T(4,128)S(1)} %log_add_fusion, ...), kind=kLoop, calls=%fused_computation.77 | loop fusion | flops 6635520 | bytes 13722624 | tf_op jit(solution)/shard_map/reshape.71
  70.7 1.4 fusion.30
  72.0 1.1 fusion.31
  73.1 1.1 convolution_bitcast_fusion.6
  74.2 1.2 convolution_bitcast_fusion.4
  75.4 1.1 convolution_bitcast_fusion.2
  76.5 5.6 %all-to-all-done.1 = f32[32,1,3072]{2,1,0:T(1,128)} async-done(((f32[32,1,3072]{2,1,0:T(1,128)}), f32[32,1,3072]{2,1,0:T(1,128)}, u32[]{:S(2)}, u32[]{:S(2)}) %all-to-all-start.1) | async-done | bytes 393248 | tf_op jit(solution)/shard_map/all_to_all | solution.py:51
  82.1 1.8 %reduce_sum.119 = f32[3072]{0:T(1024)} reduce(f32[32,1,3072]{2,1,0:T(1,128)} %all-to-all-done.1, f32[]{:T(128)} %constant.17.clone.1), dimensions={0,1}, to_apply=%region_17.18 | reduce | flops 95232 | bytes 405508 | tf_op jit(solution)/shard_map/reduce_sum | solution.py:51
  83.9 0.7 pad.6.clone
  84.9 4.1 %copy.205 = f32[16,1,39936]{2,1,0:T(1,128)} copy(f32[16,1,39936]{2,0,1:T(8,128)S(1)} %maximum_bitcast_fusion) | data formatting | bytes 5111808 | tf_op jit(solution)/shard_map/all_to_all | solution.py:231
  89.0 6.8 %all-to-all-start.2 = ((f32[16,1,39936]{2,1,0:T(1,128)}), f32[16,1,39936]{2,1,0:T(1,128)}, u32[]{:S(2)}, u32[]{:S(2)}) async-start(f32[16,1,39936]{2,1,0:T(1,128)} %copy.205), calls=%async_computation.2 | async-start | bytes 5111808 | tf_op jit(solution)/shard_map/all_to_all | solution.py:231
  96.3 0.8 pad_maximum_fusion.2
  97.1 1.5 collective-permute-start.5
  98.6 0.8 pad_maximum_fusion.1
  99.4 1.3 collective-permute-start.4
  100.7 0.8 pad_maximum_fusion
  101.5 1.4 collective-permute-start.3
  106.8 0.9 copy.206
  107.7 12.8 %collective-permute-done.5 = f32[384,1,256]{0,2,1:T(8,128)} collective-permute-done((f32[384,1,256]{0,2,1:T(8,128)}, f32[384,1,256]{0,2,1:T(8,128)}, u32[]{:S(2)}, u32[]{:S(2)}) %collective-permute-start.5) | collective-permute-done | bytes 393248 | tf_op jit(solution)/shard_map/ppermute | solution.py:21
  120.5 24.3 %collective-permute-done.3 = f32[384,1,256]{0,2,1:T(8,128)} collective-permute-done((f32[384,1,256]{0,2,1:T(8,128)}, f32[384,1,256]{0,2,1:T(8,128)}, u32[]{:S(2)}, u32[]{:S(2)}) %collective-permute-start.3) | collective-permute-done | bytes 393248 | tf_op jit(solution)/shard_map/ppermute | solution.py:21
  144.8 1.5 fusion.64
  146.4 0.8 copy.207
  147.1 2.0 %fusion.65 = bf16[384,128]{0,1:T(8,128)(2,1)S(1)} fusion(f32[384,1,256]{0,2,1:T(8,128)} %collective-permute-done.5, f32[384,1,256]{0,2,1:T(8,128)} %collective-permute-done.4, f32[384,1,256]{0,2,1:T(8,128)} %collective-permute-done.3, f32[1,3,384,384]{2,3,1,0:T(8,128)} %copy-done.6, bf16[384,1,3,128]{0,3,2,1:T(8,128)(2,1)S(1)} %bitcast.378), kind=kOutput, calls=%fused_computation.119 | convolution fusion | flops 113885184 | bytes 2752512 | tf_op jit(solution)/shard_map/hgqt,qhgd->thd/dot_general | solution.py:98
  149.2 0.8 copy.208
  149.9 2.2 %copy.250 = f32[16,1,39936]{2,0,1:T(8,128)S(1)} copy(f32[16,1,39936]{2,1,0:T(1,128)} %all-to-all-done.2) | data formatting | bytes 5111808
  152.3 0.7 div.27
  153.0 1.1 copy.251
  (134 shorter events, 17.3 us)
Async XLA Ops:
  0.6 1.1 copy-start
  1.4 4.2 %copy-start.31 = (f32[24,2,8]{0,2,1:T(8,128)}, f32[24,2,8]{0,2,1:T(8,128)S(1)}, u32[]{:S(2)}) copy-start(f32[24,2,8]{0,2,1:T(8,128)S(1)} %fusion.79) | copy-start | bytes 4612
  1.7 2.6 %copy-start.15 = (bf16[24,6144]{1,0:T(8,128)(2,1)S(1)}, bf16[24,6144]{1,0:T(8,128)(2,1)}, u32[]{:S(2)}) copy-start(bf16[24,6144]{1,0:T(8,128)(2,1)} %param.17) | copy-start | bytes 884740
  1.7 2.6 %copy-start.20 = (bf16[8,6144]{1,0:T(8,128)(2,1)S(1)}, bf16[8,6144]{1,0:T(8,128)(2,1)}, u32[]{:S(2)}) copy-start(bf16[8,6144]{1,0:T(8,128)(2,1)} %param.18) | copy-start | bytes 294916
  1.7 2.8 %copy-start.34 = (s32[24,2]{0,1:T(2,128)S(1)}, s32[24,2]{0,1:T(2,128)}, u32[]{:S(2)}) copy-start(s32[24,2]{0,1:T(2,128)} %param.19) | copy-start | bytes 580
  1.7 3.3 %copy-start.33 = (s32[384]{0:T(512)S(1)}, s32[384]{0:T(512)}, u32[]{:S(2)}) copy-start(s32[384]{0:T(512)} %param.14) | copy-start | bytes 4612
  1.7 4.1 %copy-start.16 = (bf16[384,128]{1,0:T(8,128)(2,1)S(1)}, bf16[384,128]{1,0:T(8,128)(2,1)}, u32[]{:S(2)}) copy-start(bf16[384,128]{1,0:T(8,128)(2,1)} %param.11) | copy-start | bytes 294916
  1.7 4.1 %copy-start.22 = (bf16[384,128]{1,0:T(8,128)(2,1)S(1)}, bf16[384,128]{1,0:T(8,128)(2,1)}, u32[]{:S(2)}) copy-start(bf16[384,128]{1,0:T(8,128)(2,1)} %param.12) | copy-start | bytes 294916
  4.2 25.5 %copy-start.25 = (bf16[384,384]{1,0:T(8,128)(2,1)S(1)}, bf16[384,384]{1,0:T(8,128)(2,1)}, u32[]{:S(2)}) copy-start(bf16[384,384]{1,0:T(8,128)(2,1)} %param.10) | copy-start | bytes 884740
  4.2 25.7 %copy-start.26 = (bf16[384,384]{1,0:T(8,128)(2,1)S(1)}, bf16[384,384]{1,0:T(8,128)(2,1)}, u32[]{:S(2)}) copy-start(bf16[384,384]{1,0:T(8,128)(2,1)} %param.13) | copy-start | bytes 884740
  4.3 25.9 %copy-start.27 = (bf16[24,6144]{1,0:T(8,128)(2,1)S(1)}, bf16[24,6144]{1,0:T(8,128)(2,1)}, u32[]{:S(2)}) copy-start(bf16[24,6144]{1,0:T(8,128)(2,1)} %param.15) | copy-start | bytes 884740
  5.1 0.5 copy-start.37
  5.6 24.6 %copy-start.35 = (f32[24]{0:T(128)}, f32[24]{0:T(128)S(1)}, u32[]{:S(2)}) copy-start(f32[24]{0:T(128)S(1)} %multiply_bitcast_fusion) | copy-start | bytes 292
  6.6 50.0 %collective-permute-start.2 = (bf16[392,256]{1,0:T(8,128)(2,1)}, bf16[392,256]{1,0:T(8,128)(2,1)}, u32[]{:S(2)}, u32[]{:S(2)}) collective-permute-start(bf16[392,256]{1,0:T(8,128)(2,1)} %fusion.61), channel_id=1, source_target_pairs={{0,48},{16,64},{32,80},{48,96},{64,112},{80,128},{96,144},{112,160... | collective-permute-start | bytes 602120 | tf_op jit(solution)/shard_map/ppermute | solution.py:21
  14.3 41.7 %collective-permute-start.1 = (bf16[392,256]{1,0:T(8,128)(2,1)}, bf16[392,256]{1,0:T(8,128)(2,1)}, u32[]{:S(2)}, u32[]{:S(2)}) collective-permute-start(bf16[392,256]{1,0:T(8,128)(2,1)} %fusion.61), channel_id=1, source_target_pairs={{0,32},{16,48},{32,64},{48,80},{64,96},{80,112},{96,128},{112,144}... | collective-permute-start | bytes 602120 | tf_op jit(solution)/shard_map/ppermute | solution.py:21
  18.5 38.8 %collective-permute-start = (bf16[392,256]{1,0:T(8,128)(2,1)}, bf16[392,256]{1,0:T(8,128)(2,1)}, u32[]{:S(2)}, u32[]{:S(2)}) collective-permute-start(bf16[392,256]{1,0:T(8,128)(2,1)} %fusion.61), channel_id=1, source_target_pairs={{0,16},{16,32},{32,48},{48,64},{64,80},{80,96},{96,112},{112,128},... | collective-permute-start | bytes 602120 | tf_op jit(solution)/shard_map/ppermute | solution.py:21
  22.8 17.4 %all-to-all-start = ((f32[16,1,3072]{2,1,0:T(1,128)}), f32[16,1,3072]{2,1,0:T(1,128)}, u32[]{:S(2)}, u32[]{:S(2)}) async-start(f32[16,1,3072]{2,1,0:T(1,128)} %all_to_all.24), calls=%async_computation | async-start | bytes 393216 | tf_op jit(solution)/shard_map/all_to_all | solution.py:41
  36.4 2.6 %copy-start.21 = (bf16[8,6144]{1,0:T(8,128)(2,1)S(1)}, bf16[8,6144]{1,0:T(8,128)(2,1)}, u32[]{:S(2)}) copy-start(bf16[8,6144]{1,0:T(8,128)(2,1)} %param.18) | copy-start | bytes 294916
  36.4 2.6 %copy-start.32 = (f32[24,2,8]{0,2,1:T(8,128)S(1)}, f32[24,2,8]{0,2,1:T(8,128)}, u32[]{:S(2)}) copy-start(f32[24,2,8]{0,2,1:T(8,128)} %copy-done.31) | copy-start | bytes 4612
  36.4 2.6 %copy-start.36 = (f32[24]{0:T(128)S(1)}, f32[24]{0:T(128)}, u32[]{:S(2)}) copy-start(f32[24]{0:T(128)} %copy-done.35) | copy-start | bytes 292
  42.2 39.9 %all-to-all-start.1 = ((f32[32,1,3072]{2,1,0:T(1,128)}), f32[32,1,3072]{2,1,0:T(1,128)}, u32[]{:S(2)}, u32[]{:S(2)}) async-start(f32[32,1,3072]{2,1,0:T(1,128)} %broadcast_in_dim.111), calls=%async_computation.1 | async-start | bytes 786432 | tf_op jit(solution)/shard_map/all_to_all | solution.py:51
  59.6 6.2 %copy-start.7 = (pred[384,384]{0,1:T(8,128)(4,1)}, pred[384,384]{0,1:T(8,128)(4,1)S(1)}, u32[]{:S(2)}) copy-start(pred[384,384]{0,1:T(8,128)(4,1)S(1)} %get-tuple-element.67) | copy-start | bytes 442372
  62.0 4.5 %copy-start.9 = (bf16[384,1,256]{2,0,1:T(8,128)(2,1)}, bf16[384,1,256]{2,0,1:T(8,128)(2,1)S(1)}, u32[]{:S(2)}) copy-start(bf16[384,1,256]{2,0,1:T(8,128)(2,1)S(1)} %slice_bitcast_fusion) | copy-start | bytes 589828
  63.4 3.7 %copy-start.11 = (bf16[384,1,256]{2,0,1:T(8,128)(2,1)}, bf16[384,1,256]{2,0,1:T(8,128)(2,1)S(1)}, u32[]{:S(2)}) copy-start(bf16[384,1,256]{2,0,1:T(8,128)(2,1)S(1)} %slice_bitcast_fusion.1) | copy-start | bytes 589828
  64.8 3.0 %copy-start.13 = (bf16[384,1,256]{2,0,1:T(8,128)(2,1)}, bf16[384,1,256]{2,0,1:T(8,128)(2,1)S(1)}, u32[]{:S(2)}) copy-start(bf16[384,1,256]{2,0,1:T(8,128)(2,1)S(1)} %slice_bitcast_fusion.2) | copy-start | bytes 589828
  64.8 1.0 copy-start.23
  70.7 3.6 %copy-start.2 = (bf16[3,384,384]{1,2,0:T(8,128)(2,1)}, bf16[3,384,384]{1,2,0:T(8,128)(2,1)S(1)}, u32[]{:S(2)}) copy-start(bf16[3,384,384]{1,2,0:T(8,128)(2,1)S(1)} %get-tuple-element.64) | copy-start | bytes 2654212
  70.7 3.6 %copy-start.4 = (bf16[3,384,384]{1,2,0:T(8,128)(2,1)}, bf16[3,384,384]{1,2,0:T(8,128)(2,1)S(1)}, u32[]{:S(2)}) copy-start(bf16[3,384,384]{1,2,0:T(8,128)(2,1)S(1)} %get-tuple-element.65) | copy-start | bytes 2654212
  89.0 6.9 %copy-start.1 = (bf16[3,384,384]{1,2,0:T(8,128)(2,1)S(1)}, bf16[3,384,384]{1,2,0:T(8,128)(2,1)}, u32[]{:S(2)}) copy-start(bf16[3,384,384]{1,2,0:T(8,128)(2,1)} %get-tuple-element.63) | copy-start | bytes 2654212
  89.0 7.3 %copy-start.30 = (f32[384,1,128]{0,2,1:T(8,128)S(1)}, f32[384,1,128]{0,2,1:T(8,128)}, u32[]{:S(2)}) copy-start(f32[384,1,128]{0,2,1:T(8,128)} %convolution_bitcast_fusion.2) | copy-start | bytes 589828
  89.0 60.9 %all-to-all-start.2 = ((f32[16,1,39936]{2,1,0:T(1,128)}), f32[16,1,39936]{2,1,0:T(1,128)}, u32[]{:S(2)}, u32[]{:S(2)}) async-start(f32[16,1,39936]{2,1,0:T(1,128)} %copy.205), calls=%async_computation.2 | async-start | bytes 5111808 | tf_op jit(solution)/shard_map/all_to_all | solution.py:231
  95.9 2.8 %copy-start.19 = (f32[384,1,128]{0,2,1:T(8,128)S(1)}, f32[384,1,128]{0,2,1:T(8,128)}, u32[]{:S(2)}) copy-start(f32[384,1,128]{0,2,1:T(8,128)} %fusion.31) | copy-start | bytes 589828
  95.9 2.8 %copy-start.29 = (f32[384,1,128]{0,2,1:T(8,128)S(1)}, f32[384,1,128]{0,2,1:T(8,128)}, u32[]{:S(2)}) copy-start(f32[384,1,128]{0,2,1:T(8,128)} %convolution_bitcast_fusion.4) | copy-start | bytes 589828
  95.9 4.8 %copy-start.18 = (f32[384,1,128]{0,2,1:T(8,128)S(1)}, f32[384,1,128]{0,2,1:T(8,128)}, u32[]{:S(2)}) copy-start(f32[384,1,128]{0,2,1:T(8,128)} %fusion.30) | copy-start | bytes 589828
  95.9 4.8 %copy-start.28 = (f32[384,1,128]{0,2,1:T(8,128)S(1)}, f32[384,1,128]{0,2,1:T(8,128)}, u32[]{:S(2)}) copy-start(f32[384,1,128]{0,2,1:T(8,128)} %convolution_bitcast_fusion.6) | copy-start | bytes 589828
  95.9 7.0 %copy-start.8 = (pred[384,384]{0,1:T(8,128)(4,1)S(1)}, pred[384,384]{0,1:T(8,128)(4,1)}, u32[]{:S(2)}) copy-start(pred[384,384]{0,1:T(8,128)(4,1)} %copy-done.7) | copy-start | bytes 442372
  95.9 7.0 %copy-start.17 = (bf16[384,128]{1,0:T(8,128)(2,1)S(1)}, bf16[384,128]{1,0:T(8,128)(2,1)}, u32[]{:S(2)}) copy-start(bf16[384,128]{1,0:T(8,128)(2,1)} %param.11) | copy-start | bytes 294916
  97.1 23.4 %collective-permute-start.5 = (f32[384,1,256]{0,2,1:T(8,128)}, f32[384,1,256]{0,2,1:T(8,128)}, u32[]{:S(2)}, u32[]{:S(2)}) collective-permute-start(f32[384,1,256]{0,2,1:T(8,128)} %pad_maximum_fusion.2), channel_id=1, source_target_pairs={{48,0},{64,16},{80,32},{96,48},{112,64},{128,80},{144,96},{160,112... | collective-permute-start | bytes 1179656 | tf_op jit(solution)/shard_map/ppermute | solution.py:21
  99.4 21.1 %collective-permute-start.4 = (f32[384,1,256]{0,2,1:T(8,128)}, f32[384,1,256]{0,2,1:T(8,128)}, u32[]{:S(2)}, u32[]{:S(2)}) collective-permute-start(f32[384,1,256]{0,2,1:T(8,128)} %pad_maximum_fusion.1), channel_id=1, source_target_pairs={{32,0},{48,16},{64,32},{80,48},{96,64},{112,80},{128,96},{144,112}... | collective-permute-start | bytes 1179656 | tf_op jit(solution)/shard_map/ppermute | solution.py:21
  101.5 2.1 %copy-start.24 = (bf16[384,128]{1,0:T(8,128)(2,1)S(1)}, bf16[384,128]{1,0:T(8,128)(2,1)}, u32[]{:S(2)}) copy-start(bf16[384,128]{1,0:T(8,128)(2,1)} %param.12) | copy-start | bytes 294916
  101.5 43.3 %collective-permute-start.3 = (f32[384,1,256]{0,2,1:T(8,128)}, f32[384,1,256]{0,2,1:T(8,128)}, u32[]{:S(2)}, u32[]{:S(2)}) collective-permute-start(f32[384,1,256]{0,2,1:T(8,128)} %pad_maximum_fusion), channel_id=1, source_target_pairs={{16,0},{32,16},{48,32},{64,48},{80,64},{96,80},{112,96},{128,112},... | collective-permute-start | bytes 1179656 | tf_op jit(solution)/shard_map/ppermute | solution.py:21
  103.6 1.3 copy-start.6
  103.6 1.8 %copy-start.5 = (bf16[3,384,384]{1,2,0:T(8,128)(2,1)S(1)}, bf16[3,384,384]{1,2,0:T(8,128)(2,1)}, u32[]{:S(2)}) copy-start(bf16[3,384,384]{1,2,0:T(8,128)(2,1)} %copy-done.4) | copy-start | bytes 2654212
  103.6 1.8 %copy-start.14 = (bf16[384,1,256]{2,0,1:T(8,128)(2,1)S(1)}, bf16[384,1,256]{2,0,1:T(8,128)(2,1)}, u32[]{:S(2)}) copy-start(bf16[384,1,256]{2,0,1:T(8,128)(2,1)} %copy-done.13) | copy-start | bytes 589828
  104.0 1.8 %copy-start.3 = (bf16[3,384,384]{1,2,0:T(8,128)(2,1)S(1)}, bf16[3,384,384]{1,2,0:T(8,128)(2,1)}, u32[]{:S(2)}) copy-start(bf16[3,384,384]{1,2,0:T(8,128)(2,1)} %copy-done.2) | copy-start | bytes 2654212
  104.0 1.8 %copy-start.12 = (bf16[384,1,256]{2,0,1:T(8,128)(2,1)S(1)}, bf16[384,1,256]{2,0,1:T(8,128)(2,1)}, u32[]{:S(2)}) copy-start(bf16[384,1,256]{2,0,1:T(8,128)(2,1)} %copy-done.11) | copy-start | bytes 589828
  105.5 1.0 copy-start.10
